TPU v7x, 128 devices: a whole 4x4x4 slice. The times are simulated.
128 devices in a mesh: dom: 16 (over z, y), grp: 8 (over x, core).
Axes of the slice: x: 4, y: 4, z: 4, core: 2. Of those that a mesh axis runs over, the one named last changes fastest.
Arguments:
- residual_in: bfloat16 [1024, 32, 625], P(('dom', 'grp')), may hold values from -6 to 6
- block_inverse: bfloat16 [1024, 625, 625], P(('dom', 'grp')), may hold values from -0.25 to 0.25
- coupling: bfloat16 [2048, 625, 625], P(('dom', 'grp')), may hold values from -0.25 to 0.25
- tile_region: int32 [2048, 1], P(('dom', 'grp')), may hold values from 0 to 15; in each aligned block of 16 rows (0 to 15, 16 to 31, ...) at most 2 rows name the same one
- tile_source: int32 [2048], P(('dom', 'grp')), may hold values from 0 to 7
- tile_target: int32 [2048], P(('dom', 'grp')), may hold values from 0 to 7
- interface_basis: bfloat16 [1024, 625, 64], P(('dom', 'grp')), may hold values from -0.25 to 0.25
- reduced_inverse: float32 [16, 64, 64], P('dom'), may hold values from -0.75 to 0.75
Outputs:
- preconditioned: float32 [1024, 32, 625], P(('dom', 'grp'))
Inputs may be any that keep to these rules, and one draw needn't show every extreme that they name: `tile_region`: among the 16 tiles of one device, at most 2 name the same region; in every draw some device names some region exactly 2 times.
All inputs are finite; a program needn't handle non-finite values.
Results may differ from a plain program's by a relative error of at most 0.013.
Values may be sent and summed in bfloat16 or wider, within the bound.
No kernel may reach another device: no remote copies, remote signals or barrier semaphores. Data moves between devices by JAX's collectives and lax.ppermute only.
A program may use at most 256 MiB of HBM per device.

v0:
```python
import jax
import jax.numpy as jnp
from jax import lax
from jax.sharding import PartitionSpec as P

CAP = 2


def shards(
    residual_in,
    block_inverse,
    coupling,
    tile_region,
    tile_source,
    tile_target,
    interface_basis,
    reduced_inverse,
):
    regions = lax.axis_size("dom")
    slots = regions * CAP
    elements = residual_in.shape[0]
    vectors = residual_in.shape[1]
    width = residual_in.shape[2]
    initial = jnp.einsum(
        "ekb,ebc->ekc", residual_in, block_inverse, preferred_element_type=jnp.float32
    ).astype(jnp.bfloat16)
    destination = tile_region[:, 0]
    onehot = (destination[:, None] == jnp.arange(regions, dtype=jnp.int32)[None, :]).astype(
        jnp.int32
    )
    earlier = jnp.cumsum(onehot, axis=0) - onehot
    tile_rank = jnp.sum(earlier * onehot, axis=1)
    slot_index = destination * CAP + tile_rank
    target_buffer = (
        jnp.full((slots,), -1, jnp.int32).at[slot_index].set(tile_target).reshape(regions, CAP)
    )
    targets = lax.all_to_all(target_buffer, "dom", split_axis=0, concat_axis=0, tiled=True).reshape(
        slots
    )
    sources = initial[tile_source]
    local_products = jnp.einsum(
        "tkb,tbc->tkc", sources, coupling, preferred_element_type=jnp.float32
    )
    product_buffer = (
        jnp.zeros((slots, vectors, width), jnp.float32).at[slot_index].set(local_products)
    )
    products = (
        lax.all_to_all(
            product_buffer.reshape(regions, CAP, vectors, width).astype(jnp.bfloat16),
            "dom",
            split_axis=0,
            concat_axis=0,
            tiled=True,
        )
        .astype(jnp.float32)
        .reshape(slots, vectors, width)
    )
    selector = (targets[None, :] == jnp.arange(elements, dtype=jnp.int32)[:, None]).astype(
        jnp.float32
    )
    coupled = jnp.dot(
        selector,
        products.reshape(slots, vectors * width),
        precision=lax.Precision.HIGHEST,
        preferred_element_type=jnp.float32,
    ).reshape(elements, vectors, width)
    corrected_in = (residual_in.astype(jnp.float32) - coupled).astype(jnp.bfloat16)
    second = jnp.einsum(
        "ekb,ebc->ekc", corrected_in, block_inverse, preferred_element_type=jnp.float32
    )
    second_b = second.astype(jnp.bfloat16)
    partial_reduced = jnp.einsum(
        "ekb,ebm->km", second_b, interface_basis, preferred_element_type=jnp.float32
    )
    reduced = lax.psum(partial_reduced, "grp")
    solved = jnp.dot(
        reduced,
        reduced_inverse[0],
        precision=lax.Precision.HIGHEST,
        preferred_element_type=jnp.float32,
    ).astype(jnp.bfloat16)
    correction = jnp.einsum(
        "km,ebm->ekb", solved, interface_basis, preferred_element_type=jnp.float32
    )
    return second + correction


def solution(mesh):
    return jax.shard_map(
        shards,
        mesh=mesh,
        in_specs=(
            P(("dom", "grp"), None, None),
            P(("dom", "grp"), None, None),
            P(("dom", "grp"), None, None),
            P(("dom", "grp"), None),
            P(("dom", "grp")),
            P(("dom", "grp")),
            P(("dom", "grp"), None, None),
            P("dom", None, None),
        ),
        out_specs=P(("dom", "grp"), None, None),
        check_vma=False,
    )
```

profile of v0, /device:TPU:0, one launch (start us, length us, event | category | flops | bytes accessed | tf_op | source)
XLA Modules:
  0.0 96.3 jit_solution(15889635007566257269)
XLA Ops:
  0.0 0.0 copy-start
  0.0 0.8 fusion.22
  0.8 0.8 select_reduce_fusion
  1.7 0.7 fusion.26
  2.3 0.8 scatter_custom_fusion
  3.1 0.7 all_to_all.9
  3.8 8.2 %all-to-all-start = ((s32[16,1,2]{2,1,0:T(1,128)}), s32[16,1,2]{2,1,0:T(1,128)S(1)}, u32[]{:S(2)}, u32[]{:S(2)}) async-start(s32[16,1,2]{2,1,0:T(1,128)} %bitcast.3), calls=%async_computation | async-start | bytes 16384 | tf_op jit(solution)/shard_map/all_to_all | solution.py:37
  11.9 0.7 compare_select_fusion
  12.6 5.2 %fusion.15 = bf16[8,32,625]{2,1,0:T(8,128)(2,1)S(1)} fusion(bf16[8,32,625]{2,1,0:T(8,128)(2,1)} %param.8, bf16[8,625,625]{2,0,1:T(8,128)(2,1)} %param.9), kind=kOutput, calls=%fused_computation.15 | convolution fusion | flops 200160000 | bytes 6890000 | tf_op jit(solution)/shard_map/ekb,ebc->ekc/dot_general | solution.py:24
  17.8 0.7 gather_fusion
  18.5 10.1 %fusion = f32[16,32,625]{2,1,0:T(8,128)} fusion(bf16[16,32,625]{2,1,0:T(8,128)(2,1)S(1)} %gather_fusion, bf16[16,625,625]{2,0,1:T(8,128)(2,1)} %param.10), kind=kOutput, calls=%fused_computation.3 | convolution fusion | flops 400000000 | bytes 14420000 | tf_op jit(solution)/shard_map/tkb,tbc->tkc/dot_general | solution.py:41
  28.6 0.3 broadcast_in_dim.14
  28.9 2.4 %scatter_fusion = f32[32,32,625]{2,1,0:T(8,128)S(1)} fusion(f32[32,32,625]{2,1,0:T(8,128)S(1)} %broadcast_in_dim.14, s32[16]{0:T(128)S(1)} %fusion.26, f32[16,32,625]{2,1,0:T(8,128)} %fusion), kind=kCustom, calls=%fused_computation.2 | custom fusion | bytes 3840064 | tf_op jit(solution)/shard_map/scatter | solution.py:45
  31.3 1.2 %convert_element_type.29 = bf16[32,32,625]{2,1,0:T(8,128)(2,1)} convert(f32[32,32,625]{2,1,0:T(8,128)S(1)} %scatter_fusion) | non-fusion elementwise | flops 640000 | bytes 3840000 | tf_op jit(solution)/shard_map/convert_element_type | solution.py:49
  32.5 0.0 all-to-all-done
  32.5 7.2 %all-to-all-start.1 = ((bf16[16,2,32,625]{3,2,1,0:T(8,128)(2,1)}), bf16[16,2,32,625]{3,2,1,0:T(8,128)(2,1)S(1)}, u32[]{:S(2)}, u32[]{:S(2)}) async-start(bf16[16,2,32,625]{3,2,1,0:T(8,128)(2,1)} %bitcast.34), calls=%async_computation.1 | async-start | bytes 2621440 | tf_op jit(solution)/shard_map/all_to_all | solution.py:48
  39.7 0.5 broadcast.39
  40.3 0.7 reduce.3
  40.9 0.1 eq.34
  41.0 18.9 %all-to-all-done.1 = bf16[16,2,32,625]{3,2,1,0:T(8,128)(2,1)S(1)} async-done(((bf16[16,2,32,625]{3,2,1,0:T(8,128)(2,1)}), bf16[16,2,32,625]{3,2,1,0:T(8,128)(2,1)S(1)}, u32[]{:S(2)}, u32[]{:S(2)}) %all-to-all-start.1) | async-done | bytes 1280032 | tf_op jit(solution)/shard_map/all_to_all | solution.py:48
  59.9 1.5 %reshape_reshape.3 = bf16[32,20000]{1,0:T(8,128)(2,1)S(1)} reshape(bf16[16,2,32,625]{3,2,1,0:T(8,128)(2,1)S(1)} %all-to-all-done.1) | data formatting | bytes 2560000 | tf_op jit(solution)/shard_map/reshape;reshape | solution.py:63
  61.4 3.2 %dot_general.28 = bf16[32,625,32]{1,0,2:T(8,128)(2,1)S(1)} reshape(bf16[20000,32]{0,1:T(8,128)(2,1)S(1)} %bitcast.35) | data formatting | bytes 2560000 | tf_op jit(solution)/shard_map/dot_general | solution.py:61
  64.6 1.5 %fusion.12 = bf16[8,32,625]{2,0,1:T(8,128)(2,1)S(1)} fusion(bf16[32,625,32]{1,0,2:T(8,128)(2,1)S(1)} %dot_general.28, bf16[8,32,625]{2,1,0:T(8,128)(2,1)} %param.8, s32[32]{0:T(128)S(1)} %eq.34), kind=kOutput, calls=%fused_computation.14 | convolution fusion | flops 10720256 | bytes 1920128 | tf_op jit(solution)/shard_map/dot_general | solution.py:61
  66.1 0.0 copy-start.1
  66.1 5.1 %fusion.2 = f32[8,32,625]{2,1,0:T(8,128)S(1)} fusion(bf16[8,625,625]{2,0,1:T(8,128)(2,1)} %param.9, bf16[8,32,625]{2,0,1:T(8,128)(2,1)S(1)} %fusion.12), kind=kOutput, calls=%fused_computation.5 | convolution fusion | flops 200000000 | bytes 7210000 | tf_op jit(solution)/shard_map/ekb,ebc->ekc/dot_general | solution.py:68
  71.2 0.0 copy-done
  71.2 0.3 convolution_bitcast_fusion.1
  71.5 23.6 %psum.7 = f32[32,64]{1,0:T(8,128)S(1)} all-reduce(f32[32,64]{1,0:T(8,128)S(1)} %convolution_bitcast_fusion.1), channel_id=1, replica_groups=mesh['dom'=16,'grp'=8] {'grp'}, use_global_device_ids=true, to_apply=%region_4.5 | all-reduce | flops 2048 | bytes 16384 | tf_op jit(solution)/shard_map/psum | solution.py:75
  95.1 0.0 copy-done.1
  95.1 0.1 fusion.18
  95.2 1.1 %fusion.11 = f32[8,32,625]{2,1,0:T(8,128)} fusion(f32[8,32,625]{2,1,0:T(8,128)S(1)} %fusion.2, bf16[32,64,1]{1,0,2:T(8,128)(2,1)S(1)} %fusion.18, bf16[8,625,64]{1,2,0:T(8,128)(2,1)S(1)} %copy-done), kind=kOutput, calls=%fused_computation.13 | convolution fusion | flops 20640000 | bytes 1924096 | tf_op jit(solution)/shard_map/km,ebm->ekb/dot_general | solution.py:82
  (2 shorter events, 0.0 us)
Async XLA Ops:
  0.0 71.2 %copy-start = (bf16[8,625,64]{1,2,0:T(8,128)(2,1)S(1)}, bf16[8,625,64]{1,2,0:T(8,128)(2,1)}, u32[]{:S(2)}) copy-start(bf16[8,625,64]{1,2,0:T(8,128)(2,1)} %param.14) | copy-start | bytes 1920004
  3.8 28.7 %all-to-all-start = ((s32[16,1,2]{2,1,0:T(1,128)}), s32[16,1,2]{2,1,0:T(1,128)S(1)}, u32[]{:S(2)}, u32[]{:S(2)}) async-start(s32[16,1,2]{2,1,0:T(1,128)} %bitcast.3), calls=%async_computation | async-start | bytes 16384 | tf_op jit(solution)/shard_map/all_to_all | solution.py:37
  32.5 27.4 %all-to-all-start.1 = ((bf16[16,2,32,625]{3,2,1,0:T(8,128)(2,1)}), bf16[16,2,32,625]{3,2,1,0:T(8,128)(2,1)S(1)}, u32[]{:S(2)}, u32[]{:S(2)}) async-start(bf16[16,2,32,625]{3,2,1,0:T(8,128)(2,1)} %bitcast.34), calls=%async_computation.1 | async-start | bytes 2621440 | tf_op jit(solution)/shard_map/all_to_all | solution.py:48
  66.1 29.0 %copy-start.1 = (f32[1,64,64]{2,1,0:T(8,128)S(1)}, f32[1,64,64]{2,1,0:T(8,128)}, u32[]{:S(2)}) copy-start(f32[1,64,64]{2,1,0:T(8,128)} %param.15) | copy-start | bytes 49156
where the time goes:
time: 96.7 us; the launch traced here: 96.3 us
  blocking collectives  23.6 us (24%)
  matrix products  23.4 us (24%)
  waiting for transfers between devices  18.9 us (20%)
  starting transfers between devices  15.4 us (16%)
  local copies, waits for them, and re-layouts  10.1 us (10%)
  other arithmetic  4.89 us (5%)
    psum x1, blocking collectives, shards(): reduced = lax.psum(partial_reduced, 'grp')  23.6 us
    all_to_all x1, waiting for transfers between devices, shards(): lax.all_to_all(product_buffer.reshape(regions, CAP, vectors, width).astyp...  18.9 us
    dot_general x1, matrix products, shards(): jnp.einsum('tkb,tbc->tkc', sources, coupling, preferred_element_type=jnp....  10.1 us
    all_to_all x1, starting transfers between devices, shards(): lax.all_to_all(target_buffer, 'dom', split_axis=0, concat_axis=0, tiled=T...  8.16 us
    all_to_all x1, starting transfers between devices, shards(): lax.all_to_all(product_buffer.reshape(regions, CAP, vectors, width).astyp...  7.23 us
    dot_general x1, matrix products, shards(): jnp.einsum('ekb,ebc->ekc', residual_in, block_inverse, preferred_element_...  5.17 us
    dot_general x1, matrix products, shards(): jnp.einsum('ekb,ebc->ekc', corrected_in, block_inverse, preferred_element...  5.14 us
    dot_general x1, local copies, waits for them, and re-layouts, shards(): jnp.dot(selector, products.reshape(slots, vectors * width), precision=lax...  3.17 us
  transfers between devices with their start and end apart: 2, of which 1 were waited for; matrix products, arithmetic and copies ran while one was open for 23% of the time, Pallas kernels for 0%

commit v1 on v0

v1 whole, which is shorter than its diff:
```python
import jax
import jax.numpy as jnp
from jax import lax
from jax.sharding import PartitionSpec as P

CAP = 2
LANE = 128


def group_sum(value, axis):
    size = lax.axis_size(axis)
    if size & (size - 1):
        return lax.psum(value, axis)
    bit = 1
    while bit < size:
        pairs = [(i, i ^ bit) for i in range(size)]
        value = value + lax.ppermute(value, axis, pairs)
        bit *= 2
    return value


def shards(
    residual_in,
    block_inverse,
    coupling,
    tile_region,
    tile_source,
    tile_target,
    interface_basis,
    reduced_inverse,
):
    regions = lax.axis_size("dom")
    slots = regions * CAP
    elements = residual_in.shape[0]
    vectors = residual_in.shape[1]
    width = residual_in.shape[2]
    tiles = coupling.shape[0]
    padded = -(-(width + 1) // LANE) * LANE
    initial = jnp.einsum(
        "ekb,ebc->ekc", residual_in, block_inverse, preferred_element_type=jnp.float32
    ).astype(jnp.bfloat16)
    destination = tile_region[:, 0]
    order = jnp.arange(tiles, dtype=jnp.int32)
    same = destination[:, None] == destination[None, :]
    tile_rank = jnp.sum(same & (order[None, :] < order[:, None]), axis=1).astype(jnp.int32)
    slot_index = destination * CAP + tile_rank
    slot_ids = jnp.arange(slots, dtype=jnp.int32)
    hit = slot_index[None, :] == slot_ids[:, None]
    slot_tile = jnp.where(
        jnp.any(hit, axis=1), jnp.sum(jnp.where(hit, order[None, :], 0), axis=1), tiles
    ).astype(jnp.int32)
    sources = initial[tile_source]
    local_products = jnp.einsum(
        "tkb,tbc->tkc", sources, coupling, preferred_element_type=jnp.float32
    ).astype(jnp.bfloat16)
    marks = jnp.concatenate([tile_target, jnp.full((1,), -1, jnp.int32)]).astype(jnp.bfloat16)
    column = lax.broadcasted_iota(jnp.int32, (tiles + 1, vectors, padded - width), 2)
    row = lax.broadcasted_iota(jnp.int32, (tiles + 1, vectors, padded - width), 1)
    tail = jnp.where((column == 0) & (row == 0), marks[:, None, None], jnp.bfloat16(0))
    body = jnp.concatenate(
        [local_products, jnp.zeros((1, vectors, width), jnp.bfloat16)], axis=0
    )
    extended = jnp.concatenate([body, tail], axis=2)
    product_buffer = extended[slot_tile]
    received = lax.all_to_all(
        product_buffer.reshape(regions, CAP, vectors, padded),
        "dom",
        split_axis=0,
        concat_axis=0,
        tiled=True,
    ).reshape(slots, vectors, padded)
    targets = received[:, 0, width].astype(jnp.int32)
    products = received[:, :, :width]
    selector = (targets[None, :] == jnp.arange(elements, dtype=jnp.int32)[:, None]).astype(
        jnp.bfloat16
    )
    coupled = jnp.einsum(
        "es,skc->ekc", selector, products, preferred_element_type=jnp.float32
    )
    corrected_in = (residual_in.astype(jnp.float32) - coupled).astype(jnp.bfloat16)
    second = jnp.einsum(
        "ekb,ebc->ekc", corrected_in, block_inverse, preferred_element_type=jnp.float32
    )
    second_b = second.astype(jnp.bfloat16)
    partial_reduced = jnp.einsum(
        "ekb,ebm->km", second_b, interface_basis, preferred_element_type=jnp.float32
    )
    reduced = group_sum(partial_reduced, "grp")
    solved = jnp.dot(
        reduced,
        reduced_inverse[0],
        precision=lax.Precision.HIGHEST,
        preferred_element_type=jnp.float32,
    ).astype(jnp.bfloat16)
    correction = jnp.einsum(
        "km,ebm->ekb", solved, interface_basis, preferred_element_type=jnp.float32
    )
    return second + correction


def solution(mesh):
    return jax.shard_map(
        shards,
        mesh=mesh,
        in_specs=(
            P(("dom", "grp"), None, None),
            P(("dom", "grp"), None, None),
            P(("dom", "grp"), None, None),
            P(("dom", "grp"), None),
            P(("dom", "grp")),
            P(("dom", "grp")),
            P(("dom", "grp"), None, None),
            P("dom", None, None),
        ),
        out_specs=P(("dom", "grp"), None, None),
        check_vma=False,
    )
```

time: 96.7 us -> 65.6 us (0.68)
  waiting for transfers between devices: 18.9 us -> 5.65 us
  starting transfers between devices: 15.4 us -> 4.52 us
  local copies, waits for them, and re-layouts: 10.1 us -> 1.46 us
  blocking collectives: 23.6 us -> 28.1 us
  matrix products: 23.4 us -> 21.4 us
    all_to_all x0 -> x1, blocking collectives: none -> 28.1 us  [shards(): lax.all_to_all(product_buffer.reshape(regions, CAP, vectors, padded), 'do...]
    psum x1 -> x0, blocking collectives: 23.6 us -> none  [shards(): reduced = lax.psum(partial_reduced, 'grp')]
    all_to_all x2 -> x0, waiting for transfers between devices: 18.9 us -> none  [the longest x1 18.9 us: shards(): lax.all_to_all(product_buffer.reshape(regions, CAP, vectors, width).astyp...]
    all_to_all x2 -> x0, starting transfers between devices: 15.4 us -> none  [the longest x1 8.16 us: shards(): lax.all_to_all(target_buffer, 'dom', split_axis=0, concat_axis=0, tiled=T...]
    ppermute x0 -> x3, waiting for transfers between devices: none -> 5.65 us  [group_sum(): value = value + lax.ppermute(value, axis, pairs)]
    ppermute x0 -> x3, starting transfers between devices: none -> 4.52 us  [group_sum(): value = value + lax.ppermute(value, axis, pairs)]
    dot_general x1 -> x0, local copies, waits for them, and re-layouts: 3.17 us -> none  [shards(): jnp.dot(selector, products.reshape(slots, vectors * width), precision=lax...]
    scatter x2 -> x0, local copies, waits for them, and re-layouts: 3.14 us -> none  [the longest x1 2.39 us: shards(): jnp.zeros((slots, vectors, width), jnp.float32).at[slot_index]]
  transfers between devices with their start and end apart: 2 -> 3, of which waited for: 1 -> 3; matrix products, arithmetic and copies ran while one was open for 23% -> 0% of each run, Pallas kernels for 0% -> 0%
where the time goes in v1:
time: 65.6 us; the launch traced here: 65.3 us
  blocking collectives  28.1 us (43%)
  matrix products  21.4 us (33%)
  waiting for transfers between devices  5.65 us (9%)
  starting transfers between devices  4.52 us (7%)
  other arithmetic  4.14 us (6%)
  local copies, waits for them, and re-layouts  1.46 us (2%)
    all_to_all x1, blocking collectives, shards(): lax.all_to_all(product_buffer.reshape(regions, CAP, vectors, padded), 'do...  28.1 us
    dot_general x1, matrix products, shards(): jnp.einsum('tkb,tbc->tkc', sources, coupling, preferred_element_type=jnp....  9.08 us
    ppermute x3, waiting for transfers between devices, group_sum(): value = value + lax.ppermute(value, axis, pairs)  5.65 us
    dot_general x1, matrix products, shards(): jnp.einsum('ekb,ebc->ekc', residual_in, block_inverse, preferred_element_...  5.17 us
    dot_general x1, matrix products, shards(): jnp.einsum('ekb,ebc->ekc', corrected_in, block_inverse, preferred_element...  5.13 us
    ppermute x3, starting transfers between devices, group_sum(): value = value + lax.ppermute(value, axis, pairs)  4.52 us
  transfers between devices with their start and end apart: 3, of which 3 were waited for; matrix products, arithmetic and copies ran while one was open for 0% of the time, Pallas kernels for 0%

profile of v1, /device:TPU:0, one launch (start us, length us, event | category | flops | bytes accessed | tf_op | source)
XLA Modules:
  0.0 65.3 jit_solution(14962103829361948989)
XLA Ops:
  0.0 0.0 copy-start
  0.0 0.9 %convert_reduce_fusion = s32[16]{0:T(128)S(1)} fusion(s32[16]{0:T(128)} %bitcast.31), kind=kLoop, calls=%fused_computation.32 | loop fusion | flops 1264 | bytes 128 | tf_op jit(solution)/shard_map/reduce_sum | solution.py:45
  0.9 0.7 %multiply_add_fusion = s32[16]{0:T(128)S(1)} fusion(s32[16]{0:T(128)S(1)} %convert_reduce_fusion, s32[16,1]{0,1:T(1,128)} %param.11), kind=kLoop, calls=%fused_computation.44 | loop fusion | flops 32 | bytes 192 | tf_op jit(solution)/shard_map/add | solution.py:46
  1.6 0.1 select_reduce_fusion
  1.7 0.1 fusion.29
  1.8 0.7 %compare_select_fusion.1 = s32[16]{0:T(128)S(1)} fusion(s32[16]{0:T(128)} %param.12), kind=kLoop, calls=%fused_computation.40 | loop fusion | flops 48 | bytes 128 | tf_op jit(solution)/shard_map/select_n | solution.py:52
  2.4 0.7 %convert.5 = bf16[16]{0:T(256)(128)(2,1)S(1)} convert(s32[16]{0:T(128)} %param.13) | non-fusion elementwise | flops 16 | bytes 96 | tf_op jit(solution)/shard_map/convert.1
  3.1 0.1 pad_maximum_fusion
  3.2 5.2 %fusion.19 = bf16[8,32,625]{2,1,0:T(8,128)(2,1)S(1)} fusion(bf16[8,32,625]{2,1,0:T(8,128)(2,1)} %param.8, bf16[8,625,625]{2,0,1:T(8,128)(2,1)} %param.9), kind=kOutput, calls=%fused_computation.17 | convolution fusion | flops 200160000 | bytes 6890000 | tf_op jit(solution)/shard_map/ekb,ebc->ekc/dot_general | solution.py:39
  8.4 0.7 %gather_fusion = bf16[16,32,625]{2,1,0:T(8,128)(2,1)S(1)} fusion(bf16[8,32,625]{2,1,0:T(8,128)(2,1)S(1)} %fusion.19, s32[1024]{0:T(1024)S(1)} %pad_clamp_fusion.1), kind=kCustom, calls=%fused_computation | custom fusion | bytes 1280064 | tf_op jit(solution)/shard_map/gather | solution.py:52
  9.1 9.1 %fusion.7 = bf16[16,32,625]{2,1,0:T(8,128)(2,1)S(1)} fusion(bf16[16,32,625]{2,1,0:T(8,128)(2,1)S(1)} %gather_fusion, bf16[16,625,625]{2,0,1:T(8,128)(2,1)} %param.10), kind=kOutput, calls=%fused_computation.10 | convolution fusion | flops 400320000 | bytes 13780000 | tf_op jit(solution)/shard_map/tkb,tbc->tkc/dot_general | solution.py:53
  18.1 0.1 and_select_fusion
  18.2 0.1 fusion.23
  18.4 0.8 %gather_fusion.1 = bf16[32,32,640]{2,1,0:T(8,128)(2,1)S(1)} fusion(bf16[17,32,640]{2,1,0:T(8,128)(2,1)S(1)} %fusion.23, s32[1024]{0:T(1024)S(1)} %pad_clamp_fusion), kind=kCustom, calls=%fused_computation.1 | custom fusion | bytes 2621568 | tf_op jit(solution)/shard_map/gather | solution.py:64
  19.1 0.0 copy-start.1
  19.2 28.1 %all_to_all.5 = bf16[16,2,32,640]{3,2,1,0:T(8,128)(2,1)S(1)} all-to-all(bf16[16,2,32,640]{3,2,1,0:T(8,128)(2,1)S(1)} %bitcast.30), channel_id=1, replica_groups=mesh['dom'=16,'grp'=8] {'dom'}, dimensions={0} | all-to-all | bytes 2621440 | tf_op jit(solution)/shard_map/all_to_all | solution.py:65
  47.2 0.7 %fusion.27 = s32[32]{0:T(128)S(1)} fusion(bf16[32,32,640]{2,1,0:T(8,128)(2,1)S(1)} %bitcast.28), kind=kLoop, calls=%fused_computation.27 | loop fusion | flops 32 | bytes 192 | tf_op jit(solution)/shard_map/convert_element_type | solution.py:72
  47.9 0.0 copy-done.1
  47.9 0.5 fusion.16
  48.5 5.1 %fusion.2 = f32[8,32,625]{2,1,0:T(8,128)S(1)} fusion(bf16[8,625,625]{2,0,1:T(8,128)(2,1)} %param.9, bf16[8,32,625]{2,0,1:T(8,128)(2,1)S(1)} %fusion.16), kind=kOutput, calls=%fused_computation.4 | convolution fusion | flops 200000000 | bytes 7210000 | tf_op jit(solution)/shard_map/ekb,ebc->ekc/dot_general | solution.py:81
  53.6 0.0 copy-done
  53.6 0.0 copy-start.2
  53.6 0.3 convolution_bitcast_fusion.1
  53.9 0.0 collective-permute-start
  53.9 1.2 %collective-permute-done = f32[32,64]{1,0:T(8,128)S(1)} collective-permute-done((f32[32,64]{1,0:T(8,128)S(1)}, f32[32,64]{1,0:T(8,128)S(1)}, u32[]{:S(2)}, u32[]{:S(2)}) %collective-permute-start) | collective-permute-done | bytes 8224 | tf_op jit(solution)/shard_map/ppermute | solution.py:17
  55.1 1.5 %collective-permute-start.1 = (f32[32,64]{1,0:T(8,128)S(1)}, f32[32,64]{1,0:T(8,128)S(1)}, u32[]{:S(2)}, u32[]{:S(2)}) collective-permute-start(f32[32,64]{1,0:T(8,128)S(1)} %add.41), channel_id=1, source_target_pairs={{0,2},{1,3},{2,0},{3,1},{4,6},{5,7},{6,4},{7,5},{8,10},{9,11},{10,... | collective-permute-start | bytes 24584 | tf_op jit(solution)/shard_map/ppermute | solution.py:17
  56.6 2.2 %collective-permute-done.1 = f32[32,64]{1,0:T(8,128)S(1)} collective-permute-done((f32[32,64]{1,0:T(8,128)S(1)}, f32[32,64]{1,0:T(8,128)S(1)}, u32[]{:S(2)}, u32[]{:S(2)}) %collective-permute-start.1) | collective-permute-done | bytes 8224 | tf_op jit(solution)/shard_map/ppermute | solution.py:17
  58.9 3.0 %collective-permute-start.2 = (f32[32,64]{1,0:T(8,128)S(1)}, f32[32,64]{1,0:T(8,128)S(1)}, u32[]{:S(2)}, u32[]{:S(2)}) collective-permute-start(f32[32,64]{1,0:T(8,128)S(1)} %add.42), channel_id=1, source_target_pairs={{0,4},{1,5},{2,6},{3,7},{4,0},{5,1},{6,2},{7,3},{8,12},{9,13},{10,... | collective-permute-start | bytes 24584 | tf_op jit(solution)/shard_map/ppermute | solution.py:17
  61.9 2.2 %collective-permute-done.2 = f32[32,64]{1,0:T(8,128)S(1)} collective-permute-done((f32[32,64]{1,0:T(8,128)S(1)}, f32[32,64]{1,0:T(8,128)S(1)}, u32[]{:S(2)}, u32[]{:S(2)}) %collective-permute-start.2) | collective-permute-done | bytes 8224 | tf_op jit(solution)/shard_map/ppermute | solution.py:17
  64.1 0.0 copy-done.2
  64.1 0.1 fusion.22
  64.3 1.1 %fusion.15 = f32[8,32,625]{2,1,0:T(8,128)} fusion(f32[8,32,625]{2,1,0:T(8,128)S(1)} %fusion.2, bf16[32,64,1]{1,0,2:T(8,128)(2,1)S(1)} %fusion.22, bf16[8,625,64]{1,2,0:T(8,128)(2,1)S(1)} %copy-done), kind=kOutput, calls=%fused_computation.15 | convolution fusion | flops 20640000 | bytes 1924096 | tf_op jit(solution)/shard_map/km,ebm->ekb/dot_general | solution.py:95
  (7 shorter events, 0.0 us)
Async XLA Ops:
  0.0 53.6 %copy-start = (bf16[8,625,64]{1,2,0:T(8,128)(2,1)S(1)}, bf16[8,625,64]{1,2,0:T(8,128)(2,1)}, u32[]{:S(2)}) copy-start(bf16[8,625,64]{1,2,0:T(8,128)(2,1)} %param.14) | copy-start | bytes 1920004
  19.1 28.8 %copy-start.1 = (bf16[8,32,625]{2,1,0:T(8,128)(2,1)S(1)}, bf16[8,32,625]{2,1,0:T(8,128)(2,1)}, u32[]{:S(2)}) copy-start(bf16[8,32,625]{2,1,0:T(8,128)(2,1)} %param.8) | copy-start | bytes 960004
  53.6 10.5 %copy-start.2 = (f32[1,64,64]{2,1,0:T(8,128)S(1)}, f32[1,64,64]{2,1,0:T(8,128)}, u32[]{:S(2)}) copy-start(f32[1,64,64]{2,1,0:T(8,128)} %param.15) | copy-start | bytes 49156
  53.9 1.2 %collective-permute-start = (f32[32,64]{1,0:T(8,128)S(1)}, f32[32,64]{1,0:T(8,128)S(1)}, u32[]{:S(2)}, u32[]{:S(2)}) collective-permute-start(f32[32,64]{1,0:T(8,128)S(1)} %convolution_bitcast_fusion.1), channel_id=1, source_target_pairs={{0,1},{1,0},{2,3},{3,2},{4,5},{5,4},{6,7},{7,6},{8,9},{9,8},{10,11... | collective-permute-start | bytes 24584 | tf_op jit(solution)/shard_map/ppermute | solution.py:17
  55.1 3.7 %collective-permute-start.1 = (f32[32,64]{1,0:T(8,128)S(1)}, f32[32,64]{1,0:T(8,128)S(1)}, u32[]{:S(2)}, u32[]{:S(2)}) collective-permute-start(f32[32,64]{1,0:T(8,128)S(1)} %add.41), channel_id=1, source_target_pairs={{0,2},{1,3},{2,0},{3,1},{4,6},{5,7},{6,4},{7,5},{8,10},{9,11},{10,... | collective-permute-start | bytes 24584 | tf_op jit(solution)/shard_map/ppermute | solution.py:17
  58.9 5.2 %collective-permute-start.2 = (f32[32,64]{1,0:T(8,128)S(1)}, f32[32,64]{1,0:T(8,128)S(1)}, u32[]{:S(2)}, u32[]{:S(2)}) collective-permute-start(f32[32,64]{1,0:T(8,128)S(1)} %add.42), channel_id=1, source_target_pairs={{0,4},{1,5},{2,6},{3,7},{4,0},{5,1},{6,2},{7,3},{8,12},{9,13},{10,... | collective-permute-start | bytes 24584 | tf_op jit(solution)/shard_map/ppermute | solution.py:17

commit v2 on v1

--- a/solution.py
+++ b/solution.py
@@ -78,14 +78,20 @@
         "es,skc->ekc", selector, products, preferred_element_type=jnp.float32
     )
     corrected_in = (residual_in.astype(jnp.float32) - coupled).astype(jnp.bfloat16)
+    projected = jnp.einsum(
+        "ebc,ecm->ebm", block_inverse, interface_basis, preferred_element_type=jnp.float32
+    )
+    projected_hi = projected.astype(jnp.bfloat16)
+    projected_lo = (projected - projected_hi.astype(jnp.float32)).astype(jnp.bfloat16)
+    partial_reduced = jnp.einsum(
+        "ekb,ebm->km", corrected_in, projected_hi, preferred_element_type=jnp.float32
+    ) + jnp.einsum(
+        "ekb,ebm->km", corrected_in, projected_lo, preferred_element_type=jnp.float32
+    )
+    reduced = group_sum(partial_reduced, "grp")
     second = jnp.einsum(
         "ekb,ebc->ekc", corrected_in, block_inverse, preferred_element_type=jnp.float32
     )
-    second_b = second.astype(jnp.bfloat16)
-    partial_reduced = jnp.einsum(
-        "ekb,ebm->km", second_b, interface_basis, preferred_element_type=jnp.float32
-    )
-    reduced = group_sum(partial_reduced, "grp")
     solved = jnp.dot(
         reduced,
         reduced_inverse[0],

time: 65.6 us -> 66.3 us (1.011)
  blocking collectives: 28.1 us -> 0 us
  waiting for transfers between devices: 5.65 us -> 19.3 us
  starting transfers between devices: 4.52 us -> 12.8 us
  matrix products: 21.4 us -> 27.7 us
  local copies, waits for them, and re-layouts: 1.46 us -> 2.52 us
    all_to_all x1 -> x0, blocking collectives: 28.1 us -> none  [shards(): lax.all_to_all(product_buffer.reshape(regions, CAP, vectors, padded), 'do...]
    all_to_all x0 -> x1, waiting for transfers between devices: none -> 15.9 us  [shards(): lax.all_to_all(product_buffer.reshape(regions, CAP, vectors, padded), 'do...]
    all_to_all x0 -> x1, starting transfers between devices: none -> 8.16 us  [shards(): lax.all_to_all(product_buffer.reshape(regions, CAP, vectors, padded), 'do...]
    dot_general x1 -> x3, matrix products: 0.3 us -> 5.63 us  [the longest x1 5.04 us: shards(): jnp.einsum('ebc,ecm->ebm', block_inverse, interface_basis, preferred_elem...]
    ppermute x3, waiting for transfers between devices: 5.65 us -> 3.42 us  [group_sum(): value = value + lax.ppermute(value, axis, pairs)]
    gather x1, local copies, waits for them, and re-layouts: 0.78 us -> 1.76 us  [shards(): product_buffer = extended[slot_tile]]
    dot_general x1, matrix products: 0.5 us -> 1.48 us  [shards(): jnp.einsum('es,skc->ekc', selector, products, preferred_element_type=jnp....]
  transfers between devices with their start and end apart: 3 -> 4, of which waited for: 3 -> 3; matrix products, arithmetic and copies ran while one was open for 0% -> 15% of each run, Pallas kernels for 0% -> 0%
where the time goes in v2:
time: 66.3 us; the launch traced here: 65.9 us
  matrix products  27.7 us (42%)
  waiting for transfers between devices  19.3 us (29%)
  starting transfers between devices  12.8 us (19%)
  other arithmetic  3.51 us (5%)
  local copies, waits for them, and re-layouts  2.52 us (4%)
    all_to_all x1, waiting for transfers between devices, shards(): lax.all_to_all(product_buffer.reshape(regions, CAP, vectors, padded), 'do...  15.9 us
    dot_general x1, matrix products, shards(): jnp.einsum('tkb,tbc->tkc', sources, coupling, preferred_element_type=jnp....  9.08 us
    all_to_all x1, starting transfers between devices, shards(): lax.all_to_all(product_buffer.reshape(regions, CAP, vectors, padded), 'do...  8.16 us
    dot_general x1, matrix products, shards(): jnp.einsum('ekb,ebc->ekc', residual_in, block_inverse, preferred_element_...  5.17 us
    dot_general x1, matrix products, shards(): jnp.einsum('ekb,ebc->ekc', corrected_in, block_inverse, preferred_element...  5.13 us
    dot_general x1, matrix products, shards(): jnp.einsum('ebc,ecm->ebm', block_inverse, interface_basis, preferred_elem...  5.04 us
    ppermute x3, starting transfers between devices, group_sum(): value = value + lax.ppermute(value, axis, pairs)  4.6 us
    ppermute x3, waiting for transfers between devices, group_sum(): value = value + lax.ppermute(value, axis, pairs)  3.42 us
  transfers between devices with their start and end apart: 4, of which 3 were waited for; matrix products, arithmetic and copies ran while one was open for 15% of the time, Pallas kernels for 0%

profile of v2, /device:TPU:0, one launch (start us, length us, event | category | flops | bytes accessed | tf_op | source)
XLA Modules:
  0.0 65.9 jit_solution(6531494646789645366)
XLA Ops:
  0.0 0.0 copy-start
  0.0 0.9 %convert_reduce_fusion.1 = s32[16]{0:T(128)S(1)} fusion(s32[16]{0:T(128)} %bitcast.34), kind=kLoop, calls=%fused_computation.39 | loop fusion | flops 1264 | bytes 128 | tf_op jit(solution)/shard_map/reduce_sum | solution.py:45
  0.9 0.7 %multiply_add_fusion = s32[16]{0:T(128)S(1)} fusion(s32[16]{0:T(128)S(1)} %convert_reduce_fusion.1, s32[16,1]{0,1:T(1,128)} %param.11), kind=kLoop, calls=%fused_computation.51 | loop fusion | flops 32 | bytes 192 | tf_op jit(solution)/shard_map/add | solution.py:46
  1.6 0.1 select_reduce_fusion
  1.7 0.1 fusion.34
  1.8 0.7 %compare_select_fusion.1 = s32[16]{0:T(128)S(1)} fusion(s32[16]{0:T(128)} %param.12), kind=kLoop, calls=%fused_computation.47 | loop fusion | flops 48 | bytes 128 | tf_op jit(solution)/shard_map/select_n | solution.py:52
  2.4 0.7 convert.5
  3.1 0.1 pad_maximum_fusion
  3.2 5.2 %fusion.21 = bf16[8,32,625]{2,1,0:T(8,128)(2,1)S(1)} fusion(bf16[8,32,625]{2,1,0:T(8,128)(2,1)} %param.8, bf16[8,625,625]{2,0,1:T(8,128)(2,1)} %param.9), kind=kOutput, calls=%fused_computation.20 | convolution fusion | flops 200160000 | bytes 6890000 | tf_op jit(solution)/shard_map/ekb,ebc->ekc/dot_general | solution.py:39
  8.4 0.7 %gather_fusion = bf16[16,32,625]{2,1,0:T(8,128)(2,1)S(1)} fusion(bf16[8,32,625]{2,1,0:T(8,128)(2,1)S(1)} %fusion.21, s32[1024]{0:T(1024)S(1)} %pad_clamp_fusion.1), kind=kCustom, calls=%fused_computation | custom fusion | bytes 1280064 | tf_op jit(solution)/shard_map/gather | solution.py:52
  9.1 9.1 %fusion.9 = bf16[16,32,625]{2,1,0:T(8,128)(2,1)S(1)} fusion(bf16[16,32,625]{2,1,0:T(8,128)(2,1)S(1)} %gather_fusion, bf16[16,625,625]{2,0,1:T(8,128)(2,1)} %param.10), kind=kOutput, calls=%fused_computation.12 | convolution fusion | flops 400320000 | bytes 13780000 | tf_op jit(solution)/shard_map/tkb,tbc->tkc/dot_general | solution.py:53
  18.1 0.1 and_select_fusion
  18.2 0.1 fusion.26
  18.4 1.8 %gather_fusion.1 = bf16[32,32,640]{2,1,0:T(8,128)(2,1)} fusion(bf16[17,32,640]{2,1,0:T(8,128)(2,1)S(1)} %fusion.26, s32[1024]{0:T(1024)S(1)} %pad_clamp_fusion), kind=kCustom, calls=%fused_computation.1 | custom fusion | bytes 2621568 | tf_op jit(solution)/shard_map/gather | solution.py:64
  20.1 8.2 %all-to-all-start = ((bf16[16,2,32,640]{3,2,1,0:T(8,128)(2,1)}), bf16[16,2,32,640]{3,2,1,0:T(8,128)(2,1)S(1)}, u32[]{:S(2)}, u32[]{:S(2)}) async-start(bf16[16,2,32,640]{3,2,1,0:T(8,128)(2,1)} %bitcast.3), calls=%async_computation | async-start | bytes 2621440 | tf_op jit(solution)/shard_map/all_to_all | solution.py:65
  28.3 0.0 copy-done
  28.3 5.0 %fusion.2 = f32[8,625,64]{1,2,0:T(8,128)S(1)} fusion(bf16[8,625,64]{1,2,0:T(8,128)(2,1)S(1)} %copy-done, bf16[8,625,625]{2,0,1:T(8,128)(2,1)} %param.9), kind=kOutput, calls=%fused_computation.4 | convolution fusion | flops 400000000 | bytes 8170000 | tf_op jit(solution)/shard_map/ebc,ecm->ebm/dot_general | solution.py:81
  33.3 15.9 %all-to-all-done = bf16[16,2,32,640]{3,2,1,0:T(8,128)(2,1)S(1)} async-done(((bf16[16,2,32,640]{3,2,1,0:T(8,128)(2,1)}), bf16[16,2,32,640]{3,2,1,0:T(8,128)(2,1)S(1)}, u32[]{:S(2)}, u32[]{:S(2)}) %all-to-all-start) | async-done | bytes 1310752 | tf_op jit(solution)/shard_map/all_to_all | solution.py:65
  49.2 0.1 slice.12
  49.3 0.1 convert_reduce_fusion
  49.4 1.5 %fusion.18 = bf16[8,32,625]{2,0,1:T(8,128)(2,1)S(1)} fusion(bf16[32,32,625]{2,1,0:T(8,128)(2,1)S(1)} %bitcast.33, bf16[8,32,625]{2,1,0:T(8,128)(2,1)} %param.8, s32[32]{0:T(128)S(1)} %convert_reduce_fusion), kind=kOutput, calls=%fused_computation.19 | convolution fusion | flops 10720256 | bytes 1920128 | tf_op jit(solution)/shard_map/es,skc->ekc/dot_general | solution.py:77
  50.9 0.3 convolution_bitcast_fusion.2
  51.2 0.3 fusion.24
  51.5 0.1 collective-permute-start
  51.6 1.2 %collective-permute-done = f32[32,64]{1,0:T(8,128)S(1)} collective-permute-done((f32[32,64]{1,0:T(8,128)S(1)}, f32[32,64]{1,0:T(8,128)S(1)}, u32[]{:S(2)}, u32[]{:S(2)}) %collective-permute-start) | collective-permute-done | bytes 8224 | tf_op jit(solution)/shard_map/ppermute | solution.py:17
  52.8 1.5 %collective-permute-start.1 = (f32[32,64]{1,0:T(8,128)S(1)}, f32[32,64]{1,0:T(8,128)S(1)}, u32[]{:S(2)}, u32[]{:S(2)}) collective-permute-start(f32[32,64]{1,0:T(8,128)S(1)} %add.45), channel_id=1, source_target_pairs={{0,2},{1,3},{2,0},{3,1},{4,6},{5,7},{6,4},{7,5},{8,10},{9,11},{10,... | collective-permute-start | bytes 24584 | tf_op jit(solution)/shard_map/ppermute | solution.py:17
  54.3 2.2 %collective-permute-done.1 = f32[32,64]{1,0:T(8,128)S(1)} collective-permute-done((f32[32,64]{1,0:T(8,128)S(1)}, f32[32,64]{1,0:T(8,128)S(1)}, u32[]{:S(2)}, u32[]{:S(2)}) %collective-permute-start.1) | collective-permute-done | bytes 8224 | tf_op jit(solution)/shard_map/ppermute | solution.py:17
  56.5 0.0 copy-start.1
  56.5 3.0 %collective-permute-start.2 = (f32[32,64]{1,0:T(8,128)S(1)}, f32[32,64]{1,0:T(8,128)S(1)}, u32[]{:S(2)}, u32[]{:S(2)}) collective-permute-start(f32[32,64]{1,0:T(8,128)S(1)} %add.46), channel_id=1, source_target_pairs={{0,4},{1,5},{2,6},{3,7},{4,0},{5,1},{6,2},{7,3},{8,12},{9,13},{10,... | collective-permute-start | bytes 24584 | tf_op jit(solution)/shard_map/ppermute | solution.py:17
  59.5 5.1 %fusion.4 = f32[8,32,625]{2,1,0:T(8,128)S(1)} fusion(bf16[8,625,625]{2,0,1:T(8,128)(2,1)} %param.9, bf16[8,32,625]{2,0,1:T(8,128)(2,1)S(1)} %fusion.18), kind=kOutput, calls=%fused_computation.6 | convolution fusion | flops 200000000 | bytes 7210000 | tf_op jit(solution)/shard_map/ekb,ebc->ekc/dot_general | solution.py:92
  64.7 0.0 collective-permute-done.2
  64.7 0.0 copy-done.1
  64.7 0.1 fusion.25
  64.8 1.1 %fusion.17 = f32[8,32,625]{2,1,0:T(8,128)} fusion(f32[8,32,625]{2,1,0:T(8,128)S(1)} %fusion.4, bf16[32,64,1]{1,0,2:T(8,128)(2,1)S(1)} %fusion.25, bf16[8,625,64]{1,2,0:T(8,128)(2,1)S(1)} %copy-done), kind=kOutput, calls=%fused_computation.18 | convolution fusion | flops 20640000 | bytes 1924096 | tf_op jit(solution)/shard_map/km,ebm->ekb/dot_general | solution.py:101
  (7 shorter events, 0.0 us)
Async XLA Ops:
  0.0 28.3 %copy-start = (bf16[8,625,64]{1,2,0:T(8,128)(2,1)S(1)}, bf16[8,625,64]{1,2,0:T(8,128)(2,1)}, u32[]{:S(2)}) copy-start(bf16[8,625,64]{1,2,0:T(8,128)(2,1)} %param.14) | copy-start | bytes 1920004
  20.1 29.1 %all-to-all-start = ((bf16[16,2,32,640]{3,2,1,0:T(8,128)(2,1)}), bf16[16,2,32,640]{3,2,1,0:T(8,128)(2,1)S(1)}, u32[]{:S(2)}, u32[]{:S(2)}) async-start(bf16[16,2,32,640]{3,2,1,0:T(8,128)(2,1)} %bitcast.3), calls=%async_computation | async-start | bytes 2621440 | tf_op jit(solution)/shard_map/all_to_all | solution.py:65
  51.5 1.3 %collective-permute-start = (f32[32,64]{1,0:T(8,128)S(1)}, f32[32,64]{1,0:T(8,128)S(1)}, u32[]{:S(2)}, u32[]{:S(2)}) collective-permute-start(f32[32,64]{1,0:T(8,128)S(1)} %fusion.24), channel_id=1, source_target_pairs={{0,1},{1,0},{2,3},{3,2},{4,5},{5,4},{6,7},{7,6},{8,9},{9,8},{10,11... | collective-permute-start | bytes 24584 | tf_op jit(solution)/shard_map/ppermute | solution.py:17
  52.8 3.7 %collective-permute-start.1 = (f32[32,64]{1,0:T(8,128)S(1)}, f32[32,64]{1,0:T(8,128)S(1)}, u32[]{:S(2)}, u32[]{:S(2)}) collective-permute-start(f32[32,64]{1,0:T(8,128)S(1)} %add.45), channel_id=1, source_target_pairs={{0,2},{1,3},{2,0},{3,1},{4,6},{5,7},{6,4},{7,5},{8,10},{9,11},{10,... | collective-permute-start | bytes 24584 | tf_op jit(solution)/shard_map/ppermute | solution.py:17
  56.5 8.2 %copy-start.1 = (f32[1,64,64]{2,1,0:T(8,128)S(1)}, f32[1,64,64]{2,1,0:T(8,128)}, u32[]{:S(2)}) copy-start(f32[1,64,64]{2,1,0:T(8,128)} %param.15) | copy-start | bytes 49156
  56.5 8.2 %collective-permute-start.2 = (f32[32,64]{1,0:T(8,128)S(1)}, f32[32,64]{1,0:T(8,128)S(1)}, u32[]{:S(2)}, u32[]{:S(2)}) collective-permute-start(f32[32,64]{1,0:T(8,128)S(1)} %add.46), channel_id=1, source_target_pairs={{0,4},{1,5},{2,6},{3,7},{4,0},{5,1},{6,2},{7,3},{8,12},{9,13},{10,... | collective-permute-start | bytes 24584 | tf_op jit(solution)/shard_map/ppermute | solution.py:17

commit v3 on v2

--- a/solution.py
+++ b/solution.py
@@ -39,7 +39,12 @@
     initial = jnp.einsum(
         "ekb,ebc->ekc", residual_in, block_inverse, preferred_element_type=jnp.float32
     ).astype(jnp.bfloat16)
-    destination = tile_region[:, 0]
+    info = lax.optimization_barrier(
+        jnp.concatenate([tile_region[:, 0], tile_source, tile_target])
+    )
+    destination = info[:tiles]
+    tile_source = info[tiles : 2 * tiles]
+    tile_target = info[2 * tiles :]
     order = jnp.arange(tiles, dtype=jnp.int32)
     same = destination[:, None] == destination[None, :]
     tile_rank = jnp.sum(same & (order[None, :] < order[:, None]), axis=1).astype(jnp.int32)
@@ -89,8 +94,23 @@
         "ekb,ebm->km", corrected_in, projected_lo, preferred_element_type=jnp.float32
     )
     reduced = group_sum(partial_reduced, "grp")
-    second = jnp.einsum(
-        "ekb,ebc->ekc", corrected_in, block_inverse, preferred_element_type=jnp.float32
+    half = elements // 2
+    second = jnp.concatenate(
+        [
+            jnp.einsum(
+                "ekb,ebc->ekc",
+                corrected_in[:half],
+                block_inverse[:half],
+                preferred_element_type=jnp.float32,
+            ),
+            jnp.einsum(
+                "ekb,ebc->ekc",
+                corrected_in[half:],
+                block_inverse[half:],
+                preferred_element_type=jnp.float32,
+            ),
+        ],
+        axis=0,
     )
     solved = jnp.dot(
         reduced,

time: 66.3 us -> 65 us (0.980)
  local copies, waits for them, and re-layouts: 2.52 us -> 10.2 us
  waiting for transfers between devices: 19.3 us -> 14.1 us
  matrix products: 27.7 us -> 25.8 us
  other arithmetic: 3.51 us -> 1.7 us
    unnamed x4 -> x15, local copies, waits for them, and re-layouts: 0.01 us -> 6.54 us
    all_to_all x1, waiting for transfers between devices: 15.9 us -> 11.2 us  [shards(): lax.all_to_all(product_buffer.reshape(regions, CAP, vectors, padded), 'do...]
    dot_general x1 -> x2, matrix products: 5.13 us -> 3.16 us  [the longest x1 2.54 us: shards(): jnp.einsum('ekb,ebc->ekc', corrected_in[:half], block_inverse[:half], pre...]
    dot_general x1, matrix products: 5.04 us -> 3.28 us  [shards(): jnp.einsum('ebc,ecm->ebm', block_inverse, interface_basis, preferred_elem...]
    dot_general x1, matrix products: 0.29 us -> 1.75 us  [shards(): jnp.einsum('ekb,ebm->km', corrected_in, projected_hi, preferred_element_t...]
    slice x1, local copies, waits for them, and re-layouts: 0.09 us -> 0.92 us  [shards(): targets = received[:, 0, width].astype(jnp.int32)]
    concatenate x0 -> x1, other arithmetic: none -> 0.83 us  [shards(): jnp.concatenate([tile_region[:, 0], tile_source, tile_target])]
    reduce_sum x1, other arithmetic: 0.92 us -> 0.18 us  [shards(): jnp.sum(same & (order[None, :] < order[:, None]), axis=1).astype(jnp.int32)]
  transfers between devices with their start and end apart: 4 -> 4, of which waited for: 3 -> 3; matrix products, arithmetic and copies ran while one was open for 15% -> 20% of each run, Pallas kernels for 0% -> 0%
where the time goes in v3:
time: 65 us; the launch traced here: 64.7 us
  matrix products  25.8 us (40%)
  waiting for transfers between devices  14.1 us (22%)
  starting transfers between devices  12.7 us (20%)
  local copies, waits for them, and re-layouts  10.2 us (16%)
  other arithmetic  1.7 us (3%)
    all_to_all x1, waiting for transfers between devices, shards(): lax.all_to_all(product_buffer.reshape(regions, CAP, vectors, padded), 'do...  11.2 us
    dot_general x1, matrix products, shards(): jnp.einsum('tkb,tbc->tkc', sources, coupling, preferred_element_type=jnp....  9.07 us
    all_to_all x1, starting transfers between devices, shards(): lax.all_to_all(product_buffer.reshape(regions, CAP, vectors, padded), 'do...  8.34 us
    unnamed x15, local copies, waits for them, and re-layouts  6.54 us
    dot_general x1, matrix products, shards(): jnp.einsum('ekb,ebc->ekc', residual_in, block_inverse, preferred_element_...  5.17 us
    ppermute x3, starting transfers between devices, group_sum(): value = value + lax.ppermute(value, axis, pairs)  4.38 us
    dot_general x1, matrix products, shards(): jnp.einsum('ebc,ecm->ebm', block_inverse, interface_basis, preferred_elem...  3.28 us
    ppermute x3, waiting for transfers between devices, group_sum(): value = value + lax.ppermute(value, axis, pairs)  2.95 us
  transfers between devices with their start and end apart: 4, of which 3 were waited for; matrix products, arithmetic and copies ran while one was open for 20% of the time, Pallas kernels for 0%

profile of v3, /device:TPU:0, one launch (start us, length us, event | category | flops | bytes accessed | tf_op | source)
XLA Modules:
  0.0 64.7 jit_solution(6608107481429199942)
XLA Ops:
  0.0 0.0 copy-start
  0.0 0.8 %pad_add_fusion = s32[48]{0:T(128)S(1)} fusion(s32[16]{0:T(128)} %param.13, s32[16]{0:T(128)} %param.12, s32[16]{0:T(128)} %bitcast.36), kind=kLoop, calls=%fused_computation.49 | loop fusion | flops 96 | bytes 384 | tf_op jit(solution)/shard_map/concatenate | solution.py:43
  0.8 0.2 convert_reduce_fusion.1
  1.0 0.1 multiply_add_fusion
  1.1 0.1 select_reduce_fusion
  1.2 0.1 fusion.30
  1.3 0.1 slice.29
  1.4 0.1 pad_maximum_fusion
  1.5 5.2 %convolution_convert_fusion = bf16[8,32,625]{2,1,0:T(8,128)(2,1)S(1)} fusion(bf16[8,32,625]{2,1,0:T(8,128)(2,1)} %param.8, bf16[8,625,625]{2,0,1:T(8,128)(2,1)} %param.9), kind=kOutput, calls=%fused_computation.18 | convolution fusion | flops 200160000 | bytes 6890000 | tf_op jit(solution)/shard_map/ekb,ebc->ekc/dot_general | solution.py:39
  6.6 0.7 %gather_fusion = bf16[16,32,625]{2,1,0:T(8,128)(2,1)S(1)} fusion(bf16[8,32,625]{2,1,0:T(8,128)(2,1)S(1)} %convolution_convert_fusion, s32[1024]{0:T(1024)S(1)} %pad_clamp_fusion.1), kind=kCustom, calls=%fused_computation | custom fusion | bytes 1280064 | tf_op jit(solution)/shard_map/gather | solution.py:57
  7.3 9.1 %fusion.7 = bf16[16,32,625]{2,1,0:T(8,128)(2,1)S(1)} fusion(bf16[16,32,625]{2,1,0:T(8,128)(2,1)S(1)} %gather_fusion, bf16[16,625,625]{2,0,1:T(8,128)(2,1)} %param.10), kind=kOutput, calls=%fused_computation.10 | convolution fusion | flops 400320000 | bytes 13780000 | tf_op jit(solution)/shard_map/tkb,tbc->tkc/dot_general | solution.py:58
  16.4 0.1 and_select_fusion
  16.5 0.1 fusion.21
  16.6 1.9 %gather_fusion.1 = bf16[32,32,640]{2,1,0:T(8,128)(2,1)} fusion(bf16[17,32,640]{2,1,0:T(8,128)(2,1)S(1)} %fusion.21, s32[1024]{0:T(1024)S(1)} %pad_clamp_fusion), kind=kCustom, calls=%fused_computation.1 | custom fusion | bytes 2621568 | tf_op jit(solution)/shard_map/gather | solution.py:69
  18.5 0.0 slice-start
  18.5 8.3 %all-to-all-start = ((bf16[16,2,32,640]{3,2,1,0:T(8,128)(2,1)}), bf16[16,2,32,640]{3,2,1,0:T(8,128)(2,1)}, u32[]{:S(2)}, u32[]{:S(2)}) async-start(bf16[16,2,32,640]{3,2,1,0:T(8,128)(2,1)} %bitcast.34), calls=%async_computation | async-start | bytes 2621440 | tf_op jit(solution)/shard_map/all_to_all | solution.py:70
  26.8 0.0 slice-start.1
  26.8 6.5 %copy.30 = bf16[8,625,625]{2,1,0:T(8,128)(2,1)} copy(bf16[8,625,625]{2,0,1:T(8,128)(2,1)} %param.9) | data formatting | bytes 12500000 | tf_op args[1]
  33.3 0.0 copy-done
  33.3 0.0 slice-done
  33.3 0.0 slice-done.1
  33.4 0.0 copy-start.3
  33.4 3.3 %fusion.36 = f32[8,625,64]{1,2,0:T(8,128)} fusion(bf16[8,625,64]{1,2,0:T(8,128)(2,1)S(1)} %copy-done, bf16[8,625,625]{2,0,1:T(8,128)(2,1)S(1)} %bitcast.33), kind=kOutput, calls=%fused_computation.54 | convolution fusion | flops 400000000 | bytes 8170000 | tf_op jit(solution)/shard_map/ebc,ecm->ebm/dot_general | solution.py:86
  36.7 0.0 copy-start.2
  36.7 11.2 %all-to-all-done = bf16[16,2,32,640]{3,2,1,0:T(8,128)(2,1)} async-done(((bf16[16,2,32,640]{3,2,1,0:T(8,128)(2,1)}), bf16[16,2,32,640]{3,2,1,0:T(8,128)(2,1)}, u32[]{:S(2)}, u32[]{:S(2)}) %all-to-all-start) | async-done | bytes 1310752 | tf_op jit(solution)/shard_map/all_to_all | solution.py:70
  47.8 0.9 %slice.41 = bf16[32,1,1]{2,1,0:T(2,128)(2,1)S(1)} slice(bf16[32,32,640]{2,1,0:T(8,128)(2,1)} %bitcast.4), slice={[0:32], [0:1], [625:626]} | slice | bytes 128 | tf_op jit(solution)/shard_map/slice | solution.py:77
  48.7 0.1 convert_reduce_fusion
  48.9 0.0 copy-done.3
  48.9 1.8 %fusion.16 = bf16[8,32,625]{2,0,1:T(8,128)(2,1)S(1)} fusion(bf16[32,32,625]{2,1,0:T(8,128)(2,1)} %bitcast.31, bf16[8,32,625]{2,1,0:T(8,128)(2,1)S(1)} %copy-done.3, s32[32]{0:T(128)S(1)} %convert_reduce_fusion), kind=kOutput, calls=%fused_computation.17 | convolution fusion | flops 10720256 | bytes 1920128 | tf_op jit(solution)/shard_map/es,skc->ekc/dot_general | solution.py:82
  50.7 0.0 copy-start.1
  50.7 1.8 %convolution_bitcast_fusion.2 = f32[32,64]{1,0:T(8,128)S(1)} fusion(f32[8,625,64]{1,2,0:T(8,128)} %fusion.36, bf16[8,32,625]{2,0,1:T(8,128)(2,1)S(1)} %fusion.16), kind=kOutput, calls=%fused_computation.21 | convolution fusion | flops 20800000 | bytes 1608192 | tf_op jit(solution)/shard_map/ekb,ebm->km/dot_general | solution.py:91
  52.5 0.0 copy-done.2
  52.5 0.3 fusion.19
  52.8 0.1 collective-permute-start
  52.9 0.1 fusion.39
  53.0 1.1 %collective-permute-done = f32[32,64]{1,0:T(8,128)S(1)} collective-permute-done((f32[32,64]{1,0:T(8,128)S(1)}, f32[32,64]{1,0:T(8,128)S(1)}, u32[]{:S(2)}, u32[]{:S(2)}) %collective-permute-start) | collective-permute-done | bytes 8224 | tf_op jit(solution)/shard_map/ppermute | solution.py:17
  54.0 1.5 %collective-permute-start.1 = (f32[32,64]{1,0:T(8,128)S(1)}, f32[32,64]{1,0:T(8,128)S(1)}, u32[]{:S(2)}, u32[]{:S(2)}) collective-permute-start(f32[32,64]{1,0:T(8,128)S(1)} %add.41), channel_id=1, source_target_pairs={{0,2},{1,3},{2,0},{3,1},{4,6},{5,7},{6,4},{7,5},{8,10},{9,11},{10,... | collective-permute-start | bytes 24584 | tf_op jit(solution)/shard_map/ppermute | solution.py:17
  55.5 0.0 copy-start.4
  55.5 2.5 %fusion.4 = f32[4,32,625]{2,1,0:T(8,128)S(1)} fusion(bf16[8,625,625]{2,1,0:T(8,128)(2,1)} %copy.30, bf16[4,32,625]{2,0,1:T(4,128)(2,1)S(1)} %get-tuple-element.5), kind=kOutput, calls=%fused_computation.6 | convolution fusion | flops 100000000 | bytes 3715840 | tf_op jit(solution)/shard_map/ekb,ebc->ekc/dot_general | solution.py:100
  58.1 0.0 collective-permute-done.1
  58.1 2.8 %collective-permute-start.2 = (f32[32,64]{1,0:T(8,128)S(1)}, f32[32,64]{1,0:T(8,128)S(1)}, u32[]{:S(2)}, u32[]{:S(2)}) collective-permute-start(f32[32,64]{1,0:T(8,128)S(1)} %add.42), channel_id=1, source_target_pairs={{0,4},{1,5},{2,6},{3,7},{4,0},{5,1},{6,2},{7,3},{8,12},{9,13},{10,... | collective-permute-start | bytes 24584 | tf_op jit(solution)/shard_map/ppermute | solution.py:17
  60.9 0.0 copy-done.1
  60.9 0.6 fusion.2
  61.5 1.9 %collective-permute-done.2 = f32[32,64]{1,0:T(8,128)S(1)} collective-permute-done((f32[32,64]{1,0:T(8,128)S(1)}, f32[32,64]{1,0:T(8,128)S(1)}, u32[]{:S(2)}, u32[]{:S(2)}) %collective-permute-start.2) | collective-permute-done | bytes 8224 | tf_op jit(solution)/shard_map/ppermute | solution.py:17
  63.4 0.0 copy-done.4
  63.4 0.1 fusion.20
  63.6 1.1 %fusion.15 = f32[8,32,625]{2,1,0:T(8,128)} fusion(bf16[32,64,1]{1,0,2:T(8,128)(2,1)S(1)} %fusion.20, bf16[8,625,64]{1,2,0:T(8,128)(2,1)S(1)} %copy-done, f32[4,32,625]{2,1,0:T(8,128)S(1)} %fusion.2, f32[4,32,625]{2,1,0:T(8,128)S(1)} %fusion.4), kind=kOutput, calls=%fused_computation.16 | convolution fusion | flops 20800000 | bytes 1924096 | tf_op jit(solution)/shard_map/km,ebm->ekb/dot_general | solution.py:121
  (9 shorter events, 0.0 us)
Async XLA Ops:
  0.0 33.3 %copy-start = (bf16[8,625,64]{1,2,0:T(8,128)(2,1)S(1)}, bf16[8,625,64]{1,2,0:T(8,128)(2,1)}, u32[]{:S(2)}) copy-start(bf16[8,625,64]{1,2,0:T(8,128)(2,1)} %param.14) | copy-start | bytes 1920004
  18.5 14.9 %slice-start = ((s8[6400000]{0:T(1024)(128)(4,1)}), s8[2205696]{0:T(1024)(128)(4,1)S(1)}, s32[]{:S(2)}) async-start(s8[6400000]{0:T(1024)(128)(4,1)} %bitcast.32), calls=%async_computation.1 | async-start | bytes 4411392
  18.5 29.3 %all-to-all-start = ((bf16[16,2,32,640]{3,2,1,0:T(8,128)(2,1)}), bf16[16,2,32,640]{3,2,1,0:T(8,128)(2,1)}, u32[]{:S(2)}, u32[]{:S(2)}) async-start(bf16[16,2,32,640]{3,2,1,0:T(8,128)(2,1)} %bitcast.34), calls=%async_computation | async-start | bytes 2621440 | tf_op jit(solution)/shard_map/all_to_all | solution.py:70
  26.8 6.5 %slice-start.1 = ((s8[6400000]{0:T(1024)(128)(4,1)}), s8[4194304]{0:T(1024)(128)(4,1)S(1)}, s32[]{:S(2)}) async-start(s8[6400000]{0:T(1024)(128)(4,1)} %bitcast.32), calls=%async_computation.2 | async-start | bytes 8388608
  33.4 15.5 %copy-start.3 = (bf16[8,32,625]{2,1,0:T(8,128)(2,1)S(1)}, bf16[8,32,625]{2,1,0:T(8,128)(2,1)}, u32[]{:S(2)}) copy-start(bf16[8,32,625]{2,1,0:T(8,128)(2,1)} %param.8) | copy-start | bytes 960004
  36.7 15.8 %copy-start.2 = (f32[8,625,64]{1,2,0:T(8,128)S(1)}, f32[8,625,64]{1,2,0:T(8,128)}, u32[]{:S(2)}) copy-start(f32[8,625,64]{1,2,0:T(8,128)} %fusion.36) | copy-start | bytes 3840004
  50.7 10.2 %copy-start.1 = (bf16[8,625,625]{2,1,0:T(8,128)(2,1)S(1)}, bf16[8,625,625]{2,1,0:T(8,128)(2,1)}, u32[]{:S(2)}) copy-start(bf16[8,625,625]{2,1,0:T(8,128)(2,1)} %copy.30) | copy-start | bytes 18750004
  52.8 1.3 %collective-permute-start = (f32[32,64]{1,0:T(8,128)S(1)}, f32[32,64]{1,0:T(8,128)S(1)}, u32[]{:S(2)}, u32[]{:S(2)}) collective-permute-start(f32[32,64]{1,0:T(8,128)S(1)} %fusion.19), channel_id=1, source_target_pairs={{0,1},{1,0},{2,3},{3,2},{4,5},{5,4},{6,7},{7,6},{8,9},{9,8},{10,11... | collective-permute-start | bytes 24584 | tf_op jit(solution)/shard_map/ppermute | solution.py:17
  54.0 4.0 %collective-permute-start.1 = (f32[32,64]{1,0:T(8,128)S(1)}, f32[32,64]{1,0:T(8,128)S(1)}, u32[]{:S(2)}, u32[]{:S(2)}) collective-permute-start(f32[32,64]{1,0:T(8,128)S(1)} %add.41), channel_id=1, source_target_pairs={{0,2},{1,3},{2,0},{3,1},{4,6},{5,7},{6,4},{7,5},{8,10},{9,11},{10,... | collective-permute-start | bytes 24584 | tf_op jit(solution)/shard_map/ppermute | solution.py:17
  55.5 7.9 %copy-start.4 = (f32[1,64,64]{2,1,0:T(8,128)S(1)}, f32[1,64,64]{2,1,0:T(8,128)}, u32[]{:S(2)}) copy-start(f32[1,64,64]{2,1,0:T(8,128)} %param.15) | copy-start | bytes 49156
  58.1 5.3 %collective-permute-start.2 = (f32[32,64]{1,0:T(8,128)S(1)}, f32[32,64]{1,0:T(8,128)S(1)}, u32[]{:S(2)}, u32[]{:S(2)}) collective-permute-start(f32[32,64]{1,0:T(8,128)S(1)} %add.42), channel_id=1, source_target_pairs={{0,4},{1,5},{2,6},{3,7},{4,0},{5,1},{6,2},{7,3},{8,12},{9,13},{10,... | collective-permute-start | bytes 24584 | tf_op jit(solution)/shard_map/ppermute | solution.py:17

commit v4 on v3

--- a/solution.py
+++ b/solution.py
@@ -86,12 +86,11 @@
     projected = jnp.einsum(
         "ebc,ecm->ebm", block_inverse, interface_basis, preferred_element_type=jnp.float32
     )
-    projected_hi = projected.astype(jnp.bfloat16)
-    projected_lo = (projected - projected_hi.astype(jnp.float32)).astype(jnp.bfloat16)
     partial_reduced = jnp.einsum(
-        "ekb,ebm->km", corrected_in, projected_hi, preferred_element_type=jnp.float32
-    ) + jnp.einsum(
-        "ekb,ebm->km", corrected_in, projected_lo, preferred_element_type=jnp.float32
+        "ekb,ebm->km",
+        corrected_in,
+        projected.astype(jnp.bfloat16),
+        preferred_element_type=jnp.float32,
     )
     reduced = group_sum(partial_reduced, "grp")
     half = elements // 2

time: 65 us -> 66.1 us (1.017)
  waiting for transfers between devices: 14.1 us -> 15.6 us
  local copies, waits for them, and re-layouts: 10.2 us -> 9.11 us
    all_to_all x1, waiting for transfers between devices: 11.2 us -> 14.5 us  [shards(): lax.all_to_all(product_buffer.reshape(regions, CAP, vectors, padded), 'do...]
    dot_general x1, matrix products: 0.61 us -> 2.53 us  [shards(): jnp.einsum('ekb,ebc->ekc', corrected_in[half:], block_inverse[half:], pre...]
    ppermute x3, waiting for transfers between devices: 2.95 us -> 1.07 us  [group_sum(): value = value + lax.ppermute(value, axis, pairs)]
    dot_general x1, matrix products: 1.82 us -> 0.5 us  [shards(): jnp.einsum('es,skc->ekc', selector, products, preferred_element_type=jnp....]
    slice x1, local copies, waits for them, and re-layouts: 0.92 us -> 0.09 us  [shards(): targets = received[:, 0, width].astype(jnp.int32)]
    unnamed x15 -> x7, local copies, waits for them, and re-layouts: 6.54 us -> 6.42 us
    dot_general x3 -> x1, matrix products: 5.33 us -> 5.23 us  [shards(): jnp.einsum('ekb,ebm->km', corrected_in, projected.astype(jnp.bfloat16), p...]
  transfers between devices with their start and end apart: 4 -> 4, of which waited for: 3 -> 2; matrix products, arithmetic and copies ran while one was open for 20% -> 18% of each run, Pallas kernels for 0% -> 0%
where the time goes in v4:
time: 66.1 us; the launch traced here: 65.3 us
  matrix products  26.3 us (40%)
  waiting for transfers between devices  15.6 us (24%)
  starting transfers between devices  12.5 us (19%)
  local copies, waits for them, and re-layouts  9.11 us (14%)
  other arithmetic  1.7 us (3%)
    all_to_all x1, waiting for transfers between devices, shards(): lax.all_to_all(product_buffer.reshape(regions, CAP, vectors, padded), 'do...  14.5 us
    dot_general x1, matrix products, shards(): jnp.einsum('tkb,tbc->tkc', sources, coupling, preferred_element_type=jnp....  9.08 us
    all_to_all x1, starting transfers between devices, shards(): lax.all_to_all(product_buffer.reshape(regions, CAP, vectors, padded), 'do...  8.16 us
    unnamed x7, local copies, waits for them, and re-layouts  6.42 us
    dot_general x1, matrix products, shards(): jnp.einsum('ekb,ebm->km', corrected_in, projected.astype(jnp.bfloat16), p...  5.23 us
    dot_general x1, matrix products, shards(): jnp.einsum('ekb,ebc->ekc', residual_in, block_inverse, preferred_element_...  5.17 us
    ppermute x3, starting transfers between devices, group_sum(): value = value + lax.ppermute(value, axis, pairs)  4.32 us
    dot_general x1, matrix products, shards(): jnp.einsum('ekb,ebc->ekc', corrected_in[half:], block_inverse[half:], pre...  2.53 us
  transfers between devices with their start and end apart: 4, of which 2 were waited for; matrix products, arithmetic and copies ran while one was open for 18% of the time, Pallas kernels for 0%

profile of v4, /device:TPU:0, one launch (start us, length us, event | category | flops | bytes accessed | tf_op | source)
XLA Modules:
  0.0 65.3 jit_solution(11779110857407626924)
XLA Ops:
  0.0 0.0 copy-start
  0.0 0.8 %pad_add_fusion = s32[48]{0:T(128)S(1)} fusion(s32[16]{0:T(128)} %param.13, s32[16]{0:T(128)} %param.12, s32[16]{0:T(128)} %bitcast.31), kind=kLoop, calls=%fused_computation.45 | loop fusion | flops 96 | bytes 384 | tf_op jit(solution)/shard_map/concatenate | solution.py:43
  0.8 0.2 convert_reduce_fusion.1
  1.0 0.1 multiply_add_fusion
  1.1 0.1 select_reduce_fusion
  1.2 0.1 fusion.28
  1.3 0.1 slice.29
  1.4 0.1 pad_maximum_fusion
  1.5 5.2 %convolution_convert_fusion.1 = bf16[8,32,625]{2,1,0:T(8,128)(2,1)S(1)} fusion(bf16[8,32,625]{2,1,0:T(8,128)(2,1)} %param.8, bf16[8,625,625]{2,0,1:T(8,128)(2,1)} %param.9), kind=kOutput, calls=%fused_computation.19 | convolution fusion | flops 200160000 | bytes 6890000 | tf_op jit(solution)/shard_map/ekb,ebc->ekc/dot_general | solution.py:39
  6.6 0.7 %gather_fusion = bf16[16,32,625]{2,1,0:T(8,128)(2,1)S(1)} fusion(bf16[8,32,625]{2,1,0:T(8,128)(2,1)S(1)} %convolution_convert_fusion.1, s32[1024]{0:T(1024)S(1)} %pad_clamp_fusion.1), kind=kCustom, calls=%fused_computation | custom fusion | bytes 1280064 | tf_op jit(solution)/shard_map/gather | solution.py:57
  7.3 9.1 %fusion.7 = bf16[16,32,625]{2,1,0:T(8,128)(2,1)S(1)} fusion(bf16[16,32,625]{2,1,0:T(8,128)(2,1)S(1)} %gather_fusion, bf16[16,625,625]{2,0,1:T(8,128)(2,1)} %param.10), kind=kOutput, calls=%fused_computation.10 | convolution fusion | flops 400320000 | bytes 13780000 | tf_op jit(solution)/shard_map/tkb,tbc->tkc/dot_general | solution.py:58
  16.4 0.1 and_select_fusion
  16.5 0.1 fusion.22
  16.6 1.8 %gather_fusion.1 = bf16[32,32,640]{2,1,0:T(8,128)(2,1)} fusion(bf16[17,32,640]{2,1,0:T(8,128)(2,1)S(1)} %fusion.22, s32[1024]{0:T(1024)S(1)} %pad_clamp_fusion), kind=kCustom, calls=%fused_computation.1 | custom fusion | bytes 2621568 | tf_op jit(solution)/shard_map/gather | solution.py:69
  18.4 8.2 %all-to-all-start = ((bf16[16,2,32,640]{3,2,1,0:T(8,128)(2,1)}), bf16[16,2,32,640]{3,2,1,0:T(8,128)(2,1)S(1)}, u32[]{:S(2)}, u32[]{:S(2)}) async-start(bf16[16,2,32,640]{3,2,1,0:T(8,128)(2,1)} %bitcast.3), calls=%async_computation | async-start | bytes 2621440 | tf_op jit(solution)/shard_map/all_to_all | solution.py:70
  26.5 0.0 copy-start.1
  26.6 6.4 %copy.26 = bf16[8,625,625]{2,1,0:T(8,128)(2,1)} copy(bf16[8,625,625]{2,0,1:T(8,128)(2,1)} %param.9) | data formatting | bytes 12500000 | tf_op args[1]
  33.0 14.5 %all-to-all-done = bf16[16,2,32,640]{3,2,1,0:T(8,128)(2,1)S(1)} async-done(((bf16[16,2,32,640]{3,2,1,0:T(8,128)(2,1)}), bf16[16,2,32,640]{3,2,1,0:T(8,128)(2,1)S(1)}, u32[]{:S(2)}, u32[]{:S(2)}) %all-to-all-start) | async-done | bytes 1310752 | tf_op jit(solution)/shard_map/all_to_all | solution.py:70
  47.5 0.1 slice.41
  47.6 0.1 convert_reduce_fusion
  47.7 0.0 copy-done.1
  47.7 0.5 fusion.17
  48.2 0.0 copy-done
  48.2 5.2 %fusion.20 = f32[32,64]{1,0:T(8,128)S(1)} fusion(bf16[8,625,64]{1,2,0:T(8,128)(2,1)S(1)} %copy-done, bf16[8,32,625]{2,0,1:T(8,128)(2,1)S(1)} %fusion.17, bf16[8,625,625]{2,0,1:T(8,128)(2,1)} %param.9), kind=kOutput, calls=%fused_computation.20 | convolution fusion | flops 420800000 | bytes 7218192 | tf_op jit(solution)/shard_map/ekb,ebm->km/dot_general | solution.py:89
  53.4 0.0 copy-start.2
  53.4 0.0 collective-permute-start
  53.5 0.1 fusion.37
  53.6 1.1 %collective-permute-done = f32[32,64]{1,0:T(8,128)S(1)} collective-permute-done((f32[32,64]{1,0:T(8,128)S(1)}, f32[32,64]{1,0:T(8,128)S(1)}, u32[]{:S(2)}, u32[]{:S(2)}) %collective-permute-start) | collective-permute-done | bytes 8224 | tf_op jit(solution)/shard_map/ppermute | solution.py:17
  54.6 1.5 %collective-permute-start.1 = (f32[32,64]{1,0:T(8,128)S(1)}, f32[32,64]{1,0:T(8,128)S(1)}, u32[]{:S(2)}, u32[]{:S(2)}) collective-permute-start(f32[32,64]{1,0:T(8,128)S(1)} %add.37), channel_id=1, source_target_pairs={{0,2},{1,3},{2,0},{3,1},{4,6},{5,7},{6,4},{7,5},{8,10},{9,11},{10,... | collective-permute-start | bytes 24584 | tf_op jit(solution)/shard_map/ppermute | solution.py:17
  56.1 2.5 %fusion.4 = f32[4,32,625]{2,1,0:T(8,128)S(1)} fusion(bf16[8,625,625]{2,1,0:T(8,128)(2,1)} %copy.26, bf16[4,32,625]{2,0,1:T(4,128)(2,1)S(1)} %get-tuple-element.5), kind=kOutput, calls=%fused_computation.6 | convolution fusion | flops 100000000 | bytes 3715840 | tf_op jit(solution)/shard_map/ekb,ebc->ekc/dot_general | solution.py:99
  58.7 0.0 collective-permute-done.1
  58.7 2.8 %collective-permute-start.2 = (f32[32,64]{1,0:T(8,128)S(1)}, f32[32,64]{1,0:T(8,128)S(1)}, u32[]{:S(2)}, u32[]{:S(2)}) collective-permute-start(f32[32,64]{1,0:T(8,128)S(1)} %add.38), channel_id=1, source_target_pairs={{0,4},{1,5},{2,6},{3,7},{4,0},{5,1},{6,2},{7,3},{8,12},{9,13},{10,... | collective-permute-start | bytes 24584 | tf_op jit(solution)/shard_map/ppermute | solution.py:17
  61.5 2.5 %fusion.2 = f32[4,32,625]{2,1,0:T(8,128)S(1)} fusion(bf16[8,625,625]{2,1,0:T(8,128)(2,1)} %copy.26, bf16[4,32,625]{2,0,1:T(4,128)(2,1)S(1)} %get-tuple-element.6), kind=kOutput, calls=%fused_computation.4 | convolution fusion | flops 100000000 | bytes 3715840 | tf_op jit(solution)/shard_map/ekb,ebc->ekc/dot_general | solution.py:105
  64.0 0.0 collective-permute-done.2
  64.0 0.0 copy-done.2
  64.1 0.1 fusion.21
  64.2 1.1 %fusion.15 = f32[8,32,625]{2,1,0:T(8,128)} fusion(bf16[32,64,1]{1,0,2:T(8,128)(2,1)S(1)} %fusion.21, bf16[8,625,64]{1,2,0:T(8,128)(2,1)S(1)} %copy-done, f32[4,32,625]{2,1,0:T(8,128)S(1)} %fusion.2, f32[4,32,625]{2,1,0:T(8,128)S(1)} %fusion.4), kind=kOutput, calls=%fused_computation.16 | convolution fusion | flops 20800000 | bytes 1924096 | tf_op jit(solution)/shard_map/km,ebm->ekb/dot_general | solution.py:120
  (8 shorter events, 0.0 us)
Async XLA Ops:
  0.0 48.2 %copy-start = (bf16[8,625,64]{1,2,0:T(8,128)(2,1)S(1)}, bf16[8,625,64]{1,2,0:T(8,128)(2,1)}, u32[]{:S(2)}) copy-start(bf16[8,625,64]{1,2,0:T(8,128)(2,1)} %param.14) | copy-start | bytes 1920004
  18.4 29.1 %all-to-all-start = ((bf16[16,2,32,640]{3,2,1,0:T(8,128)(2,1)}), bf16[16,2,32,640]{3,2,1,0:T(8,128)(2,1)S(1)}, u32[]{:S(2)}, u32[]{:S(2)}) async-start(bf16[16,2,32,640]{3,2,1,0:T(8,128)(2,1)} %bitcast.3), calls=%async_computation | async-start | bytes 2621440 | tf_op jit(solution)/shard_map/all_to_all | solution.py:70
  26.5 21.1 %copy-start.1 = (bf16[8,32,625]{2,1,0:T(8,128)(2,1)S(1)}, bf16[8,32,625]{2,1,0:T(8,128)(2,1)}, u32[]{:S(2)}) copy-start(bf16[8,32,625]{2,1,0:T(8,128)(2,1)} %param.8) | copy-start | bytes 960004
  53.4 10.6 %copy-start.2 = (f32[1,64,64]{2,1,0:T(8,128)S(1)}, f32[1,64,64]{2,1,0:T(8,128)}, u32[]{:S(2)}) copy-start(f32[1,64,64]{2,1,0:T(8,128)} %param.15) | copy-start | bytes 49156
  53.4 1.2 %collective-permute-start = (f32[32,64]{1,0:T(8,128)S(1)}, f32[32,64]{1,0:T(8,128)S(1)}, u32[]{:S(2)}, u32[]{:S(2)}) collective-permute-start(f32[32,64]{1,0:T(8,128)S(1)} %fusion.20), channel_id=1, source_target_pairs={{0,1},{1,0},{2,3},{3,2},{4,5},{5,4},{6,7},{7,6},{8,9},{9,8},{10,11... | collective-permute-start | bytes 24584 | tf_op jit(solution)/shard_map/ppermute | solution.py:17
  54.6 4.0 %collective-permute-start.1 = (f32[32,64]{1,0:T(8,128)S(1)}, f32[32,64]{1,0:T(8,128)S(1)}, u32[]{:S(2)}, u32[]{:S(2)}) collective-permute-start(f32[32,64]{1,0:T(8,128)S(1)} %add.37), channel_id=1, source_target_pairs={{0,2},{1,3},{2,0},{3,1},{4,6},{5,7},{6,4},{7,5},{8,10},{9,11},{10,... | collective-permute-start | bytes 24584 | tf_op jit(solution)/shard_map/ppermute | solution.py:17
  58.7 5.3 %collective-permute-start.2 = (f32[32,64]{1,0:T(8,128)S(1)}, f32[32,64]{1,0:T(8,128)S(1)}, u32[]{:S(2)}, u32[]{:S(2)}) collective-permute-start(f32[32,64]{1,0:T(8,128)S(1)} %add.38), channel_id=1, source_target_pairs={{0,4},{1,5},{2,6},{3,7},{4,0},{5,1},{6,2},{7,3},{8,12},{9,13},{10,... | collective-permute-start | bytes 24584 | tf_op jit(solution)/shard_map/ppermute | solution.py:17

commit v5 on v4

--- a/solution.py
+++ b/solution.py
@@ -89,7 +89,7 @@
     partial_reduced = jnp.einsum(
         "ekb,ebm->km",
         corrected_in,
-        projected.astype(jnp.bfloat16),
+        lax.optimization_barrier(projected.astype(jnp.bfloat16)),
         preferred_element_type=jnp.float32,
     )
     reduced = group_sum(partial_reduced, "grp")

time: 66.1 us -> 63.3 us (0.958)
  matrix products: 26.3 us -> 23.1 us
  local copies, waits for them, and re-layouts: 9.11 us -> 10.1 us
    dot_general x1 -> x2, matrix products: 5.23 us -> 2.51 us  [the longest x1 2.22 us: shards(): jnp.einsum('ebc,ecm->ebm', block_inverse, interface_basis, preferred_elem...]
    all_to_all x1, waiting for transfers between devices: 14.5 us -> 12.2 us  [shards(): lax.all_to_all(product_buffer.reshape(regions, CAP, vectors, padded), 'do...]
    dot_general x1, matrix products: 2.53 us -> 0.61 us  [shards(): jnp.einsum('ekb,ebc->ekc', corrected_in[half:], block_inverse[half:], pre...]
    ppermute x3, waiting for transfers between devices: 1.07 us -> 2.96 us  [group_sum(): value = value + lax.ppermute(value, axis, pairs)]
    dot_general x1, matrix products: 0.5 us -> 2.02 us  [shards(): jnp.einsum('es,skc->ekc', selector, products, preferred_element_type=jnp....]
    slice x1, local copies, waits for them, and re-layouts: 0.09 us -> 0.92 us  [shards(): targets = received[:, 0, width].astype(jnp.int32)]
    unnamed x7 -> x11, local copies, waits for them, and re-layouts: 6.42 us -> 6.51 us
  transfers between devices with their start and end apart: 4 -> 4, of which waited for: 2 -> 3; matrix products, arithmetic and copies ran while one was open for 18% -> 19% of each run, Pallas kernels for 0% -> 0%
where the time goes in v5:
time: 63.3 us; the launch traced here: 63 us
  matrix products  23.1 us (36%)
  waiting for transfers between devices  15.2 us (24%)
  starting transfers between devices  12.6 us (20%)
  local copies, waits for them, and re-layouts  10.1 us (16%)
  other arithmetic  1.7 us (3%)
    all_to_all x1, waiting for transfers between devices, shards(): lax.all_to_all(product_buffer.reshape(regions, CAP, vectors, padded), 'do...  12.2 us
    dot_general x1, matrix products, shards(): jnp.einsum('tkb,tbc->tkc', sources, coupling, preferred_element_type=jnp....  9.07 us
    all_to_all x1, starting transfers between devices, shards(): lax.all_to_all(product_buffer.reshape(regions, CAP, vectors, padded), 'do...  8.34 us
    unnamed x11, local copies, waits for them, and re-layouts  6.51 us
    dot_general x1, matrix products, shards(): jnp.einsum('ekb,ebc->ekc', residual_in, block_inverse, preferred_element_...  5.17 us
    ppermute x3, starting transfers between devices, group_sum(): value = value + lax.ppermute(value, axis, pairs)  4.3 us
    ppermute x3, waiting for transfers between devices, group_sum(): value = value + lax.ppermute(value, axis, pairs)  2.96 us
    dot_general x1, matrix products, shards(): jnp.einsum('ekb,ebc->ekc', corrected_in[:half], block_inverse[:half], pre...  2.54 us
  transfers between devices with their start and end apart: 4, of which 3 were waited for; matrix products, arithmetic and copies ran while one was open for 19% of the time, Pallas kernels for 0%

profile of v5, /device:TPU:0, one launch (start us, length us, event | category | flops | bytes accessed | tf_op | source)
XLA Modules:
  0.0 63.0 jit_solution(6757530319987989328)
XLA Ops:
  0.0 0.0 copy-start
  0.0 0.8 %pad_add_fusion = s32[48]{0:T(128)S(1)} fusion(s32[16]{0:T(128)} %param.13, s32[16]{0:T(128)} %param.12, s32[16]{0:T(128)} %bitcast.33), kind=kLoop, calls=%fused_computation.44 | loop fusion | flops 96 | bytes 384 | tf_op jit(solution)/shard_map/concatenate | solution.py:43
  0.8 0.2 convert_reduce_fusion.1
  1.0 0.1 multiply_add_fusion
  1.1 0.1 select_reduce_fusion
  1.2 0.1 fusion.26
  1.3 0.1 slice.29
  1.4 0.1 pad_maximum_fusion
  1.5 5.2 %convolution_convert_fusion.1 = bf16[8,32,625]{2,1,0:T(8,128)(2,1)S(1)} fusion(bf16[8,32,625]{2,1,0:T(8,128)(2,1)} %param.8, bf16[8,625,625]{2,0,1:T(8,128)(2,1)} %param.9), kind=kOutput, calls=%fused_computation.18 | convolution fusion | flops 200160000 | bytes 6890000 | tf_op jit(solution)/shard_map/ekb,ebc->ekc/dot_general | solution.py:39
  6.6 0.7 %gather_fusion = bf16[16,32,625]{2,1,0:T(8,128)(2,1)S(1)} fusion(bf16[8,32,625]{2,1,0:T(8,128)(2,1)S(1)} %convolution_convert_fusion.1, s32[1024]{0:T(1024)S(1)} %pad_clamp_fusion.1), kind=kCustom, calls=%fused_computation | custom fusion | bytes 1280064 | tf_op jit(solution)/shard_map/gather | solution.py:57
  7.3 9.1 %fusion.7 = bf16[16,32,625]{2,1,0:T(8,128)(2,1)S(1)} fusion(bf16[16,32,625]{2,1,0:T(8,128)(2,1)S(1)} %gather_fusion, bf16[16,625,625]{2,0,1:T(8,128)(2,1)} %param.10), kind=kOutput, calls=%fused_computation.10 | convolution fusion | flops 400320000 | bytes 13780000 | tf_op jit(solution)/shard_map/tkb,tbc->tkc/dot_general | solution.py:58
  16.4 0.1 and_select_fusion
  16.5 0.1 fusion.20
  16.6 1.9 %gather_fusion.1 = bf16[32,32,640]{2,1,0:T(8,128)(2,1)} fusion(bf16[17,32,640]{2,1,0:T(8,128)(2,1)S(1)} %fusion.20, s32[1024]{0:T(1024)S(1)} %pad_clamp_fusion), kind=kCustom, calls=%fused_computation.1 | custom fusion | bytes 2621568 | tf_op jit(solution)/shard_map/gather | solution.py:69
  18.5 0.0 slice-start
  18.5 8.3 %all-to-all-start = ((bf16[16,2,32,640]{3,2,1,0:T(8,128)(2,1)}), bf16[16,2,32,640]{3,2,1,0:T(8,128)(2,1)}, u32[]{:S(2)}, u32[]{:S(2)}) async-start(bf16[16,2,32,640]{3,2,1,0:T(8,128)(2,1)} %bitcast.31), calls=%async_computation | async-start | bytes 2621440 | tf_op jit(solution)/shard_map/all_to_all | solution.py:70
  26.8 0.0 slice-start.1
  26.8 6.5 %copy.26 = bf16[8,625,625]{2,1,0:T(8,128)(2,1)} copy(bf16[8,625,625]{2,0,1:T(8,128)(2,1)} %param.9) | data formatting | bytes 12500000 | tf_op args[1]
  33.3 0.0 copy-done
  33.3 0.0 slice-done
  33.3 0.0 slice-done.1
  33.3 2.2 %convolution_convert_fusion = bf16[8,625,64]{1,2,0:T(8,128)(2,1)S(1)} fusion(bf16[8,625,64]{1,2,0:T(8,128)(2,1)S(1)} %copy-done, bf16[8,625,625]{2,0,1:T(8,128)(2,1)S(1)} %bitcast.30), kind=kOutput, calls=%fused_computation.11 | convolution fusion | flops 400320000 | bytes 7530000 | tf_op jit(solution)/shard_map/ebc,ecm->ebm/dot_general | solution.py:86
  35.6 12.2 %all-to-all-done = bf16[16,2,32,640]{3,2,1,0:T(8,128)(2,1)} async-done(((bf16[16,2,32,640]{3,2,1,0:T(8,128)(2,1)}), bf16[16,2,32,640]{3,2,1,0:T(8,128)(2,1)}, u32[]{:S(2)}, u32[]{:S(2)}) %all-to-all-start) | async-done | bytes 1310752 | tf_op jit(solution)/shard_map/all_to_all | solution.py:70
  47.8 0.9 %slice.41 = bf16[32,1,1]{2,1,0:T(2,128)(2,1)S(1)} slice(bf16[32,32,640]{2,1,0:T(8,128)(2,1)} %bitcast.4), slice={[0:32], [0:1], [625:626]} | slice | bytes 128 | tf_op jit(solution)/shard_map/slice | solution.py:77
  48.7 0.1 convert_reduce_fusion
  48.9 0.0 copy-start.1
  48.9 2.0 %fusion.16 = bf16[8,32,625]{2,0,1:T(8,128)(2,1)S(1)} fusion(bf16[32,32,625]{2,1,0:T(8,128)(2,1)} %bitcast.28, bf16[8,32,625]{2,1,0:T(8,128)(2,1)} %param.8, s32[32]{0:T(128)S(1)} %convert_reduce_fusion), kind=kOutput, calls=%fused_computation.17 | convolution fusion | flops 10720256 | bytes 1920128 | tf_op jit(solution)/shard_map/es,skc->ekc/dot_general | solution.py:82
  50.9 0.3 convolution_bitcast_fusion.1
  51.2 0.0 collective-permute-start
  51.2 0.1 fusion.34
  51.3 1.1 %collective-permute-done = f32[32,64]{1,0:T(8,128)S(1)} collective-permute-done((f32[32,64]{1,0:T(8,128)S(1)}, f32[32,64]{1,0:T(8,128)S(1)}, u32[]{:S(2)}, u32[]{:S(2)}) %collective-permute-start) | collective-permute-done | bytes 8224 | tf_op jit(solution)/shard_map/ppermute | solution.py:17
  52.4 1.5 %collective-permute-start.1 = (f32[32,64]{1,0:T(8,128)S(1)}, f32[32,64]{1,0:T(8,128)S(1)}, u32[]{:S(2)}, u32[]{:S(2)}) collective-permute-start(f32[32,64]{1,0:T(8,128)S(1)} %add.37), channel_id=1, source_target_pairs={{0,2},{1,3},{2,0},{3,1},{4,6},{5,7},{6,4},{7,5},{8,10},{9,11},{10,... | collective-permute-start | bytes 24584 | tf_op jit(solution)/shard_map/ppermute | solution.py:17
  53.9 0.0 copy-start.2
  53.9 2.5 %fusion.4 = f32[4,32,625]{2,1,0:T(8,128)S(1)} fusion(bf16[8,625,625]{2,1,0:T(8,128)(2,1)} %copy.26, bf16[4,32,625]{2,0,1:T(4,128)(2,1)S(1)} %get-tuple-element.5), kind=kOutput, calls=%fused_computation.6 | convolution fusion | flops 100000000 | bytes 3715840 | tf_op jit(solution)/shard_map/ekb,ebc->ekc/dot_general | solution.py:99
  56.4 0.0 collective-permute-done.1
  56.4 2.8 %collective-permute-start.2 = (f32[32,64]{1,0:T(8,128)S(1)}, f32[32,64]{1,0:T(8,128)S(1)}, u32[]{:S(2)}, u32[]{:S(2)}) collective-permute-start(f32[32,64]{1,0:T(8,128)S(1)} %add.38), channel_id=1, source_target_pairs={{0,4},{1,5},{2,6},{3,7},{4,0},{5,1},{6,2},{7,3},{8,12},{9,13},{10,... | collective-permute-start | bytes 24584 | tf_op jit(solution)/shard_map/ppermute | solution.py:17
  59.2 0.0 copy-done.1
  59.2 0.6 fusion.2
  59.9 1.9 %collective-permute-done.2 = f32[32,64]{1,0:T(8,128)S(1)} collective-permute-done((f32[32,64]{1,0:T(8,128)S(1)}, f32[32,64]{1,0:T(8,128)S(1)}, u32[]{:S(2)}, u32[]{:S(2)}) %collective-permute-start.2) | collective-permute-done | bytes 8224 | tf_op jit(solution)/shard_map/ppermute | solution.py:17
  61.8 0.0 copy-done.2
  61.8 0.1 fusion.19
  61.9 1.1 %fusion.15 = f32[8,32,625]{2,1,0:T(8,128)} fusion(bf16[32,64,1]{1,0,2:T(8,128)(2,1)S(1)} %fusion.19, bf16[8,625,64]{1,2,0:T(8,128)(2,1)S(1)} %copy-done, f32[4,32,625]{2,1,0:T(8,128)S(1)} %fusion.2, f32[4,32,625]{2,1,0:T(8,128)S(1)} %fusion.4), kind=kOutput, calls=%fused_computation.16 | convolution fusion | flops 20800000 | bytes 1924096 | tf_op jit(solution)/shard_map/km,ebm->ekb/dot_general | solution.py:120
  (9 shorter events, 0.0 us)
Async XLA Ops:
  0.0 33.3 %copy-start = (bf16[8,625,64]{1,2,0:T(8,128)(2,1)S(1)}, bf16[8,625,64]{1,2,0:T(8,128)(2,1)}, u32[]{:S(2)}) copy-start(bf16[8,625,64]{1,2,0:T(8,128)(2,1)} %param.14) | copy-start | bytes 1920004
  18.5 14.9 %slice-start = ((s8[6400000]{0:T(1024)(128)(4,1)}), s8[2205696]{0:T(1024)(128)(4,1)S(1)}, s32[]{:S(2)}) async-start(s8[6400000]{0:T(1024)(128)(4,1)} %bitcast.29), calls=%async_computation.1 | async-start | bytes 4411392
  18.5 29.3 %all-to-all-start = ((bf16[16,2,32,640]{3,2,1,0:T(8,128)(2,1)}), bf16[16,2,32,640]{3,2,1,0:T(8,128)(2,1)}, u32[]{:S(2)}, u32[]{:S(2)}) async-start(bf16[16,2,32,640]{3,2,1,0:T(8,128)(2,1)} %bitcast.31), calls=%async_computation | async-start | bytes 2621440 | tf_op jit(solution)/shard_map/all_to_all | solution.py:70
  26.8 6.5 %slice-start.1 = ((s8[6400000]{0:T(1024)(128)(4,1)}), s8[4194304]{0:T(1024)(128)(4,1)S(1)}, s32[]{:S(2)}) async-start(s8[6400000]{0:T(1024)(128)(4,1)} %bitcast.29), calls=%async_computation.2 | async-start | bytes 8388608
  48.9 10.4 %copy-start.1 = (bf16[8,625,625]{2,1,0:T(8,128)(2,1)S(1)}, bf16[8,625,625]{2,1,0:T(8,128)(2,1)}, u32[]{:S(2)}) copy-start(bf16[8,625,625]{2,1,0:T(8,128)(2,1)} %copy.26) | copy-start | bytes 18750004
  51.2 1.2 %collective-permute-start = (f32[32,64]{1,0:T(8,128)S(1)}, f32[32,64]{1,0:T(8,128)S(1)}, u32[]{:S(2)}, u32[]{:S(2)}) collective-permute-start(f32[32,64]{1,0:T(8,128)S(1)} %convolution_bitcast_fusion.1), channel_id=1, source_target_pairs={{0,1},{1,0},{2,3},{3,2},{4,5},{5,4},{6,7},{7,6},{8,9},{9,8},{10,11... | collective-permute-start | bytes 24584 | tf_op jit(solution)/shard_map/ppermute | solution.py:17
  52.4 4.0 %collective-permute-start.1 = (f32[32,64]{1,0:T(8,128)S(1)}, f32[32,64]{1,0:T(8,128)S(1)}, u32[]{:S(2)}, u32[]{:S(2)}) collective-permute-start(f32[32,64]{1,0:T(8,128)S(1)} %add.37), channel_id=1, source_target_pairs={{0,2},{1,3},{2,0},{3,1},{4,6},{5,7},{6,4},{7,5},{8,10},{9,11},{10,... | collective-permute-start | bytes 24584 | tf_op jit(solution)/shard_map/ppermute | solution.py:17
  53.9 7.9 %copy-start.2 = (f32[1,64,64]{2,1,0:T(8,128)S(1)}, f32[1,64,64]{2,1,0:T(8,128)}, u32[]{:S(2)}) copy-start(f32[1,64,64]{2,1,0:T(8,128)} %param.15) | copy-start | bytes 49156
  56.4 5.3 %collective-permute-start.2 = (f32[32,64]{1,0:T(8,128)S(1)}, f32[32,64]{1,0:T(8,128)S(1)}, u32[]{:S(2)}, u32[]{:S(2)}) collective-permute-start(f32[32,64]{1,0:T(8,128)S(1)} %add.38), channel_id=1, source_target_pairs={{0,4},{1,5},{2,6},{3,7},{4,0},{5,1},{6,2},{7,3},{8,12},{9,13},{10,... | collective-permute-start | bytes 24584 | tf_op jit(solution)/shard_map/ppermute | solution.py:17

commit v6 on v5

--- a/solution.py
+++ b/solution.py
@@ -11,6 +11,13 @@
     size = lax.axis_size(axis)
     if size & (size - 1):
         return lax.psum(value, axis)
+    if size == 8:
+        value = value + lax.ppermute(value, axis, [(i, i ^ 1) for i in range(size)])
+        parts = [value] + [
+            lax.ppermute(value, axis, [(i, (i + shift) % size) for i in range(size)])
+            for shift in (2, 4, 6)
+        ]
+        return (parts[0] + parts[2]) + (parts[1] + parts[3])
     bit = 1
     while bit < size:
         pairs = [(i, i ^ bit) for i in range(size)]

time: 63.3 us -> 63.9 us (level)
  starting transfers between devices: 12.6 us -> 13.5 us
    ppermute x3 -> x4, starting transfers between devices: 4.3 us -> 5.13 us  [the longest x3 5.12 us: group_sum(): lax.ppermute(value, axis, [(i, (i + shift) % size) for i in range(size)])]
    ppermute x3 -> x4, waiting for transfers between devices: 2.96 us -> 2.33 us  [the longest x3 2.33 us: group_sum(): lax.ppermute(value, axis, [(i, (i + shift) % size) for i in range(size)])]
  transfers between devices with their start and end apart: 4 -> 5, of which waited for: 3 -> 3; matrix products, arithmetic and copies ran while one was open for 19% -> 19% of each run, Pallas kernels for 0% -> 0%
where the time goes in v6:
time: 63.9 us; the launch traced here: 63.2 us
  matrix products  23.1 us (36%)
  waiting for transfers between devices  14.6 us (23%)
  starting transfers between devices  13.5 us (21%)
  local copies, waits for them, and re-layouts  10.1 us (16%)
  other arithmetic  1.7 us (3%)
    all_to_all x1, waiting for transfers between devices, shards(): lax.all_to_all(product_buffer.reshape(regions, CAP, vectors, padded), 'do...  12.2 us
    dot_general x1, matrix products, shards(): jnp.einsum('tkb,tbc->tkc', sources, coupling, preferred_element_type=jnp....  9.07 us
    all_to_all x1, starting transfers between devices, shards(): lax.all_to_all(product_buffer.reshape(regions, CAP, vectors, padded), 'do...  8.34 us
    unnamed x11, local copies, waits for them, and re-layouts  6.51 us
    dot_general x1, matrix products, shards(): jnp.einsum('ekb,ebc->ekc', residual_in, block_inverse, preferred_element_...  5.17 us
    ppermute x3, starting transfers between devices, group_sum(): lax.ppermute(value, axis, [(i, (i + shift) % size) for i in range(size)])  5.12 us
    dot_general x1, matrix products, shards(): jnp.einsum('ekb,ebc->ekc', corrected_in[:half], block_inverse[:half], pre...  2.54 us
    ppermute x3, waiting for transfers between devices, group_sum(): lax.ppermute(value, axis, [(i, (i + shift) % size) for i in range(size)])  2.33 us
  transfers between devices with their start and end apart: 5, of which 3 were waited for; matrix products, arithmetic and copies ran while one was open for 19% of the time, Pallas kernels for 0%

profile of v6, /device:TPU:0, one launch (start us, length us, event | category | flops | bytes accessed | tf_op | source)
XLA Modules:
  0.0 63.2 jit_solution(1519058496634818517)
XLA Ops:
  0.0 0.0 copy-start
  0.0 0.8 %pad_add_fusion = s32[48]{0:T(128)S(1)} fusion(s32[16]{0:T(128)} %param.13, s32[16]{0:T(128)} %param.12, s32[16]{0:T(128)} %bitcast.33), kind=kLoop, calls=%fused_computation.46 | loop fusion | flops 96 | bytes 384 | tf_op jit(solution)/shard_map/concatenate | solution.py:50
  0.8 0.2 convert_reduce_fusion.1
  1.0 0.1 multiply_add_fusion
  1.1 0.1 select_reduce_fusion
  1.2 0.1 fusion.28
  1.3 0.1 slice.29
  1.4 0.1 pad_maximum_fusion
  1.5 5.2 %convolution_convert_fusion.1 = bf16[8,32,625]{2,1,0:T(8,128)(2,1)S(1)} fusion(bf16[8,32,625]{2,1,0:T(8,128)(2,1)} %param.8, bf16[8,625,625]{2,0,1:T(8,128)(2,1)} %param.9), kind=kOutput, calls=%fused_computation.18 | convolution fusion | flops 200160000 | bytes 6890000 | tf_op jit(solution)/shard_map/ekb,ebc->ekc/dot_general | solution.py:46
  6.6 0.7 %gather_fusion = bf16[16,32,625]{2,1,0:T(8,128)(2,1)S(1)} fusion(bf16[8,32,625]{2,1,0:T(8,128)(2,1)S(1)} %convolution_convert_fusion.1, s32[1024]{0:T(1024)S(1)} %pad_clamp_fusion.1), kind=kCustom, calls=%fused_computation | custom fusion | bytes 1280064 | tf_op jit(solution)/shard_map/gather | solution.py:64
  7.3 9.1 %fusion.7 = bf16[16,32,625]{2,1,0:T(8,128)(2,1)S(1)} fusion(bf16[16,32,625]{2,1,0:T(8,128)(2,1)S(1)} %gather_fusion, bf16[16,625,625]{2,0,1:T(8,128)(2,1)} %param.10), kind=kOutput, calls=%fused_computation.10 | convolution fusion | flops 400320000 | bytes 13780000 | tf_op jit(solution)/shard_map/tkb,tbc->tkc/dot_general | solution.py:65
  16.4 0.1 and_select_fusion
  16.5 0.1 fusion.20
  16.6 1.8 %gather_fusion.1 = bf16[32,32,640]{2,1,0:T(8,128)(2,1)} fusion(bf16[17,32,640]{2,1,0:T(8,128)(2,1)S(1)} %fusion.20, s32[1024]{0:T(1024)S(1)} %pad_clamp_fusion), kind=kCustom, calls=%fused_computation.1 | custom fusion | bytes 2621568 | tf_op jit(solution)/shard_map/gather | solution.py:76
  18.5 0.0 slice-start
  18.5 8.3 %all-to-all-start = ((bf16[16,2,32,640]{3,2,1,0:T(8,128)(2,1)}), bf16[16,2,32,640]{3,2,1,0:T(8,128)(2,1)}, u32[]{:S(2)}, u32[]{:S(2)}) async-start(bf16[16,2,32,640]{3,2,1,0:T(8,128)(2,1)} %bitcast.31), calls=%async_computation | async-start | bytes 2621440 | tf_op jit(solution)/shard_map/all_to_all | solution.py:77
  26.8 0.0 slice-start.1
  26.8 6.5 %copy.26 = bf16[8,625,625]{2,1,0:T(8,128)(2,1)} copy(bf16[8,625,625]{2,0,1:T(8,128)(2,1)} %param.9) | data formatting | bytes 12500000 | tf_op args[1]
  33.3 0.0 copy-done
  33.3 0.0 slice-done
  33.3 0.0 slice-done.1
  33.3 2.2 %convolution_convert_fusion = bf16[8,625,64]{1,2,0:T(8,128)(2,1)S(1)} fusion(bf16[8,625,64]{1,2,0:T(8,128)(2,1)S(1)} %copy-done, bf16[8,625,625]{2,0,1:T(8,128)(2,1)S(1)} %bitcast.30), kind=kOutput, calls=%fused_computation.11 | convolution fusion | flops 400320000 | bytes 7530000 | tf_op jit(solution)/shard_map/ebc,ecm->ebm/dot_general | solution.py:93
  35.6 12.2 %all-to-all-done = bf16[16,2,32,640]{3,2,1,0:T(8,128)(2,1)} async-done(((bf16[16,2,32,640]{3,2,1,0:T(8,128)(2,1)}), bf16[16,2,32,640]{3,2,1,0:T(8,128)(2,1)}, u32[]{:S(2)}, u32[]{:S(2)}) %all-to-all-start) | async-done | bytes 1310752 | tf_op jit(solution)/shard_map/all_to_all | solution.py:77
  47.8 0.9 %slice.41 = bf16[32,1,1]{2,1,0:T(2,128)(2,1)S(1)} slice(bf16[32,32,640]{2,1,0:T(8,128)(2,1)} %bitcast.4), slice={[0:32], [0:1], [625:626]} | slice | bytes 128 | tf_op jit(solution)/shard_map/slice | solution.py:84
  48.7 0.1 convert_reduce_fusion
  48.8 0.0 copy-start.1
  48.9 2.0 %fusion.16 = bf16[8,32,625]{2,0,1:T(8,128)(2,1)S(1)} fusion(bf16[32,32,625]{2,1,0:T(8,128)(2,1)} %bitcast.28, bf16[8,32,625]{2,1,0:T(8,128)(2,1)} %param.8, s32[32]{0:T(128)S(1)} %convert_reduce_fusion), kind=kOutput, calls=%fused_computation.17 | convolution fusion | flops 10720256 | bytes 1920128 | tf_op jit(solution)/shard_map/es,skc->ekc/dot_general | solution.py:89
  50.9 0.1 fusion.36
  51.0 0.3 convolution_bitcast_fusion.1
  51.3 0.0 collective-permute-start
  51.3 0.0 copy-start.2
  51.3 2.5 %fusion.4 = f32[4,32,625]{2,1,0:T(8,128)S(1)} fusion(bf16[8,625,625]{2,1,0:T(8,128)(2,1)} %copy.26, bf16[4,32,625]{2,0,1:T(4,128)(2,1)S(1)} %get-tuple-element.5), kind=kOutput, calls=%fused_computation.6 | convolution fusion | flops 100000000 | bytes 3715840 | tf_op jit(solution)/shard_map/ekb,ebc->ekc/dot_general | solution.py:106
  53.9 0.0 collective-permute-done
  53.9 2.8 %collective-permute-start.3 = (f32[32,64]{1,0:T(8,128)S(1)}, f32[32,64]{1,0:T(8,128)S(1)}, u32[]{:S(2)}, u32[]{:S(2)}) collective-permute-start(f32[32,64]{1,0:T(8,128)S(1)} %add.40), channel_id=1, source_target_pairs={{0,6},{1,7},{2,0},{3,1},{4,2},{5,3},{6,4},{7,5},{8,14},{9,15},{10,... | collective-permute-start | bytes 24584 | tf_op jit(solution)/shard_map/ppermute | solution.py:17
  56.7 0.0 collective-permute-start.2
  56.7 2.3 %collective-permute-start.1 = (f32[32,64]{1,0:T(8,128)S(1)}, f32[32,64]{1,0:T(8,128)S(1)}, u32[]{:S(2)}, u32[]{:S(2)}) collective-permute-start(f32[32,64]{1,0:T(8,128)S(1)} %add.40), channel_id=1, source_target_pairs={{0,4},{1,5},{2,6},{3,7},{4,0},{5,1},{6,2},{7,3},{8,12},{9,13},{10,... | collective-permute-start | bytes 24584 | tf_op jit(solution)/shard_map/ppermute | solution.py:17
  59.0 0.0 copy-done.1
  59.0 0.6 fusion.2
  59.6 0.0 collective-permute-done.3
  59.6 2.0 %collective-permute-done.2 = f32[32,64]{1,0:T(8,128)S(1)} collective-permute-done((f32[32,64]{1,0:T(8,128)S(1)}, f32[32,64]{1,0:T(8,128)S(1)}, u32[]{:S(2)}, u32[]{:S(2)}) %collective-permute-start.2) | collective-permute-done | bytes 8224 | tf_op jit(solution)/shard_map/ppermute | solution.py:17
  61.7 0.3 collective-permute-done.1
  62.0 0.0 copy-done.2
  62.0 0.1 fusion.19
  62.1 1.1 %fusion.15 = f32[8,32,625]{2,1,0:T(8,128)} fusion(bf16[32,64,1]{1,0,2:T(8,128)(2,1)S(1)} %fusion.19, bf16[8,625,64]{1,2,0:T(8,128)(2,1)S(1)} %copy-done, f32[4,32,625]{2,1,0:T(8,128)S(1)} %fusion.2, f32[4,32,625]{2,1,0:T(8,128)S(1)} %fusion.4), kind=kOutput, calls=%fused_computation.16 | convolution fusion | flops 20800000 | bytes 1924096 | tf_op jit(solution)/shard_map/km,ebm->ekb/dot_general | solution.py:127
  (8 shorter events, 0.0 us)
Async XLA Ops:
  0.0 33.3 %copy-start = (bf16[8,625,64]{1,2,0:T(8,128)(2,1)S(1)}, bf16[8,625,64]{1,2,0:T(8,128)(2,1)}, u32[]{:S(2)}) copy-start(bf16[8,625,64]{1,2,0:T(8,128)(2,1)} %param.14) | copy-start | bytes 1920004
  18.5 14.8 %slice-start = ((s8[6400000]{0:T(1024)(128)(4,1)}), s8[2205696]{0:T(1024)(128)(4,1)S(1)}, s32[]{:S(2)}) async-start(s8[6400000]{0:T(1024)(128)(4,1)} %bitcast.29), calls=%async_computation.1 | async-start | bytes 4411392
  18.5 29.3 %all-to-all-start = ((bf16[16,2,32,640]{3,2,1,0:T(8,128)(2,1)}), bf16[16,2,32,640]{3,2,1,0:T(8,128)(2,1)}, u32[]{:S(2)}, u32[]{:S(2)}) async-start(bf16[16,2,32,640]{3,2,1,0:T(8,128)(2,1)} %bitcast.31), calls=%async_computation | async-start | bytes 2621440 | tf_op jit(solution)/shard_map/all_to_all | solution.py:77
  26.8 6.5 %slice-start.1 = ((s8[6400000]{0:T(1024)(128)(4,1)}), s8[4194304]{0:T(1024)(128)(4,1)S(1)}, s32[]{:S(2)}) async-start(s8[6400000]{0:T(1024)(128)(4,1)} %bitcast.29), calls=%async_computation.2 | async-start | bytes 8388608
  48.8 10.2 %copy-start.1 = (bf16[8,625,625]{2,1,0:T(8,128)(2,1)S(1)}, bf16[8,625,625]{2,1,0:T(8,128)(2,1)}, u32[]{:S(2)}) copy-start(bf16[8,625,625]{2,1,0:T(8,128)(2,1)} %copy.26) | copy-start | bytes 18750004
  51.3 2.6 %collective-permute-start = (f32[32,64]{1,0:T(8,128)S(1)}, f32[32,64]{1,0:T(8,128)S(1)}, u32[]{:S(2)}, u32[]{:S(2)}) collective-permute-start(f32[32,64]{1,0:T(8,128)S(1)} %convolution_bitcast_fusion.1), channel_id=1, source_target_pairs={{0,1},{1,0},{2,3},{3,2},{4,5},{5,4},{6,7},{7,6},{8,9},{9,8},{10,11... | collective-permute-start | bytes 24584 | tf_op jit(solution)/shard_map/ppermute | solution.py:15
  51.3 10.7 %copy-start.2 = (f32[1,64,64]{2,1,0:T(8,128)S(1)}, f32[1,64,64]{2,1,0:T(8,128)}, u32[]{:S(2)}) copy-start(f32[1,64,64]{2,1,0:T(8,128)} %param.15) | copy-start | bytes 49156
  53.9 5.7 %collective-permute-start.3 = (f32[32,64]{1,0:T(8,128)S(1)}, f32[32,64]{1,0:T(8,128)S(1)}, u32[]{:S(2)}, u32[]{:S(2)}) collective-permute-start(f32[32,64]{1,0:T(8,128)S(1)} %add.40), channel_id=1, source_target_pairs={{0,6},{1,7},{2,0},{3,1},{4,2},{5,3},{6,4},{7,5},{8,14},{9,15},{10,... | collective-permute-start | bytes 24584 | tf_op jit(solution)/shard_map/ppermute | solution.py:17
  56.7 4.9 %collective-permute-start.2 = (f32[32,64]{1,0:T(8,128)S(1)}, f32[32,64]{1,0:T(8,128)S(1)}, u32[]{:S(2)}, u32[]{:S(2)}) collective-permute-start(f32[32,64]{1,0:T(8,128)S(1)} %add.40), channel_id=1, source_target_pairs={{0,2},{1,3},{2,4},{3,5},{4,6},{5,7},{6,0},{7,1},{8,10},{9,11},{10,... | collective-permute-start | bytes 24584 | tf_op jit(solution)/shard_map/ppermute | solution.py:17
  56.7 5.2 %collective-permute-start.1 = (f32[32,64]{1,0:T(8,128)S(1)}, f32[32,64]{1,0:T(8,128)S(1)}, u32[]{:S(2)}, u32[]{:S(2)}) collective-permute-start(f32[32,64]{1,0:T(8,128)S(1)} %add.40), channel_id=1, source_target_pairs={{0,4},{1,5},{2,6},{3,7},{4,0},{5,1},{6,2},{7,3},{8,12},{9,13},{10,... | collective-permute-start | bytes 24584 | tf_op jit(solution)/shard_map/ppermute | solution.py:17

commit v7 on v5

--- a/solution.py
+++ b/solution.py
@@ -55,8 +55,23 @@
         jnp.any(hit, axis=1), jnp.sum(jnp.where(hit, order[None, :], 0), axis=1), tiles
     ).astype(jnp.int32)
     sources = initial[tile_source]
-    local_products = jnp.einsum(
-        "tkb,tbc->tkc", sources, coupling, preferred_element_type=jnp.float32
+    middle = tiles // 2
+    local_products = jnp.concatenate(
+        [
+            jnp.einsum(
+                "tkb,tbc->tkc",
+                sources[:middle],
+                coupling[:middle],
+                preferred_element_type=jnp.float32,
+            ),
+            jnp.einsum(
+                "tkb,tbc->tkc",
+                sources[middle:],
+                coupling[middle:],
+                preferred_element_type=jnp.float32,
+            ),
+        ],
+        axis=0,
     ).astype(jnp.bfloat16)
     marks = jnp.concatenate([tile_target, jnp.full((1,), -1, jnp.int32)]).astype(jnp.bfloat16)
     column = lax.broadcasted_iota(jnp.int32, (tiles + 1, vectors, padded - width), 2)

time: 63.3 us -> 69.3 us (1.095)
  local copies, waits for them, and re-layouts: 10.1 us -> 22.6 us
  matrix products: 23.1 us -> 16.7 us
    slice x0 -> x1, local copies, waits for them, and re-layouts: none -> 11.4 us  [shards(): coupling[:middle]]
    dot_general x1 -> x2, matrix products: 9.07 us -> 5.43 us  [the longest x1 4.25 us: shards(): jnp.einsum('tkb,tbc->tkc', sources[:middle], coupling[:middle], preferred...]
    dot_general x1, matrix products: 5.17 us -> 2.27 us  [shards(): jnp.einsum('ekb,ebc->ekc', residual_in, block_inverse, preferred_element_...]
    dot_general x1, matrix products: 2.54 us -> 0.62 us  [shards(): jnp.einsum('ekb,ebc->ekc', corrected_in[:half], block_inverse[:half], pre...]
    dot_general x1, matrix products: 0.61 us -> 2.53 us  [shards(): jnp.einsum('ekb,ebc->ekc', corrected_in[half:], block_inverse[half:], pre...]
    gather x1, local copies, waits for them, and re-layouts: 0.67 us -> 1.46 us  [shards(): sources = initial[tile_source]]
    unnamed x11 -> x21, local copies, waits for them, and re-layouts: 6.51 us -> 6.64 us
  transfers between devices with their start and end apart: 4 -> 4, of which waited for: 3 -> 3; matrix products, arithmetic and copies ran while one was open for 19% -> 17% of each run, Pallas kernels for 0% -> 0%
where the time goes in v7:
time: 69.3 us; the launch traced here: 69.1 us
  local copies, waits for them, and re-layouts  22.6 us (33%)
  matrix products  16.7 us (24%)
  waiting for transfers between devices  15.2 us (22%)
  starting transfers between devices  12.7 us (18%)
  other arithmetic  1.77 us (3%)
    all_to_all x1, waiting for transfers between devices, shards(): lax.all_to_all(product_buffer.reshape(regions, CAP, vectors, padded), 'do...  12.2 us
    slice x1, local copies, waits for them, and re-layouts, shards(): coupling[:middle]  11.4 us
    all_to_all x1, starting transfers between devices, shards(): lax.all_to_all(product_buffer.reshape(regions, CAP, vectors, padded), 'do...  8.34 us
    unnamed x21, local copies, waits for them, and re-layouts  6.64 us
    ppermute x3, starting transfers between devices, group_sum(): value = value + lax.ppermute(value, axis, pairs)  4.31 us
    dot_general x1, matrix products, shards(): jnp.einsum('tkb,tbc->tkc', sources[:middle], coupling[:middle], preferred...  4.25 us
    ppermute x3, waiting for transfers between devices, group_sum(): value = value + lax.ppermute(value, axis, pairs)  2.94 us
    dot_general x1, matrix products, shards(): jnp.einsum('ekb,ebc->ekc', corrected_in[half:], block_inverse[half:], pre...  2.53 us
  transfers between devices with their start and end apart: 4, of which 3 were waited for; matrix products, arithmetic and copies ran while one was open for 17% of the time, Pallas kernels for 0%

profile of v7, /device:TPU:0, one launch (start us, length us, event | category | flops | bytes accessed | tf_op | source)
XLA Modules:
  0.0 69.1 jit_solution(7914102216442023581)
XLA Ops:
  0.0 0.0 copy-start
  0.0 0.8 %pad_add_fusion = s32[48]{0:T(128)S(1)} fusion(s32[16]{0:T(128)} %param.13, s32[16]{0:T(128)} %param.12, s32[16]{0:T(128)} %bitcast.36), kind=kLoop, calls=%fused_computation.49 | loop fusion | flops 96 | bytes 384 | tf_op jit(solution)/shard_map/concatenate | solution.py:43
  0.8 0.2 convert_reduce_fusion.1
  1.0 0.1 multiply_add_fusion
  1.1 0.1 fusion.32
  1.2 0.1 select_reduce_fusion
  1.3 0.0 copy-start.2
  1.3 0.0 copy-start.4
  1.3 11.4 %fusion.40 = (bf16[8,625,625]{2,0,1:T(8,128)(2,1)}, bf16[8,625,625]{2,0,1:T(8,128)(2,1)}) fusion(bf16[16,625,625]{2,0,1:T(8,128)(2,1)} %param.10), kind=kLoop, calls=%fused_computation.56 | loop fusion | bytes 25000000 | tf_op jit(solution)/shard_map/slice | solution.py:64
  12.7 0.0 copy-done.2
  12.7 0.0 copy-done.4
  12.7 2.3 %convolution_convert_fusion.1 = bf16[8,32,625]{2,1,0:T(8,128)(2,1)S(1)} fusion(bf16[8,32,625]{2,1,0:T(8,128)(2,1)S(1)} %copy-done.4, bf16[8,625,625]{2,0,1:T(8,128)(2,1)S(1)} %copy-done.2), kind=kOutput, calls=%fused_computation.22 | convolution fusion | flops 200160000 | bytes 6890000 | tf_op jit(solution)/shard_map/ekb,ebc->ekc/dot_general | solution.py:39
  15.0 0.0 slice-start.2
  15.0 1.5 %gather_fusion = bf16[16,32,625]{2,1,0:T(8,128)(2,1)} fusion(bf16[8,32,625]{2,1,0:T(8,128)(2,1)S(1)} %convolution_convert_fusion.1, s32[1024]{0:T(1024)S(1)} %pad_clamp_fusion.1), kind=kCustom, calls=%fused_computation | custom fusion | bytes 1280064 | tf_op jit(solution)/shard_map/gather | solution.py:57
  16.4 0.0 slice-start.3
  16.4 0.0 copy-start.3
  16.4 4.3 %fusion.19 = bf16[8,32,625]{2,1,0:T(8,128)(2,1)S(1)} fusion(bf16[16,32,625]{2,1,0:T(8,128)(2,1)} %gather_fusion, bf16[8,625,625]{2,0,1:T(8,128)(2,1)} %get-tuple-element.5), kind=kOutput, calls=%fused_computation.20 | convolution fusion | flops 200160000 | bytes 7210000 | tf_op jit(solution)/shard_map/tkb,tbc->tkc/dot_general | solution.py:61
  20.7 0.0 slice-done.2
  20.7 0.1 slice-done.3
  20.8 0.0 copy-done.3
  20.8 1.2 %fusion.22 = bf16[8,32,625]{2,1,0:T(8,128)(2,1)S(1)} fusion(bf16[16,32,625]{2,1,0:T(8,128)(2,1)S(1)} %copy-done.3, bf16[8,625,625]{2,0,1:T(8,128)(2,1)S(1)} %bitcast.33), kind=kOutput, calls=%fused_computation.21 | convolution fusion | flops 200160000 | bytes 7210000 | tf_op jit(solution)/shard_map/tkb,tbc->tkc/dot_general | solution.py:67
  22.0 0.1 slice.45
  22.1 0.1 fusion.26
  22.1 0.1 pad_maximum_fusion.1
  22.2 0.1 and_select_fusion
  22.3 0.1 pad_maximum_fusion
  22.4 1.9 %gather_fusion.1 = bf16[32,32,640]{2,1,0:T(8,128)(2,1)} fusion(bf16[17,32,640]{2,1,0:T(8,128)(2,1)S(1)} %pad_maximum_fusion, s32[1024]{0:T(1024)S(1)} %pad_clamp_fusion), kind=kCustom, calls=%fused_computation.1 | custom fusion | bytes 2621568 | tf_op jit(solution)/shard_map/gather | solution.py:84
  24.3 0.0 slice-start
  24.3 8.3 %all-to-all-start = ((bf16[16,2,32,640]{3,2,1,0:T(8,128)(2,1)}), bf16[16,2,32,640]{3,2,1,0:T(8,128)(2,1)}, u32[]{:S(2)}, u32[]{:S(2)}) async-start(bf16[16,2,32,640]{3,2,1,0:T(8,128)(2,1)} %bitcast.34), calls=%async_computation | async-start | bytes 2621440 | tf_op jit(solution)/shard_map/all_to_all | solution.py:85
  32.6 0.0 slice-start.1
  32.7 6.5 %copy.30 = bf16[8,625,625]{2,1,0:T(8,128)(2,1)} copy(bf16[8,625,625]{2,0,1:T(8,128)(2,1)} %param.9) | data formatting | bytes 12500000 | tf_op args[1]
  39.2 0.0 copy-done
  39.2 0.0 slice-done
  39.2 0.0 slice-done.1
  39.2 2.2 %convolution_convert_fusion = bf16[8,625,64]{1,2,0:T(8,128)(2,1)S(1)} fusion(bf16[8,625,64]{1,2,0:T(8,128)(2,1)S(1)} %copy-done, bf16[8,625,625]{2,0,1:T(8,128)(2,1)S(1)} %bitcast.31), kind=kOutput, calls=%fused_computation.13 | convolution fusion | flops 400320000 | bytes 7530000 | tf_op jit(solution)/shard_map/ebc,ecm->ebm/dot_general | solution.py:101
  41.4 0.0 copy-start.5
  41.4 12.2 %all-to-all-done = bf16[16,2,32,640]{3,2,1,0:T(8,128)(2,1)} async-done(((bf16[16,2,32,640]{3,2,1,0:T(8,128)(2,1)}), bf16[16,2,32,640]{3,2,1,0:T(8,128)(2,1)}, u32[]{:S(2)}, u32[]{:S(2)}) %all-to-all-start) | async-done | bytes 1310752 | tf_op jit(solution)/shard_map/all_to_all | solution.py:85
  53.6 0.0 copy-start.1
  53.6 1.1 %slice.57 = bf16[32,1,1]{2,1,0:T(2,128)(2,1)S(1)} slice(bf16[32,32,640]{2,1,0:T(8,128)(2,1)} %bitcast.4), slice={[0:32], [0:1], [625:626]} | slice | bytes 128 | tf_op jit(solution)/shard_map/slice | solution.py:92
  54.7 0.1 convert_reduce_fusion
  54.8 2.2 %fusion.16 = bf16[8,32,625]{2,0,1:T(8,128)(2,1)S(1)} fusion(bf16[32,32,625]{2,1,0:T(8,128)(2,1)} %bitcast.29, bf16[8,32,625]{2,1,0:T(8,128)(2,1)} %param.8, s32[32]{0:T(128)S(1)} %convert_reduce_fusion), kind=kOutput, calls=%fused_computation.19 | convolution fusion | flops 10720256 | bytes 1920128 | tf_op jit(solution)/shard_map/es,skc->ekc/dot_general | solution.py:97
  57.0 0.3 convolution_bitcast_fusion.1
  57.3 0.0 collective-permute-start
  57.3 0.1 fusion.41
  57.4 1.1 %collective-permute-done = f32[32,64]{1,0:T(8,128)S(1)} collective-permute-done((f32[32,64]{1,0:T(8,128)S(1)}, f32[32,64]{1,0:T(8,128)S(1)}, u32[]{:S(2)}, u32[]{:S(2)}) %collective-permute-start) | collective-permute-done | bytes 8224 | tf_op jit(solution)/shard_map/ppermute | solution.py:17
  58.5 1.5 %collective-permute-start.1 = (f32[32,64]{1,0:T(8,128)S(1)}, f32[32,64]{1,0:T(8,128)S(1)}, u32[]{:S(2)}, u32[]{:S(2)}) collective-permute-start(f32[32,64]{1,0:T(8,128)S(1)} %add.37), channel_id=1, source_target_pairs={{0,2},{1,3},{2,0},{3,1},{4,6},{5,7},{6,4},{7,5},{8,10},{9,11},{10,... | collective-permute-start | bytes 24584 | tf_op jit(solution)/shard_map/ppermute | solution.py:17
  60.0 2.5 %fusion.4 = f32[4,32,625]{2,1,0:T(8,128)S(1)} fusion(bf16[8,625,625]{2,1,0:T(8,128)(2,1)} %copy.30, bf16[4,32,625]{2,0,1:T(4,128)(2,1)S(1)} %get-tuple-element.8), kind=kOutput, calls=%fused_computation.6 | convolution fusion | flops 100000000 | bytes 3715840 | tf_op jit(solution)/shard_map/ekb,ebc->ekc/dot_general | solution.py:120
  62.5 0.0 collective-permute-done.1
  62.5 2.8 %collective-permute-start.2 = (f32[32,64]{1,0:T(8,128)S(1)}, f32[32,64]{1,0:T(8,128)S(1)}, u32[]{:S(2)}, u32[]{:S(2)}) collective-permute-start(f32[32,64]{1,0:T(8,128)S(1)} %add.38), channel_id=1, source_target_pairs={{0,4},{1,5},{2,6},{3,7},{4,0},{5,1},{6,2},{7,3},{8,12},{9,13},{10,... | collective-permute-start | bytes 24584 | tf_op jit(solution)/shard_map/ppermute | solution.py:17
  65.3 0.0 copy-done.1
  65.3 0.6 fusion.6
  66.0 1.9 %collective-permute-done.2 = f32[32,64]{1,0:T(8,128)S(1)} collective-permute-done((f32[32,64]{1,0:T(8,128)S(1)}, f32[32,64]{1,0:T(8,128)S(1)}, u32[]{:S(2)}, u32[]{:S(2)}) %collective-permute-start.2) | collective-permute-done | bytes 8224 | tf_op jit(solution)/shard_map/ppermute | solution.py:17
  67.8 0.0 copy-done.5
  67.8 0.1 fusion.25
  68.0 1.1 %fusion.15 = f32[8,32,625]{2,1,0:T(8,128)} fusion(bf16[32,64,1]{1,0,2:T(8,128)(2,1)S(1)} %fusion.25, bf16[8,625,64]{1,2,0:T(8,128)(2,1)S(1)} %copy-done, f32[4,32,625]{2,1,0:T(8,128)S(1)} %fusion.4, f32[4,32,625]{2,1,0:T(8,128)S(1)} %fusion.6), kind=kOutput, calls=%fused_computation.18 | convolution fusion | flops 20800000 | bytes 1924096 | tf_op jit(solution)/shard_map/km,ebm->ekb/dot_general | solution.py:135
  (10 shorter events, 0.0 us)
Async XLA Ops:
  0.0 39.2 %copy-start = (bf16[8,625,64]{1,2,0:T(8,128)(2,1)S(1)}, bf16[8,625,64]{1,2,0:T(8,128)(2,1)}, u32[]{:S(2)}) copy-start(bf16[8,625,64]{1,2,0:T(8,128)(2,1)} %param.14) | copy-start | bytes 1920004
  1.3 11.4 %copy-start.2 = (bf16[8,625,625]{2,0,1:T(8,128)(2,1)S(1)}, bf16[8,625,625]{2,0,1:T(8,128)(2,1)}, u32[]{:S(2)}) copy-start(bf16[8,625,625]{2,0,1:T(8,128)(2,1)} %param.9) | copy-start | bytes 18750004
  1.3 11.4 %copy-start.4 = (bf16[8,32,625]{2,1,0:T(8,128)(2,1)S(1)}, bf16[8,32,625]{2,1,0:T(8,128)(2,1)}, u32[]{:S(2)}) copy-start(bf16[8,32,625]{2,1,0:T(8,128)(2,1)} %param.8) | copy-start | bytes 960004
  15.0 5.7 %slice-start.2 = ((s8[6400000]{0:T(1024)(128)(4,1)}), s8[2205696]{0:T(1024)(128)(4,1)S(1)}, s32[]{:S(2)}) async-start(s8[6400000]{0:T(1024)(128)(4,1)} %bitcast.32), calls=%async_computation.3 | async-start | bytes 4411392
  16.4 4.4 %slice-start.3 = ((s8[6400000]{0:T(1024)(128)(4,1)}), s8[4194304]{0:T(1024)(128)(4,1)S(1)}, s32[]{:S(2)}) async-start(s8[6400000]{0:T(1024)(128)(4,1)} %bitcast.32), calls=%async_computation.4 | async-start | bytes 8388608
  16.4 4.4 %copy-start.3 = (bf16[16,32,625]{2,1,0:T(8,128)(2,1)S(1)}, bf16[16,32,625]{2,1,0:T(8,128)(2,1)}, u32[]{:S(2)}) copy-start(bf16[16,32,625]{2,1,0:T(8,128)(2,1)} %gather_fusion) | copy-start | bytes 1920004
  24.3 14.9 %slice-start = ((s8[6400000]{0:T(1024)(128)(4,1)}), s8[2205696]{0:T(1024)(128)(4,1)S(1)}, s32[]{:S(2)}) async-start(s8[6400000]{0:T(1024)(128)(4,1)} %bitcast.30), calls=%async_computation.1 | async-start | bytes 4411392
  24.3 29.3 %all-to-all-start = ((bf16[16,2,32,640]{3,2,1,0:T(8,128)(2,1)}), bf16[16,2,32,640]{3,2,1,0:T(8,128)(2,1)}, u32[]{:S(2)}, u32[]{:S(2)}) async-start(bf16[16,2,32,640]{3,2,1,0:T(8,128)(2,1)} %bitcast.34), calls=%async_computation | async-start | bytes 2621440 | tf_op jit(solution)/shard_map/all_to_all | solution.py:85
  32.6 6.5 %slice-start.1 = ((s8[6400000]{0:T(1024)(128)(4,1)}), s8[4194304]{0:T(1024)(128)(4,1)S(1)}, s32[]{:S(2)}) async-start(s8[6400000]{0:T(1024)(128)(4,1)} %bitcast.30), calls=%async_computation.2 | async-start | bytes 8388608
  41.4 26.4 %copy-start.5 = (f32[1,64,64]{2,1,0:T(8,128)S(1)}, f32[1,64,64]{2,1,0:T(8,128)}, u32[]{:S(2)}) copy-start(f32[1,64,64]{2,1,0:T(8,128)} %param.15) | copy-start | bytes 49156
  53.6 11.7 %copy-start.1 = (bf16[8,625,625]{2,1,0:T(8,128)(2,1)S(1)}, bf16[8,625,625]{2,1,0:T(8,128)(2,1)}, u32[]{:S(2)}) copy-start(bf16[8,625,625]{2,1,0:T(8,128)(2,1)} %copy.30) | copy-start | bytes 18750004
  57.3 1.2 %collective-permute-start = (f32[32,64]{1,0:T(8,128)S(1)}, f32[32,64]{1,0:T(8,128)S(1)}, u32[]{:S(2)}, u32[]{:S(2)}) collective-permute-start(f32[32,64]{1,0:T(8,128)S(1)} %convolution_bitcast_fusion.1), channel_id=1, source_target_pairs={{0,1},{1,0},{2,3},{3,2},{4,5},{5,4},{6,7},{7,6},{8,9},{9,8},{10,11... | collective-permute-start | bytes 24584 | tf_op jit(solution)/shard_map/ppermute | solution.py:17
  58.5 4.0 %collective-permute-start.1 = (f32[32,64]{1,0:T(8,128)S(1)}, f32[32,64]{1,0:T(8,128)S(1)}, u32[]{:S(2)}, u32[]{:S(2)}) collective-permute-start(f32[32,64]{1,0:T(8,128)S(1)} %add.37), channel_id=1, source_target_pairs={{0,2},{1,3},{2,0},{3,1},{4,6},{5,7},{6,4},{7,5},{8,10},{9,11},{10,... | collective-permute-start | bytes 24584 | tf_op jit(solution)/shard_map/ppermute | solution.py:17
  62.5 5.3 %collective-permute-start.2 = (f32[32,64]{1,0:T(8,128)S(1)}, f32[32,64]{1,0:T(8,128)S(1)}, u32[]{:S(2)}, u32[]{:S(2)}) collective-permute-start(f32[32,64]{1,0:T(8,128)S(1)} %add.38), channel_id=1, source_target_pairs={{0,4},{1,5},{2,6},{3,7},{4,0},{5,1},{6,2},{7,3},{8,12},{9,13},{10,... | collective-permute-start | bytes 24584 | tf_op jit(solution)/shard_map/ppermute | solution.py:17

commit v8 on v5

--- a/solution.py
+++ b/solution.py
@@ -55,8 +55,20 @@
         jnp.any(hit, axis=1), jnp.sum(jnp.where(hit, order[None, :], 0), axis=1), tiles
     ).astype(jnp.int32)
     sources = initial[tile_source]
-    local_products = jnp.einsum(
-        "tkb,tbc->tkc", sources, coupling, preferred_element_type=jnp.float32
+    cut = min(width, 3 * LANE)
+    local_products = (
+        jnp.einsum(
+            "tkb,tbc->tkc",
+            sources[:, :, :cut],
+            coupling[:, :cut, :],
+            preferred_element_type=jnp.float32,
+        )
+        + jnp.einsum(
+            "tkb,tbc->tkc",
+            sources[:, :, cut:],
+            coupling[:, cut:, :],
+            preferred_element_type=jnp.float32,
+        )
     ).astype(jnp.bfloat16)
     marks = jnp.concatenate([tile_target, jnp.full((1,), -1, jnp.int32)]).astype(jnp.bfloat16)
     column = lax.broadcasted_iota(jnp.int32, (tiles + 1, vectors, padded - width), 2)

time: 63.3 us -> 67.9 us (1.073)
  local copies, waits for them, and re-layouts: 10.1 us -> 19.6 us
  matrix products: 23.1 us -> 19.2 us
  other arithmetic: 1.7 us -> 0.96 us
    slice x0 -> x3, local copies, waits for them, and re-layouts: none -> 7.03 us  [the longest x1 7.02 us: shards(): coupling[:, :cut, :]]
    dot_general x1, matrix products: 5.17 us -> 2.28 us  [shards(): jnp.einsum('ekb,ebc->ekc', residual_in, block_inverse, preferred_element_...]
    unnamed x11 -> x21, local copies, waits for them, and re-layouts: 6.51 us -> 8.74 us
    dot_general x1, matrix products: 2.54 us -> 0.62 us  [shards(): jnp.einsum('ekb,ebc->ekc', corrected_in[:half], block_inverse[:half], pre...]
    dot_general x1, matrix products: 0.61 us -> 2.54 us  [shards(): jnp.einsum('ekb,ebc->ekc', corrected_in[half:], block_inverse[half:], pre...]
    dot_general x1 -> x2, matrix products: 9.07 us -> 7.86 us  [the longest x1 6.03 us: shards(): jnp.einsum('tkb,tbc->tkc', sources[:, :, :cut], coupling[:, :cut, :], pre...]
    concatenate x1, other arithmetic: 0.83 us -> 0.08 us  [shards(): jnp.concatenate([tile_region[:, 0], tile_source, tile_target])]
  transfers between devices with their start and end apart: 4 -> 4, of which waited for: 3 -> 3; matrix products, arithmetic and copies ran while one was open for 19% -> 18% of each run, Pallas kernels for 0% -> 0%
where the time goes in v8:
time: 67.9 us; the launch traced here: 67.7 us
  local copies, waits for them, and re-layouts  19.6 us (29%)
  matrix products  19.2 us (28%)
  waiting for transfers between devices  15.2 us (22%)
  starting transfers between devices  12.6 us (19%)
  other arithmetic  0.96 us (1%)
    all_to_all x1, waiting for transfers between devices, shards(): lax.all_to_all(product_buffer.reshape(regions, CAP, vectors, padded), 'do...  12.2 us
    unnamed x21, local copies, waits for them, and re-layouts  8.74 us
    all_to_all x1, starting transfers between devices, shards(): lax.all_to_all(product_buffer.reshape(regions, CAP, vectors, padded), 'do...  8.34 us
    slice x1, local copies, waits for them, and re-layouts, shards(): coupling[:, :cut, :]  7.02 us
    dot_general x1, matrix products, shards(): jnp.einsum('tkb,tbc->tkc', sources[:, :, :cut], coupling[:, :cut, :], pre...  6.03 us
    ppermute x3, starting transfers between devices, group_sum(): value = value + lax.ppermute(value, axis, pairs)  4.31 us
    ppermute x3, waiting for transfers between devices, group_sum(): value = value + lax.ppermute(value, axis, pairs)  2.96 us
    dot_general x1, matrix products, shards(): jnp.einsum('ekb,ebc->ekc', corrected_in[half:], block_inverse[half:], pre...  2.54 us
  transfers between devices with their start and end apart: 4, of which 3 were waited for; matrix products, arithmetic and copies ran while one was open for 18% of the time, Pallas kernels for 0%

profile of v8, /device:TPU:0, one launch (start us, length us, event | category | flops | bytes accessed | tf_op | source)
XLA Modules:
  0.0 67.7 jit_solution(14709255172276975223)
XLA Ops:
  0.0 0.0 copy-start
  0.0 7.0 %slice.42 = bf16[16,384,625]{2,0,1:T(8,128)(2,1)} slice(bf16[16,625,625]{2,0,1:T(8,128)(2,1)} %param.10), slice={[0:16], [0:384], [0:625]} | slice | bytes 15360000 | tf_op jit(solution)/shard_map/slice | solution.py:63
  7.0 0.0 copy-start.5
  7.0 0.0 copy-start.6
  7.0 0.0 copy-start.7
  7.0 0.0 copy-start.2
  7.0 0.0 copy-start.3
  7.1 0.6 copy-done.5
  7.7 0.0 copy-done.6
  7.7 0.0 copy-done.7
  7.7 0.1 pad_add_fusion
  7.8 0.2 convert_reduce_fusion.1
  8.0 0.1 multiply_add_fusion
  8.1 0.1 fusion.33
  8.1 0.1 select_reduce_fusion
  8.2 0.1 slice.45
  8.3 1.6 %copy-done.2 = bf16[8,625,625]{2,0,1:T(8,128)(2,1)S(1)} copy-done((bf16[8,625,625]{2,0,1:T(8,128)(2,1)S(1)}, bf16[8,625,625]{2,0,1:T(8,128)(2,1)}, u32[]{:S(2)}) %copy-start.2) | copy-done | bytes 6250024
  9.9 0.0 copy-done.3
  9.9 2.3 %convolution_convert_fusion.1 = bf16[8,32,625]{2,1,0:T(8,128)(2,1)S(1)} fusion(bf16[8,32,625]{2,1,0:T(8,128)(2,1)S(1)} %copy-done.3, bf16[8,625,625]{2,0,1:T(8,128)(2,1)S(1)} %copy-done.2), kind=kOutput, calls=%fused_computation.21 | convolution fusion | flops 200160000 | bytes 6890000 | tf_op jit(solution)/shard_map/ekb,ebc->ekc/dot_general | solution.py:39
  12.2 0.7 gather_fusion
  12.8 0.0 slice-start
  12.9 6.0 %fusion = f32[16,32,625]{2,1,0:T(8,128)S(1)} fusion(bf16[16,384,625]{2,0,1:T(8,128)(2,1)} %slice.42, bf16[16,32,625]{2,1,0:T(8,128)(2,1)S(1)} %gather_fusion), kind=kOutput, calls=%fused_computation.2 | convolution fusion | flops 245760000 | bytes 9353216 | tf_op jit(solution)/shard_map/tkb,tbc->tkc/dot_general | solution.py:60
  18.9 0.0 slice-done
  18.9 1.8 %fusion.12 = bf16[16,32,625]{2,1,0:T(8,128)(2,1)S(1)} fusion(f32[16,32,625]{2,1,0:T(8,128)S(1)} %fusion, bf16[16,241,625]{2,0,1:T(8,128)(2,1)S(1)} %slice-done, bf16[16,32,625]{2,1,0:T(8,128)(2,1)S(1)} %gather_fusion), kind=kOutput, calls=%fused_computation.13 | convolution fusion | flops 154880000 | bytes 7148544 | tf_op jit(solution)/shard_map/tkb,tbc->tkc/dot_general | solution.py:66
  20.7 0.1 pad_maximum_fusion
  20.8 0.1 and_select_fusion
  20.9 0.1 fusion.25
  21.0 1.9 %gather_fusion.1 = bf16[32,32,640]{2,1,0:T(8,128)(2,1)} fusion(bf16[17,32,640]{2,1,0:T(8,128)(2,1)S(1)} %fusion.25, s32[1024]{0:T(1024)S(1)} %pad_clamp_fusion), kind=kCustom, calls=%fused_computation.1 | custom fusion | bytes 2621568 | tf_op jit(solution)/shard_map/gather | solution.py:81
  22.9 0.0 slice-start.1
  22.9 8.3 %all-to-all-start = ((bf16[16,2,32,640]{3,2,1,0:T(8,128)(2,1)}), bf16[16,2,32,640]{3,2,1,0:T(8,128)(2,1)}, u32[]{:S(2)}, u32[]{:S(2)}) async-start(bf16[16,2,32,640]{3,2,1,0:T(8,128)(2,1)} %bitcast.30), calls=%async_computation | async-start | bytes 2621440 | tf_op jit(solution)/shard_map/all_to_all | solution.py:82
  31.2 0.0 slice-start.2
  31.3 6.5 %copy.30 = bf16[8,625,625]{2,1,0:T(8,128)(2,1)} copy(bf16[8,625,625]{2,0,1:T(8,128)(2,1)} %param.9) | data formatting | bytes 12500000 | tf_op args[1]
  37.8 0.0 copy-done
  37.8 0.0 slice-done.1
  37.8 0.0 slice-done.2
  37.8 2.2 %convolution_convert_fusion = bf16[8,625,64]{1,2,0:T(8,128)(2,1)S(1)} fusion(bf16[8,625,64]{1,2,0:T(8,128)(2,1)S(1)} %copy-done, bf16[8,625,625]{2,0,1:T(8,128)(2,1)S(1)} %bitcast.29), kind=kOutput, calls=%fused_computation.14 | convolution fusion | flops 400320000 | bytes 7530000 | tf_op jit(solution)/shard_map/ebc,ecm->ebm/dot_general | solution.py:98
  40.0 12.2 %all-to-all-done = bf16[16,2,32,640]{3,2,1,0:T(8,128)(2,1)} async-done(((bf16[16,2,32,640]{3,2,1,0:T(8,128)(2,1)}), bf16[16,2,32,640]{3,2,1,0:T(8,128)(2,1)}, u32[]{:S(2)}, u32[]{:S(2)}) %all-to-all-start) | async-done | bytes 1310752 | tf_op jit(solution)/shard_map/all_to_all | solution.py:82
  52.2 0.0 copy-start.1
  52.2 1.1 %slice.59 = bf16[32,1,1]{2,1,0:T(2,128)(2,1)S(1)} slice(bf16[32,32,640]{2,1,0:T(8,128)(2,1)} %bitcast.4), slice={[0:32], [0:1], [625:626]} | slice | bytes 128 | tf_op jit(solution)/shard_map/slice | solution.py:89
  53.3 0.1 convert_reduce_fusion
  53.4 2.2 %fusion.21 = bf16[8,32,625]{2,0,1:T(8,128)(2,1)S(1)} fusion(bf16[32,32,625]{2,1,0:T(8,128)(2,1)} %bitcast.27, bf16[8,32,625]{2,1,0:T(8,128)(2,1)} %param.8, s32[32]{0:T(128)S(1)} %convert_reduce_fusion), kind=kOutput, calls=%fused_computation.20 | convolution fusion | flops 10720256 | bytes 1920128 | tf_op jit(solution)/shard_map/es,skc->ekc/dot_general | solution.py:94
  55.6 0.0 copy-start.4
  55.6 0.3 convolution_bitcast_fusion.1
  55.9 0.0 collective-permute-start
  55.9 0.1 fusion.41
  56.0 1.1 %collective-permute-done = f32[32,64]{1,0:T(8,128)S(1)} collective-permute-done((f32[32,64]{1,0:T(8,128)S(1)}, f32[32,64]{1,0:T(8,128)S(1)}, u32[]{:S(2)}, u32[]{:S(2)}) %collective-permute-start) | collective-permute-done | bytes 8224 | tf_op jit(solution)/shard_map/ppermute | solution.py:17
  57.1 1.5 %collective-permute-start.1 = (f32[32,64]{1,0:T(8,128)S(1)}, f32[32,64]{1,0:T(8,128)S(1)}, u32[]{:S(2)}, u32[]{:S(2)}) collective-permute-start(f32[32,64]{1,0:T(8,128)S(1)} %add.41), channel_id=1, source_target_pairs={{0,2},{1,3},{2,0},{3,1},{4,6},{5,7},{6,4},{7,5},{8,10},{9,11},{10,... | collective-permute-start | bytes 24584 | tf_op jit(solution)/shard_map/ppermute | solution.py:17
  58.6 2.5 %fusion.4 = f32[4,32,625]{2,1,0:T(8,128)S(1)} fusion(bf16[8,625,625]{2,1,0:T(8,128)(2,1)} %copy.30, bf16[4,32,625]{2,0,1:T(4,128)(2,1)S(1)} %get-tuple-element.6), kind=kOutput, calls=%fused_computation.6 | convolution fusion | flops 100000000 | bytes 3715840 | tf_op jit(solution)/shard_map/ekb,ebc->ekc/dot_general | solution.py:117
  61.1 0.0 collective-permute-done.1
  61.1 2.8 %collective-permute-start.2 = (f32[32,64]{1,0:T(8,128)S(1)}, f32[32,64]{1,0:T(8,128)S(1)}, u32[]{:S(2)}, u32[]{:S(2)}) collective-permute-start(f32[32,64]{1,0:T(8,128)S(1)} %add.42), channel_id=1, source_target_pairs={{0,4},{1,5},{2,6},{3,7},{4,0},{5,1},{6,2},{7,3},{8,12},{9,13},{10,... | collective-permute-start | bytes 24584 | tf_op jit(solution)/shard_map/ppermute | solution.py:17
  63.9 0.0 copy-done.1
  63.9 0.6 fusion.6
  64.6 1.9 %collective-permute-done.2 = f32[32,64]{1,0:T(8,128)S(1)} collective-permute-done((f32[32,64]{1,0:T(8,128)S(1)}, f32[32,64]{1,0:T(8,128)S(1)}, u32[]{:S(2)}, u32[]{:S(2)}) %collective-permute-start.2) | collective-permute-done | bytes 8224 | tf_op jit(solution)/shard_map/ppermute | solution.py:17
  66.5 0.0 copy-done.4
  66.5 0.1 fusion.24
  66.6 1.1 %fusion.20 = f32[8,32,625]{2,1,0:T(8,128)} fusion(bf16[32,64,1]{1,0,2:T(8,128)(2,1)S(1)} %fusion.24, bf16[8,625,64]{1,2,0:T(8,128)(2,1)S(1)} %copy-done, f32[4,32,625]{2,1,0:T(8,128)S(1)} %fusion.4, f32[4,32,625]{2,1,0:T(8,128)S(1)} %fusion.6), kind=kOutput, calls=%fused_computation.19 | convolution fusion | flops 20800000 | bytes 1924096 | tf_op jit(solution)/shard_map/km,ebm->ekb/dot_general | solution.py:132
  (9 shorter events, 0.0 us)
Async XLA Ops:
  0.0 37.8 %copy-start = (bf16[8,625,64]{1,2,0:T(8,128)(2,1)S(1)}, bf16[8,625,64]{1,2,0:T(8,128)(2,1)}, u32[]{:S(2)}) copy-start(bf16[8,625,64]{1,2,0:T(8,128)(2,1)} %param.14) | copy-start | bytes 1920004
  7.0 0.7 copy-start.5
  7.0 0.7 copy-start.6
  7.0 0.7 %copy-start.7 = (s32[16,1]{0,1:T(1,128)S(1)}, s32[16,1]{0,1:T(1,128)}, u32[]{:S(2)}) copy-start(s32[16,1]{0,1:T(1,128)} %param.11) | copy-start | bytes 196
  7.0 2.9 %copy-start.2 = (bf16[8,625,625]{2,0,1:T(8,128)(2,1)S(1)}, bf16[8,625,625]{2,0,1:T(8,128)(2,1)}, u32[]{:S(2)}) copy-start(bf16[8,625,625]{2,0,1:T(8,128)(2,1)} %param.9) | copy-start | bytes 18750004
  7.0 2.9 %copy-start.3 = (bf16[8,32,625]{2,1,0:T(8,128)(2,1)S(1)}, bf16[8,32,625]{2,1,0:T(8,128)(2,1)}, u32[]{:S(2)}) copy-start(bf16[8,32,625]{2,1,0:T(8,128)(2,1)} %param.8) | copy-start | bytes 960004
  12.8 6.0 %slice-start = ((bf16[16,625,625]{2,0,1:T(8,128)(2,1)}), bf16[16,241,625]{2,0,1:T(8,128)(2,1)S(1)}, s32[]{:S(2)}) async-start(bf16[16,625,625]{2,0,1:T(8,128)(2,1)} %param.10), calls=%async_computation.1 | async-start | bytes 9871360 | tf_op jit(solution)/shard_map/slice | solution.py:69
  22.9 14.9 %slice-start.1 = ((s8[6400000]{0:T(1024)(128)(4,1)}), s8[2205696]{0:T(1024)(128)(4,1)S(1)}, s32[]{:S(2)}) async-start(s8[6400000]{0:T(1024)(128)(4,1)} %bitcast.28), calls=%async_computation.2 | async-start | bytes 4411392
  22.9 29.3 %all-to-all-start = ((bf16[16,2,32,640]{3,2,1,0:T(8,128)(2,1)}), bf16[16,2,32,640]{3,2,1,0:T(8,128)(2,1)}, u32[]{:S(2)}, u32[]{:S(2)}) async-start(bf16[16,2,32,640]{3,2,1,0:T(8,128)(2,1)} %bitcast.30), calls=%async_computation | async-start | bytes 2621440 | tf_op jit(solution)/shard_map/all_to_all | solution.py:82
  31.2 6.5 %slice-start.2 = ((s8[6400000]{0:T(1024)(128)(4,1)}), s8[4194304]{0:T(1024)(128)(4,1)S(1)}, s32[]{:S(2)}) async-start(s8[6400000]{0:T(1024)(128)(4,1)} %bitcast.28), calls=%async_computation.3 | async-start | bytes 8388608
  52.2 11.7 %copy-start.1 = (bf16[8,625,625]{2,1,0:T(8,128)(2,1)S(1)}, bf16[8,625,625]{2,1,0:T(8,128)(2,1)}, u32[]{:S(2)}) copy-start(bf16[8,625,625]{2,1,0:T(8,128)(2,1)} %copy.30) | copy-start | bytes 18750004
  55.6 10.9 %copy-start.4 = (f32[1,64,64]{2,1,0:T(8,128)S(1)}, f32[1,64,64]{2,1,0:T(8,128)}, u32[]{:S(2)}) copy-start(f32[1,64,64]{2,1,0:T(8,128)} %param.15) | copy-start | bytes 49156
  55.9 1.2 %collective-permute-start = (f32[32,64]{1,0:T(8,128)S(1)}, f32[32,64]{1,0:T(8,128)S(1)}, u32[]{:S(2)}, u32[]{:S(2)}) collective-permute-start(f32[32,64]{1,0:T(8,128)S(1)} %convolution_bitcast_fusion.1), channel_id=1, source_target_pairs={{0,1},{1,0},{2,3},{3,2},{4,5},{5,4},{6,7},{7,6},{8,9},{9,8},{10,11... | collective-permute-start | bytes 24584 | tf_op jit(solution)/shard_map/ppermute | solution.py:17
  57.1 4.0 %collective-permute-start.1 = (f32[32,64]{1,0:T(8,128)S(1)}, f32[32,64]{1,0:T(8,128)S(1)}, u32[]{:S(2)}, u32[]{:S(2)}) collective-permute-start(f32[32,64]{1,0:T(8,128)S(1)} %add.41), channel_id=1, source_target_pairs={{0,2},{1,3},{2,0},{3,1},{4,6},{5,7},{6,4},{7,5},{8,10},{9,11},{10,... | collective-permute-start | bytes 24584 | tf_op jit(solution)/shard_map/ppermute | solution.py:17
  61.1 5.3 %collective-permute-start.2 = (f32[32,64]{1,0:T(8,128)S(1)}, f32[32,64]{1,0:T(8,128)S(1)}, u32[]{:S(2)}, u32[]{:S(2)}) collective-permute-start(f32[32,64]{1,0:T(8,128)S(1)} %add.42), channel_id=1, source_target_pairs={{0,4},{1,5},{2,6},{3,7},{4,0},{5,1},{6,2},{7,3},{8,12},{9,13},{10,... | collective-permute-start | bytes 24584 | tf_op jit(solution)/shard_map/ppermute | solution.py:17

commit v9 on v5

--- a/solution.py
+++ b/solution.py
@@ -1,6 +1,7 @@
 import jax
 import jax.numpy as jnp
 from jax import lax
+from jax.experimental.layout import Layout, with_layout_constraint
 from jax.sharding import PartitionSpec as P
 
 CAP = 2
@@ -83,8 +84,9 @@
         "es,skc->ekc", selector, products, preferred_element_type=jnp.float32
     )
     corrected_in = (residual_in.astype(jnp.float32) - coupled).astype(jnp.bfloat16)
+    late_inverse = with_layout_constraint(block_inverse, Layout((0, 1, 2)))
     projected = jnp.einsum(
-        "ebc,ecm->ebm", block_inverse, interface_basis, preferred_element_type=jnp.float32
+        "ebc,ecm->ebm", late_inverse, interface_basis, preferred_element_type=jnp.float32
     )
     partial_reduced = jnp.einsum(
         "ekb,ebm->km",
@@ -99,13 +101,13 @@
             jnp.einsum(
                 "ekb,ebc->ekc",
                 corrected_in[:half],
-                block_inverse[:half],
+                late_inverse[:half],
                 preferred_element_type=jnp.float32,
             ),
             jnp.einsum(
                 "ekb,ebc->ekc",
                 corrected_in[half:],
-                block_inverse[half:],
+                late_inverse[half:],
                 preferred_element_type=jnp.float32,
             ),
         ],

time: 63.3 us -> 63.3 us (level)
  no operation moved by 1% of the time
where the time goes in v9:
time: 63.3 us; the launch traced here: 63 us
  matrix products  23.1 us (36%)
  waiting for transfers between devices  15.2 us (24%)
  starting transfers between devices  12.6 us (20%)
  local copies, waits for them, and re-layouts  10.1 us (16%)
  other arithmetic  1.7 us (3%)
    all_to_all x1, waiting for transfers between devices, shards(): lax.all_to_all(product_buffer.reshape(regions, CAP, vectors, padded), 'do...  12.2 us
    dot_general x1, matrix products, shards(): jnp.einsum('tkb,tbc->tkc', sources, coupling, preferred_element_type=jnp....  9.07 us
    all_to_all x1, starting transfers between devices, shards(): lax.all_to_all(product_buffer.reshape(regions, CAP, vectors, padded), 'do...  8.34 us
    unnamed x11, local copies, waits for them, and re-layouts  6.51 us
    dot_general x1, matrix products, shards(): jnp.einsum('ekb,ebc->ekc', residual_in, block_inverse, preferred_element_...  5.17 us
    ppermute x3, starting transfers between devices, group_sum(): value = value + lax.ppermute(value, axis, pairs)  4.3 us
    ppermute x3, waiting for transfers between devices, group_sum(): value = value + lax.ppermute(value, axis, pairs)  2.96 us
    dot_general x1, matrix products, shards(): jnp.einsum('ekb,ebc->ekc', corrected_in[half:], late_inverse[half:], pref...  2.54 us
  transfers between devices with their start and end apart: 4, of which 3 were waited for; matrix products, arithmetic and copies ran while one was open for 19% of the time, Pallas kernels for 0%

profile of v9, /device:TPU:0, one launch (start us, length us, event | category | flops | bytes accessed | tf_op | source)
XLA Modules:
  0.0 63.0 jit_solution(602011915088295791)
XLA Ops:
  0.0 0.0 copy-start
  0.0 0.8 %pad_add_fusion = s32[48]{0:T(128)S(1)} fusion(s32[16]{0:T(128)} %param.13, s32[16]{0:T(128)} %param.12, s32[16]{0:T(128)} %bitcast.33), kind=kLoop, calls=%fused_computation.44 | loop fusion | flops 96 | bytes 384 | tf_op jit(solution)/shard_map/concatenate | solution.py:44
  0.8 0.2 convert_reduce_fusion.1
  1.0 0.1 multiply_add_fusion
  1.1 0.1 select_reduce_fusion
  1.2 0.1 fusion.26
  1.3 0.1 slice.29
  1.4 0.1 pad_maximum_fusion
  1.5 5.2 %convolution_convert_fusion.1 = bf16[8,32,625]{2,1,0:T(8,128)(2,1)S(1)} fusion(bf16[8,32,625]{2,1,0:T(8,128)(2,1)} %param.8, bf16[8,625,625]{2,0,1:T(8,128)(2,1)} %param.9), kind=kOutput, calls=%fused_computation.18 | convolution fusion | flops 200160000 | bytes 6890000 | tf_op jit(solution)/shard_map/ekb,ebc->ekc/dot_general | solution.py:40
  6.6 0.7 %gather_fusion = bf16[16,32,625]{2,1,0:T(8,128)(2,1)S(1)} fusion(bf16[8,32,625]{2,1,0:T(8,128)(2,1)S(1)} %convolution_convert_fusion.1, s32[1024]{0:T(1024)S(1)} %pad_clamp_fusion.1), kind=kCustom, calls=%fused_computation | custom fusion | bytes 1280064 | tf_op jit(solution)/shard_map/gather | solution.py:58
  7.3 9.1 %fusion.7 = bf16[16,32,625]{2,1,0:T(8,128)(2,1)S(1)} fusion(bf16[16,32,625]{2,1,0:T(8,128)(2,1)S(1)} %gather_fusion, bf16[16,625,625]{2,0,1:T(8,128)(2,1)} %param.10), kind=kOutput, calls=%fused_computation.10 | convolution fusion | flops 400320000 | bytes 13780000 | tf_op jit(solution)/shard_map/tkb,tbc->tkc/dot_general | solution.py:59
  16.4 0.1 and_select_fusion
  16.5 0.1 fusion.20
  16.6 1.9 %gather_fusion.1 = bf16[32,32,640]{2,1,0:T(8,128)(2,1)} fusion(bf16[17,32,640]{2,1,0:T(8,128)(2,1)S(1)} %fusion.20, s32[1024]{0:T(1024)S(1)} %pad_clamp_fusion), kind=kCustom, calls=%fused_computation.1 | custom fusion | bytes 2621568 | tf_op jit(solution)/shard_map/gather | solution.py:70
  18.5 0.0 slice-start
  18.5 8.3 %all-to-all-start = ((bf16[16,2,32,640]{3,2,1,0:T(8,128)(2,1)}), bf16[16,2,32,640]{3,2,1,0:T(8,128)(2,1)}, u32[]{:S(2)}, u32[]{:S(2)}) async-start(bf16[16,2,32,640]{3,2,1,0:T(8,128)(2,1)} %bitcast.31), calls=%async_computation | async-start | bytes 2621440 | tf_op jit(solution)/shard_map/all_to_all | solution.py:71
  26.8 0.0 slice-start.1
  26.8 6.5 %copy.24 = bf16[8,625,625]{2,1,0:T(8,128)(2,1)} copy(bf16[8,625,625]{2,0,1:T(8,128)(2,1)} %param.9) | data formatting | bytes 12500000 | tf_op args[1]
  33.3 0.0 copy-done
  33.3 0.0 slice-done
  33.3 0.0 slice-done.1
  33.3 2.2 %convolution_convert_fusion = bf16[8,625,64]{1,2,0:T(8,128)(2,1)S(1)} fusion(bf16[8,625,64]{1,2,0:T(8,128)(2,1)S(1)} %copy-done, bf16[8,625,625]{2,0,1:T(8,128)(2,1)S(1)} %bitcast.30), kind=kOutput, calls=%fused_computation.11 | convolution fusion | flops 400320000 | bytes 7530000 | tf_op jit(solution)/shard_map/ebc,ecm->ebm/dot_general | solution.py:88
  35.6 12.2 %all-to-all-done = bf16[16,2,32,640]{3,2,1,0:T(8,128)(2,1)} async-done(((bf16[16,2,32,640]{3,2,1,0:T(8,128)(2,1)}), bf16[16,2,32,640]{3,2,1,0:T(8,128)(2,1)}, u32[]{:S(2)}, u32[]{:S(2)}) %all-to-all-start) | async-done | bytes 1310752 | tf_op jit(solution)/shard_map/all_to_all | solution.py:71
  47.8 0.9 %slice.41 = bf16[32,1,1]{2,1,0:T(2,128)(2,1)S(1)} slice(bf16[32,32,640]{2,1,0:T(8,128)(2,1)} %bitcast.4), slice={[0:32], [0:1], [625:626]} | slice | bytes 128 | tf_op jit(solution)/shard_map/slice | solution.py:78
  48.7 0.1 convert_reduce_fusion
  48.9 0.0 copy-start.1
  48.9 2.0 %fusion.16 = bf16[8,32,625]{2,0,1:T(8,128)(2,1)S(1)} fusion(bf16[32,32,625]{2,1,0:T(8,128)(2,1)} %bitcast.28, bf16[8,32,625]{2,1,0:T(8,128)(2,1)} %param.8, s32[32]{0:T(128)S(1)} %convert_reduce_fusion), kind=kOutput, calls=%fused_computation.17 | convolution fusion | flops 10720256 | bytes 1920128 | tf_op jit(solution)/shard_map/es,skc->ekc/dot_general | solution.py:83
  50.9 0.3 convolution_bitcast_fusion.1
  51.2 0.0 collective-permute-start
  51.2 0.1 fusion.34
  51.3 1.1 %collective-permute-done = f32[32,64]{1,0:T(8,128)S(1)} collective-permute-done((f32[32,64]{1,0:T(8,128)S(1)}, f32[32,64]{1,0:T(8,128)S(1)}, u32[]{:S(2)}, u32[]{:S(2)}) %collective-permute-start) | collective-permute-done | bytes 8224 | tf_op jit(solution)/shard_map/ppermute | solution.py:18
  52.4 1.5 %collective-permute-start.1 = (f32[32,64]{1,0:T(8,128)S(1)}, f32[32,64]{1,0:T(8,128)S(1)}, u32[]{:S(2)}, u32[]{:S(2)}) collective-permute-start(f32[32,64]{1,0:T(8,128)S(1)} %add.37), channel_id=1, source_target_pairs={{0,2},{1,3},{2,0},{3,1},{4,6},{5,7},{6,4},{7,5},{8,10},{9,11},{10,... | collective-permute-start | bytes 24584 | tf_op jit(solution)/shard_map/ppermute | solution.py:18
  53.9 0.0 copy-start.2
  53.9 2.5 %fusion.2 = f32[4,32,625]{2,1,0:T(8,128)S(1)} fusion(bf16[8,625,625]{2,1,0:T(8,128)(2,1)} %copy.24, bf16[4,32,625]{2,0,1:T(4,128)(2,1)S(1)} %get-tuple-element.6), kind=kOutput, calls=%fused_computation.4 | convolution fusion | flops 100000000 | bytes 3715840 | tf_op jit(solution)/shard_map/ekb,ebc->ekc/dot_general | solution.py:107
  56.4 0.0 collective-permute-done.1
  56.4 2.8 %collective-permute-start.2 = (f32[32,64]{1,0:T(8,128)S(1)}, f32[32,64]{1,0:T(8,128)S(1)}, u32[]{:S(2)}, u32[]{:S(2)}) collective-permute-start(f32[32,64]{1,0:T(8,128)S(1)} %add.38), channel_id=1, source_target_pairs={{0,4},{1,5},{2,6},{3,7},{4,0},{5,1},{6,2},{7,3},{8,12},{9,13},{10,... | collective-permute-start | bytes 24584 | tf_op jit(solution)/shard_map/ppermute | solution.py:18
  59.2 0.0 copy-done.1
  59.2 0.6 fusion.4
  59.9 1.9 %collective-permute-done.2 = f32[32,64]{1,0:T(8,128)S(1)} collective-permute-done((f32[32,64]{1,0:T(8,128)S(1)}, f32[32,64]{1,0:T(8,128)S(1)}, u32[]{:S(2)}, u32[]{:S(2)}) %collective-permute-start.2) | collective-permute-done | bytes 8224 | tf_op jit(solution)/shard_map/ppermute | solution.py:18
  61.8 0.0 copy-done.2
  61.8 0.1 fusion.19
  61.9 1.1 %fusion.15 = f32[8,32,625]{2,1,0:T(8,128)} fusion(bf16[32,64,1]{1,0,2:T(8,128)(2,1)S(1)} %fusion.19, bf16[8,625,64]{1,2,0:T(8,128)(2,1)S(1)} %copy-done, f32[4,32,625]{2,1,0:T(8,128)S(1)} %fusion.2, f32[4,32,625]{2,1,0:T(8,128)S(1)} %fusion.4), kind=kOutput, calls=%fused_computation.16 | convolution fusion | flops 20800000 | bytes 1924096 | tf_op jit(solution)/shard_map/km,ebm->ekb/dot_general | solution.py:122
  (9 shorter events, 0.0 us)
Async XLA Ops:
  0.0 33.3 %copy-start = (bf16[8,625,64]{1,2,0:T(8,128)(2,1)S(1)}, bf16[8,625,64]{1,2,0:T(8,128)(2,1)}, u32[]{:S(2)}) copy-start(bf16[8,625,64]{1,2,0:T(8,128)(2,1)} %param.14) | copy-start | bytes 1920004
  18.5 14.9 %slice-start = ((s8[6400000]{0:T(1024)(128)(4,1)}), s8[2205696]{0:T(1024)(128)(4,1)S(1)}, s32[]{:S(2)}) async-start(s8[6400000]{0:T(1024)(128)(4,1)} %bitcast.29), calls=%async_computation.1 | async-start | bytes 4411392
  18.5 29.3 %all-to-all-start = ((bf16[16,2,32,640]{3,2,1,0:T(8,128)(2,1)}), bf16[16,2,32,640]{3,2,1,0:T(8,128)(2,1)}, u32[]{:S(2)}, u32[]{:S(2)}) async-start(bf16[16,2,32,640]{3,2,1,0:T(8,128)(2,1)} %bitcast.31), calls=%async_computation | async-start | bytes 2621440 | tf_op jit(solution)/shard_map/all_to_all | solution.py:71
  26.8 6.5 %slice-start.1 = ((s8[6400000]{0:T(1024)(128)(4,1)}), s8[4194304]{0:T(1024)(128)(4,1)S(1)}, s32[]{:S(2)}) async-start(s8[6400000]{0:T(1024)(128)(4,1)} %bitcast.29), calls=%async_computation.2 | async-start | bytes 8388608
  48.9 10.4 %copy-start.1 = (bf16[8,625,625]{2,1,0:T(8,128)(2,1)S(1)}, bf16[8,625,625]{2,1,0:T(8,128)(2,1)}, u32[]{:S(2)}) copy-start(bf16[8,625,625]{2,1,0:T(8,128)(2,1)} %copy.24) | copy-start | bytes 18750004
  51.2 1.2 %collective-permute-start = (f32[32,64]{1,0:T(8,128)S(1)}, f32[32,64]{1,0:T(8,128)S(1)}, u32[]{:S(2)}, u32[]{:S(2)}) collective-permute-start(f32[32,64]{1,0:T(8,128)S(1)} %convolution_bitcast_fusion.1), channel_id=1, source_target_pairs={{0,1},{1,0},{2,3},{3,2},{4,5},{5,4},{6,7},{7,6},{8,9},{9,8},{10,11... | collective-permute-start | bytes 24584 | tf_op jit(solution)/shard_map/ppermute | solution.py:18
  52.4 4.0 %collective-permute-start.1 = (f32[32,64]{1,0:T(8,128)S(1)}, f32[32,64]{1,0:T(8,128)S(1)}, u32[]{:S(2)}, u32[]{:S(2)}) collective-permute-start(f32[32,64]{1,0:T(8,128)S(1)} %add.37), channel_id=1, source_target_pairs={{0,2},{1,3},{2,0},{3,1},{4,6},{5,7},{6,4},{7,5},{8,10},{9,11},{10,... | collective-permute-start | bytes 24584 | tf_op jit(solution)/shard_map/ppermute | solution.py:18
  53.9 7.9 %copy-start.2 = (f32[1,64,64]{2,1,0:T(8,128)S(1)}, f32[1,64,64]{2,1,0:T(8,128)}, u32[]{:S(2)}) copy-start(f32[1,64,64]{2,1,0:T(8,128)} %param.15) | copy-start | bytes 49156
  56.4 5.3 %collective-permute-start.2 = (f32[32,64]{1,0:T(8,128)S(1)}, f32[32,64]{1,0:T(8,128)S(1)}, u32[]{:S(2)}, u32[]{:S(2)}) collective-permute-start(f32[32,64]{1,0:T(8,128)S(1)} %add.38), channel_id=1, source_target_pairs={{0,4},{1,5},{2,6},{3,7},{4,0},{5,1},{6,2},{7,3},{8,12},{9,13},{10,... | collective-permute-start | bytes 24584 | tf_op jit(solution)/shard_map/ppermute | solution.py:18

commit v10 on v9

--- a/solution.py
+++ b/solution.py
@@ -1,11 +1,28 @@
 import jax
 import jax.numpy as jnp
 from jax import lax
-from jax.experimental.layout import Layout, with_layout_constraint
+from jax.experimental import pallas as pl
+from jax.experimental.pallas import tpu as pltpu
 from jax.sharding import PartitionSpec as P
 
 CAP = 2
 LANE = 128
+
+
+def resident(value):
+    def kernel(source, target, flag):
+        copy = pltpu.make_async_copy(source, target, flag.at[0])
+        copy.start()
+        copy.wait()
+
+    return pl.pallas_call(
+        kernel,
+        in_specs=[pl.BlockSpec(memory_space=pl.ANY)],
+        out_specs=pl.BlockSpec(memory_space=pltpu.VMEM),
+        out_shape=jax.ShapeDtypeStruct(value.shape, value.dtype),
+        scratch_shapes=[pltpu.SemaphoreType.DMA((1,))],
+        compiler_params=pltpu.CompilerParams(vmem_limit_bytes=48 * 1024 * 1024),
+    )(value)
 
 
 def group_sum(value, axis):
@@ -84,7 +101,7 @@
         "es,skc->ekc", selector, products, preferred_element_type=jnp.float32
     )
     corrected_in = (residual_in.astype(jnp.float32) - coupled).astype(jnp.bfloat16)
-    late_inverse = with_layout_constraint(block_inverse, Layout((0, 1, 2)))
+    late_inverse = jnp.transpose(resident(jnp.transpose(block_inverse, (1, 0, 2))), (1, 0, 2))
     projected = jnp.einsum(
         "ebc,ecm->ebm", late_inverse, interface_basis, preferred_element_type=jnp.float32
     )

time: 63.3 us -> 60.2 us (0.951)
  Pallas kernels: 0 us -> 5.48 us
  waiting for transfers between devices: 15.2 us -> 10 us
  local copies, waits for them, and re-layouts: 10.1 us -> 6.79 us
    unnamed x11 -> x12, local copies, waits for them, and re-layouts: 6.51 us -> 0.03 us
    all_to_all x1, waiting for transfers between devices: 12.2 us -> 6.1 us  [shards(): lax.all_to_all(product_buffer.reshape(regions, CAP, vectors, padded), 'do...]
    pallas_call x0 -> x1, Pallas kernels: none -> 5.48 us  [resident(): pl.pallas_call(kernel, in_specs=[pl.BlockSpec(memory_space=pl.ANY)], out_...]
    slice x0 -> x1, local copies, waits for them, and re-layouts: none -> 4.07 us  [shards(): late_inverse[:half]]
    dot_general x1, matrix products: 2.22 us -> 5.22 us  [shards(): jnp.einsum('ebc,ecm->ebm', late_inverse, interface_basis, preferred_eleme...]
    dot_general x1, matrix products: 2.54 us -> 0.79 us  [shards(): jnp.einsum('ekb,ebc->ekc', corrected_in[half:], late_inverse[half:], pref...]
    dot_general x1, matrix products: 2.02 us -> 0.5 us  [shards(): jnp.einsum('es,skc->ekc', selector, products, preferred_element_type=jnp....]
    ppermute x3, waiting for transfers between devices: 2.96 us -> 3.93 us  [group_sum(): value = value + lax.ppermute(value, axis, pairs)]
  transfers between devices with their start and end apart: 4 -> 4, of which waited for: 3 -> 4; matrix products, arithmetic and copies ran while one was open for 19% -> 18% of each run, Pallas kernels for 0% -> 9%
where the time goes in v10:
time: 60.2 us; the launch traced here: 60 us
  matrix products  23 us (38%)
  starting transfers between devices  12.8 us (21%)
  waiting for transfers between devices  10 us (17%)
  local copies, waits for them, and re-layouts  6.79 us (11%)
  Pallas kernels  5.48 us (9%)
  other arithmetic  1.7 us (3%)
    dot_general x1, matrix products, shards(): jnp.einsum('tkb,tbc->tkc', sources, coupling, preferred_element_type=jnp....  9.07 us
    all_to_all x1, starting transfers between devices, shards(): lax.all_to_all(product_buffer.reshape(regions, CAP, vectors, padded), 'do...  8.17 us
    all_to_all x1, waiting for transfers between devices, shards(): lax.all_to_all(product_buffer.reshape(regions, CAP, vectors, padded), 'do...  6.1 us
    pallas_call x1, Pallas kernels, resident(): pl.pallas_call(kernel, in_specs=[pl.BlockSpec(memory_space=pl.ANY)], out_...  5.48 us
    dot_general x1, matrix products, shards(): jnp.einsum('ebc,ecm->ebm', late_inverse, interface_basis, preferred_eleme...  5.22 us
    dot_general x1, matrix products, shards(): jnp.einsum('ekb,ebc->ekc', residual_in, block_inverse, preferred_element_...  5.17 us
    ppermute x3, starting transfers between devices, group_sum(): value = value + lax.ppermute(value, axis, pairs)  4.59 us
    slice x1, local copies, waits for them, and re-layouts, shards(): late_inverse[:half]  4.07 us
  transfers between devices with their start and end apart: 4, of which 4 were waited for; matrix products, arithmetic and copies ran while one was open for 18% of the time, Pallas kernels for 9%

profile of v10, /device:TPU:0, one launch (start us, length us, event | category | flops | bytes accessed | tf_op | source)
XLA Modules:
  0.0 60.0 jit_solution(13473986005468716402)
XLA Ops:
  0.0 0.0 copy-start
  0.0 0.8 %pad_add_fusion = s32[48]{0:T(128)S(1)} fusion(s32[16]{0:T(128)} %param.13, s32[16]{0:T(128)} %param.12, s32[16]{0:T(128)} %bitcast.37), kind=kLoop, calls=%fused_computation.48 | loop fusion | flops 96 | bytes 384 | tf_op jit(solution)/shard_map/concatenate | solution.py:61
  0.8 0.2 convert_reduce_fusion.1
  1.0 0.1 multiply_add_fusion
  1.1 0.1 fusion.36
  1.2 0.1 select_reduce_fusion
  1.3 0.1 slice.29
  1.4 5.2 %fusion.26 = bf16[8,32,625]{2,1,0:T(8,128)(2,1)S(1)} fusion(bf16[8,32,625]{2,1,0:T(8,128)(2,1)} %param.8, bf16[8,625,625]{2,0,1:T(8,128)(2,1)} %param.9), kind=kOutput, calls=%fused_computation.22 | convolution fusion | flops 200160000 | bytes 6890000 | tf_op jit(solution)/shard_map/ekb,ebc->ekc/dot_general | solution.py:57
  6.6 0.7 %gather_fusion = bf16[16,32,625]{2,1,0:T(8,128)(2,1)S(1)} fusion(bf16[8,32,625]{2,1,0:T(8,128)(2,1)S(1)} %fusion.26, s32[1024]{0:T(1024)S(1)} %pad_clamp_fusion.1), kind=kCustom, calls=%fused_computation | custom fusion | bytes 1280064 | tf_op jit(solution)/shard_map/gather | solution.py:75
  7.2 9.1 %fusion.11 = bf16[16,32,625]{2,1,0:T(8,128)(2,1)S(1)} fusion(bf16[16,32,625]{2,1,0:T(8,128)(2,1)S(1)} %gather_fusion, bf16[16,625,625]{2,0,1:T(8,128)(2,1)} %param.10), kind=kOutput, calls=%fused_computation.14 | convolution fusion | flops 400320000 | bytes 13780000 | tf_op jit(solution)/shard_map/tkb,tbc->tkc/dot_general | solution.py:76
  16.3 0.1 pad_maximum_fusion
  16.4 0.1 and_select_fusion
  16.5 0.1 fusion.30
  16.6 1.8 %gather_fusion.1 = bf16[32,32,640]{2,1,0:T(8,128)(2,1)} fusion(bf16[17,32,640]{2,1,0:T(8,128)(2,1)S(1)} %fusion.30, s32[1024]{0:T(1024)S(1)} %pad_clamp_fusion), kind=kCustom, calls=%fused_computation.1 | custom fusion | bytes 2621568 | tf_op jit(solution)/shard_map/gather | solution.py:87
  18.4 8.2 %all-to-all-start = ((bf16[16,2,32,640]{3,2,1,0:T(8,128)(2,1)}), bf16[16,2,32,640]{3,2,1,0:T(8,128)(2,1)S(1)}, u32[]{:S(2)}, u32[]{:S(2)}) async-start(bf16[16,2,32,640]{3,2,1,0:T(8,128)(2,1)} %bitcast.3), calls=%async_computation | async-start | bytes 2621440 | tf_op jit(solution)/shard_map/all_to_all | solution.py:88
  26.5 5.5 %shard_map.82 = bf16[625,8,625]{2,1,0:T(8,128)(2,1)} custom-call(bf16[625,8,625]{2,1,0:T(8,128)(2,1)} %bitcast.33), custom_call_target="tpu_custom_call" | custom-call | tf_op jit(solution)/shard_map/pallas_call | solution.py:18
  32.0 0.0 copy-done
  32.0 0.0 copy-start.1
  32.1 5.2 %fusion.14 = bf16[8,625,64]{1,2,0:T(8,128)(2,1)S(1)} fusion(bf16[8,625,64]{1,2,0:T(8,128)(2,1)S(1)} %copy-done, bf16[8,625,625]{2,0,1:T(8,128)(2,1)} %bitcast.31), kind=kOutput, calls=%fused_computation.15 | convolution fusion | flops 400320000 | bytes 7530000 | tf_op jit(solution)/shard_map/ebc,ecm->ebm/dot_general | solution.py:105
  37.3 0.0 copy-done.1
  37.3 0.0 copy-start.4
  37.3 4.1 %fusion.42 = (bf16[4,625,625]{2,0,1:T(4,128)(2,1)}, bf16[4,625,625]{2,0,1:T(4,128)(2,1)}) fusion(bf16[8,625,625]{2,0,1:T(8,128)(2,1)S(1)} %bitcast.32), kind=kLoop, calls=%fused_computation.53 | loop fusion | bytes 12500000 | tf_op jit(solution)/shard_map/slice | solution.py:121
  41.4 6.1 %all-to-all-done = bf16[16,2,32,640]{3,2,1,0:T(8,128)(2,1)S(1)} async-done(((bf16[16,2,32,640]{3,2,1,0:T(8,128)(2,1)}), bf16[16,2,32,640]{3,2,1,0:T(8,128)(2,1)S(1)}, u32[]{:S(2)}, u32[]{:S(2)}) %all-to-all-start) | async-done | bytes 1310752 | tf_op jit(solution)/shard_map/all_to_all | solution.py:88
  47.5 0.0 copy-start.3
  47.5 0.1 slice.41
  47.6 0.1 convert_reduce_fusion
  47.7 0.0 copy-done.4
  47.7 0.5 fusion.23
  48.2 0.3 convolution_bitcast_fusion.1
  48.5 0.0 copy-start.2
  48.5 0.1 collective-permute-start
  48.6 0.1 fusion.43
  48.7 1.1 %collective-permute-done = f32[32,64]{1,0:T(8,128)S(1)} collective-permute-done((f32[32,64]{1,0:T(8,128)S(1)}, f32[32,64]{1,0:T(8,128)S(1)}, u32[]{:S(2)}, u32[]{:S(2)}) %collective-permute-start) | collective-permute-done | bytes 8224 | tf_op jit(solution)/shard_map/ppermute | solution.py:35
  49.7 1.5 %collective-permute-start.1 = (f32[32,64]{1,0:T(8,128)S(1)}, f32[32,64]{1,0:T(8,128)S(1)}, u32[]{:S(2)}, u32[]{:S(2)}) collective-permute-start(f32[32,64]{1,0:T(8,128)S(1)} %add.37), channel_id=1, source_target_pairs={{0,2},{1,3},{2,0},{3,1},{4,6},{5,7},{6,4},{7,5},{8,10},{9,11},{10,... | collective-permute-start | bytes 24584 | tf_op jit(solution)/shard_map/ppermute | solution.py:35
  51.2 0.0 copy-done.3
  51.2 0.8 %fusion.6 = f32[4,32,625]{2,1,0:T(8,128)S(1)} fusion(bf16[4,625,625]{2,0,1:T(4,128)(2,1)S(1)} %copy-done.3, bf16[4,32,625]{2,0,1:T(4,128)(2,1)S(1)} %get-tuple-element.8), kind=kOutput, calls=%fused_computation.8 | convolution fusion | flops 100000000 | bytes 3605000 | tf_op jit(solution)/shard_map/ekb,ebc->ekc/dot_general | solution.py:124
  52.0 0.0 copy-start.5
  52.0 1.4 %collective-permute-done.1 = f32[32,64]{1,0:T(8,128)S(1)} collective-permute-done((f32[32,64]{1,0:T(8,128)S(1)}, f32[32,64]{1,0:T(8,128)S(1)}, u32[]{:S(2)}, u32[]{:S(2)}) %collective-permute-start.1) | collective-permute-done | bytes 8224 | tf_op jit(solution)/shard_map/ppermute | solution.py:35
  53.5 3.0 %collective-permute-start.2 = (f32[32,64]{1,0:T(8,128)S(1)}, f32[32,64]{1,0:T(8,128)S(1)}, u32[]{:S(2)}, u32[]{:S(2)}) collective-permute-start(f32[32,64]{1,0:T(8,128)S(1)} %add.38), channel_id=1, source_target_pairs={{0,4},{1,5},{2,6},{3,7},{4,0},{5,1},{6,2},{7,3},{8,12},{9,13},{10,... | collective-permute-start | bytes 24584 | tf_op jit(solution)/shard_map/ppermute | solution.py:35
  56.5 0.0 copy-done.2
  56.5 0.8 %fusion.8 = f32[4,32,625]{2,1,0:T(8,128)S(1)} fusion(bf16[4,625,625]{2,0,1:T(4,128)(2,1)S(1)} %copy-done.2, bf16[4,32,625]{2,0,1:T(4,128)(2,1)S(1)} %get-tuple-element.7), kind=kOutput, calls=%fused_computation.10 | convolution fusion | flops 100000000 | bytes 3605000 | tf_op jit(solution)/shard_map/ekb,ebc->ekc/dot_general | solution.py:118
  57.3 1.4 %collective-permute-done.2 = f32[32,64]{1,0:T(8,128)S(1)} collective-permute-done((f32[32,64]{1,0:T(8,128)S(1)}, f32[32,64]{1,0:T(8,128)S(1)}, u32[]{:S(2)}, u32[]{:S(2)}) %collective-permute-start.2) | collective-permute-done | bytes 8224 | tf_op jit(solution)/shard_map/ppermute | solution.py:35
  58.7 0.0 copy-done.5
  58.7 0.1 fusion.29
  58.9 1.1 %fusion.22 = f32[8,32,625]{2,1,0:T(8,128)} fusion(bf16[32,64,1]{1,0,2:T(8,128)(2,1)S(1)} %fusion.29, bf16[8,625,64]{1,2,0:T(8,128)(2,1)S(1)} %copy-done, f32[4,32,625]{2,1,0:T(8,128)S(1)} %fusion.6, f32[4,32,625]{2,1,0:T(8,128)S(1)} %fusion.8), kind=kOutput, calls=%fused_computation.20 | convolution fusion | flops 20800000 | bytes 1924096 | tf_op jit(solution)/shard_map/km,ebm->ekb/dot_general | solution.py:139
  (8 shorter events, 0.0 us)
Async XLA Ops:
  0.0 32.0 %copy-start = (bf16[8,625,64]{1,2,0:T(8,128)(2,1)S(1)}, bf16[8,625,64]{1,2,0:T(8,128)(2,1)}, u32[]{:S(2)}) copy-start(bf16[8,625,64]{1,2,0:T(8,128)(2,1)} %param.14) | copy-start | bytes 1920004
  18.4 29.1 %all-to-all-start = ((bf16[16,2,32,640]{3,2,1,0:T(8,128)(2,1)}), bf16[16,2,32,640]{3,2,1,0:T(8,128)(2,1)S(1)}, u32[]{:S(2)}, u32[]{:S(2)}) async-start(bf16[16,2,32,640]{3,2,1,0:T(8,128)(2,1)} %bitcast.3), calls=%async_computation | async-start | bytes 2621440 | tf_op jit(solution)/shard_map/all_to_all | solution.py:88
  32.0 5.2 %copy-start.1 = (bf16[625,8,625]{2,1,0:T(8,128)(2,1)S(1)}, bf16[625,8,625]{2,1,0:T(8,128)(2,1)}, u32[]{:S(2)}) copy-start(bf16[625,8,625]{2,1,0:T(8,128)(2,1)} %shard_map.82) | copy-start | bytes 18750004
  37.3 10.4 %copy-start.4 = (bf16[8,32,625]{2,1,0:T(8,128)(2,1)S(1)}, bf16[8,32,625]{2,1,0:T(8,128)(2,1)}, u32[]{:S(2)}) copy-start(bf16[8,32,625]{2,1,0:T(8,128)(2,1)} %param.8) | copy-start | bytes 960004
  47.5 3.8 %copy-start.3 = (bf16[4,625,625]{2,0,1:T(4,128)(2,1)S(1)}, bf16[4,625,625]{2,0,1:T(4,128)(2,1)}, u32[]{:S(2)}) copy-start(bf16[4,625,625]{2,0,1:T(4,128)(2,1)} %get-tuple-element.6) | copy-start | bytes 9375004
  48.5 8.0 %copy-start.2 = (bf16[4,625,625]{2,0,1:T(4,128)(2,1)S(1)}, bf16[4,625,625]{2,0,1:T(4,128)(2,1)}, u32[]{:S(2)}) copy-start(bf16[4,625,625]{2,0,1:T(4,128)(2,1)} %get-tuple-element.5) | copy-start | bytes 9375004
  48.5 1.2 %collective-permute-start = (f32[32,64]{1,0:T(8,128)S(1)}, f32[32,64]{1,0:T(8,128)S(1)}, u32[]{:S(2)}, u32[]{:S(2)}) collective-permute-start(f32[32,64]{1,0:T(8,128)S(1)} %convolution_bitcast_fusion.1), channel_id=1, source_target_pairs={{0,1},{1,0},{2,3},{3,2},{4,5},{5,4},{6,7},{7,6},{8,9},{9,8},{10,11... | collective-permute-start | bytes 24584 | tf_op jit(solution)/shard_map/ppermute | solution.py:35
  49.7 3.7 %collective-permute-start.1 = (f32[32,64]{1,0:T(8,128)S(1)}, f32[32,64]{1,0:T(8,128)S(1)}, u32[]{:S(2)}, u32[]{:S(2)}) collective-permute-start(f32[32,64]{1,0:T(8,128)S(1)} %add.37), channel_id=1, source_target_pairs={{0,2},{1,3},{2,0},{3,1},{4,6},{5,7},{6,4},{7,5},{8,10},{9,11},{10,... | collective-permute-start | bytes 24584 | tf_op jit(solution)/shard_map/ppermute | solution.py:35
  52.0 6.7 %copy-start.5 = (f32[1,64,64]{2,1,0:T(8,128)S(1)}, f32[1,64,64]{2,1,0:T(8,128)}, u32[]{:S(2)}) copy-start(f32[1,64,64]{2,1,0:T(8,128)} %param.15) | copy-start | bytes 49156
  53.5 5.2 %collective-permute-start.2 = (f32[32,64]{1,0:T(8,128)S(1)}, f32[32,64]{1,0:T(8,128)S(1)}, u32[]{:S(2)}, u32[]{:S(2)}) collective-permute-start(f32[32,64]{1,0:T(8,128)S(1)} %add.38), channel_id=1, source_target_pairs={{0,4},{1,5},{2,6},{3,7},{4,0},{5,1},{6,2},{7,3},{8,12},{9,13},{10,... | collective-permute-start | bytes 24584 | tf_op jit(solution)/shard_map/ppermute | solution.py:35

commit v11 on v10

--- a/solution.py
+++ b/solution.py
@@ -10,17 +10,28 @@
 
 
 def resident(value):
+    parts = 5
+    rows = value.shape[0]
+    edges = [rows * i // parts for i in range(parts + 1)]
+
     def kernel(source, target, flag):
-        copy = pltpu.make_async_copy(source, target, flag.at[0])
-        copy.start()
-        copy.wait()
+        copies = [
+            pltpu.make_async_copy(
+                source.at[pl.ds(lo, hi - lo)], target.at[pl.ds(lo, hi - lo)], flag.at[i]
+            )
+            for i, (lo, hi) in enumerate(zip(edges[:-1], edges[1:]))
+        ]
+        for copy in copies:
+            copy.start()
+        for copy in copies:
+            copy.wait()
 
     return pl.pallas_call(
         kernel,
         in_specs=[pl.BlockSpec(memory_space=pl.ANY)],
         out_specs=pl.BlockSpec(memory_space=pltpu.VMEM),
         out_shape=jax.ShapeDtypeStruct(value.shape, value.dtype),
-        scratch_shapes=[pltpu.SemaphoreType.DMA((1,))],
+        scratch_shapes=[pltpu.SemaphoreType.DMA((parts,))],
         compiler_params=pltpu.CompilerParams(vmem_limit_bytes=48 * 1024 * 1024),
     )(value)
 
@@ -74,7 +85,10 @@
     ).astype(jnp.int32)
     sources = initial[tile_source]
     local_products = jnp.einsum(
-        "tkb,tbc->tkc", sources, coupling, preferred_element_type=jnp.float32
+        "tkb,tbc->tkc",
+        sources,
+        jnp.transpose(resident(jnp.transpose(coupling, (1, 0, 2))), (1, 0, 2)),
+        preferred_element_type=jnp.float32,
     ).astype(jnp.bfloat16)
     marks = jnp.concatenate([tile_target, jnp.full((1,), -1, jnp.int32)]).astype(jnp.bfloat16)
     column = lax.broadcasted_iota(jnp.int32, (tiles + 1, vectors, padded - width), 2)

time: 60.2 us -> 67.4 us (1.12)
  Pallas kernels: 5.48 us -> 15.6 us
  matrix products: 23 us -> 20.1 us
    pallas_call x1 -> x2, Pallas kernels: 5.48 us -> 15.6 us  [resident(): pl.pallas_call(kernel, in_specs=[pl.BlockSpec(memory_space=pl.ANY)], out_...]
    dot_general x1, matrix products: 5.17 us -> 2.24 us  [shards(): jnp.einsum('ekb,ebc->ekc', residual_in, block_inverse, preferred_element_...]
  transfers between devices with their start and end apart: 4 -> 4, of which waited for: 4 -> 4; matrix products, arithmetic and copies ran while one was open for 18% -> 16% of each run, Pallas kernels for 9% -> 8%
where the time goes in v11:
time: 67.4 us; the launch traced here: 67.1 us
  matrix products  20.1 us (30%)
  Pallas kernels  15.6 us (23%)
  starting transfers between devices  12.7 us (19%)
  waiting for transfers between devices  9.88 us (15%)
  local copies, waits for them, and re-layouts  6.85 us (10%)
  other arithmetic  1.7 us (3%)
    pallas_call x2, Pallas kernels, resident(): pl.pallas_call(kernel, in_specs=[pl.BlockSpec(memory_space=pl.ANY)], out_...  15.6 us
    dot_general x1, matrix products, shards(): jnp.einsum('tkb,tbc->tkc', sources, jnp.transpose(resident(jnp.transpose(...  9.07 us
    all_to_all x1, starting transfers between devices, shards(): lax.all_to_all(product_buffer.reshape(regions, CAP, vectors, padded), 'do...  8.16 us
    all_to_all x1, waiting for transfers between devices, shards(): lax.all_to_all(product_buffer.reshape(regions, CAP, vectors, padded), 'do...  5.96 us
    dot_general x1, matrix products, shards(): jnp.einsum('ebc,ecm->ebm', late_inverse, interface_basis, preferred_eleme...  5.22 us
    ppermute x3, starting transfers between devices, group_sum(): value = value + lax.ppermute(value, axis, pairs)  4.59 us
    slice x1, local copies, waits for them, and re-layouts, shards(): late_inverse[:half]  4.11 us
    ppermute x3, waiting for transfers between devices, group_sum(): value = value + lax.ppermute(value, axis, pairs)  3.92 us
  transfers between devices with their start and end apart: 4, of which 4 were waited for; matrix products, arithmetic and copies ran while one was open for 16% of the time, Pallas kernels for 8%

profile of v11, /device:TPU:0, one launch (start us, length us, event | category | flops | bytes accessed | tf_op | source)
XLA Modules:
  0.0 67.1 jit_solution(9147070091742603917)
XLA Ops:
  0.0 0.0 copy-start
  0.0 0.8 %pad_add_fusion = s32[48]{0:T(128)S(1)} fusion(s32[16]{0:T(128)} %param.13, s32[16]{0:T(128)} %param.12, s32[16]{0:T(128)} %bitcast.41), kind=kLoop, calls=%fused_computation.48 | loop fusion | flops 96 | bytes 384 | tf_op jit(solution)/shard_map/concatenate | solution.py:72
  0.8 0.2 convert_reduce_fusion.1
  1.0 0.1 multiply_add_fusion
  1.1 0.1 fusion.36
  1.2 0.1 select_reduce_fusion
  1.3 0.0 copy-start.4
  1.4 0.0 copy-start.5
  1.4 10.1 %shard_map.82 = bf16[625,16,625]{2,1,0:T(8,128)(2,1)} custom-call(bf16[625,16,625]{2,1,0:T(8,128)(2,1)} %bitcast.35), custom_call_target="tpu_custom_call" | custom-call | tf_op jit(solution)/shard_map/pallas_call | solution.py:29
  11.4 0.1 slice.29
  11.5 0.0 copy-done.4
  11.5 0.0 copy-done.5
  11.5 2.2 %fusion.26 = bf16[8,32,625]{2,1,0:T(8,128)(2,1)S(1)} fusion(bf16[8,32,625]{2,1,0:T(8,128)(2,1)S(1)} %copy-done.5, bf16[8,625,625]{2,0,1:T(8,128)(2,1)S(1)} %copy-done.4), kind=kOutput, calls=%fused_computation.22 | convolution fusion | flops 200160000 | bytes 6890000 | tf_op jit(solution)/shard_map/ekb,ebc->ekc/dot_general | solution.py:68
  13.7 0.7 gather_fusion
  14.4 9.1 %fusion.11 = bf16[16,32,625]{2,1,0:T(8,128)(2,1)S(1)} fusion(bf16[16,32,625]{2,1,0:T(8,128)(2,1)S(1)} %gather_fusion, bf16[16,625,625]{2,0,1:T(8,128)(2,1)} %bitcast.36), kind=kOutput, calls=%fused_computation.14 | convolution fusion | flops 400320000 | bytes 13780000 | tf_op jit(solution)/shard_map/tkb,tbc->tkc/dot_general | solution.py:87
  23.5 0.1 pad_maximum_fusion
  23.6 0.1 and_select_fusion
  23.7 0.1 fusion.30
  23.8 1.8 %gather_fusion.1 = bf16[32,32,640]{2,1,0:T(8,128)(2,1)} fusion(bf16[17,32,640]{2,1,0:T(8,128)(2,1)S(1)} %fusion.30, s32[1024]{0:T(1024)S(1)} %pad_clamp_fusion), kind=kCustom, calls=%fused_computation.1 | custom fusion | bytes 2621568 | tf_op jit(solution)/shard_map/gather | solution.py:101
  25.6 8.2 %all-to-all-start = ((bf16[16,2,32,640]{3,2,1,0:T(8,128)(2,1)}), bf16[16,2,32,640]{3,2,1,0:T(8,128)(2,1)S(1)}, u32[]{:S(2)}, u32[]{:S(2)}) async-start(bf16[16,2,32,640]{3,2,1,0:T(8,128)(2,1)} %bitcast.5), calls=%async_computation | async-start | bytes 2621440 | tf_op jit(solution)/shard_map/all_to_all | solution.py:102
  33.7 5.6 %shard_map.83 = bf16[625,8,625]{2,1,0:T(8,128)(2,1)} custom-call(bf16[625,8,625]{2,1,0:T(8,128)(2,1)} %bitcast.37), custom_call_target="tpu_custom_call" | custom-call | tf_op jit(solution)/shard_map/pallas_call | solution.py:29
  39.3 0.0 copy-done
  39.3 0.0 copy-start.1
  39.4 5.2 %fusion.14 = bf16[8,625,64]{1,2,0:T(8,128)(2,1)S(1)} fusion(bf16[8,625,64]{1,2,0:T(8,128)(2,1)S(1)} %copy-done, bf16[8,625,625]{2,0,1:T(8,128)(2,1)} %bitcast.33), kind=kOutput, calls=%fused_computation.15 | convolution fusion | flops 400320000 | bytes 7530000 | tf_op jit(solution)/shard_map/ebc,ecm->ebm/dot_general | solution.py:119
  44.6 0.0 copy-done.1
  44.6 4.1 %fusion.42 = (bf16[4,625,625]{2,0,1:T(4,128)(2,1)}, bf16[4,625,625]{2,0,1:T(4,128)(2,1)}) fusion(bf16[8,625,625]{2,0,1:T(8,128)(2,1)S(1)} %bitcast.34), kind=kLoop, calls=%fused_computation.53 | loop fusion | bytes 12500000 | tf_op jit(solution)/shard_map/slice | solution.py:135
  48.7 6.0 %all-to-all-done = bf16[16,2,32,640]{3,2,1,0:T(8,128)(2,1)S(1)} async-done(((bf16[16,2,32,640]{3,2,1,0:T(8,128)(2,1)}), bf16[16,2,32,640]{3,2,1,0:T(8,128)(2,1)S(1)}, u32[]{:S(2)}, u32[]{:S(2)}) %all-to-all-start) | async-done | bytes 1310752 | tf_op jit(solution)/shard_map/all_to_all | solution.py:102
  54.7 0.0 copy-start.3
  54.7 0.1 slice.41
  54.8 0.1 convert_reduce_fusion
  54.9 0.5 fusion.23
  55.4 0.3 convolution_bitcast_fusion.1
  55.7 0.0 copy-start.2
  55.7 0.1 collective-permute-start
  55.7 0.1 fusion.43
  55.9 1.1 %collective-permute-done = f32[32,64]{1,0:T(8,128)S(1)} collective-permute-done((f32[32,64]{1,0:T(8,128)S(1)}, f32[32,64]{1,0:T(8,128)S(1)}, u32[]{:S(2)}, u32[]{:S(2)}) %collective-permute-start) | collective-permute-done | bytes 8224 | tf_op jit(solution)/shard_map/ppermute | solution.py:46
  56.9 1.5 %collective-permute-start.1 = (f32[32,64]{1,0:T(8,128)S(1)}, f32[32,64]{1,0:T(8,128)S(1)}, u32[]{:S(2)}, u32[]{:S(2)}) collective-permute-start(f32[32,64]{1,0:T(8,128)S(1)} %add.37), channel_id=1, source_target_pairs={{0,2},{1,3},{2,0},{3,1},{4,6},{5,7},{6,4},{7,5},{8,10},{9,11},{10,... | collective-permute-start | bytes 24584 | tf_op jit(solution)/shard_map/ppermute | solution.py:46
  58.4 0.0 copy-done.3
  58.4 0.8 %fusion.8 = f32[4,32,625]{2,1,0:T(8,128)S(1)} fusion(bf16[4,625,625]{2,0,1:T(4,128)(2,1)S(1)} %copy-done.3, bf16[4,32,625]{2,0,1:T(4,128)(2,1)S(1)} %get-tuple-element.7), kind=kOutput, calls=%fused_computation.10 | convolution fusion | flops 100000000 | bytes 3605000 | tf_op jit(solution)/shard_map/ekb,ebc->ekc/dot_general | solution.py:132
  59.2 0.0 copy-start.6
  59.2 1.4 %collective-permute-done.1 = f32[32,64]{1,0:T(8,128)S(1)} collective-permute-done((f32[32,64]{1,0:T(8,128)S(1)}, f32[32,64]{1,0:T(8,128)S(1)}, u32[]{:S(2)}, u32[]{:S(2)}) %collective-permute-start.1) | collective-permute-done | bytes 8224 | tf_op jit(solution)/shard_map/ppermute | solution.py:46
  60.7 3.0 %collective-permute-start.2 = (f32[32,64]{1,0:T(8,128)S(1)}, f32[32,64]{1,0:T(8,128)S(1)}, u32[]{:S(2)}, u32[]{:S(2)}) collective-permute-start(f32[32,64]{1,0:T(8,128)S(1)} %add.38), channel_id=1, source_target_pairs={{0,4},{1,5},{2,6},{3,7},{4,0},{5,1},{6,2},{7,3},{8,12},{9,13},{10,... | collective-permute-start | bytes 24584 | tf_op jit(solution)/shard_map/ppermute | solution.py:46
  63.7 0.0 copy-done.2
  63.7 0.8 %fusion.6 = f32[4,32,625]{2,1,0:T(8,128)S(1)} fusion(bf16[4,625,625]{2,0,1:T(4,128)(2,1)S(1)} %copy-done.2, bf16[4,32,625]{2,0,1:T(4,128)(2,1)S(1)} %get-tuple-element.8), kind=kOutput, calls=%fused_computation.8 | convolution fusion | flops 100000000 | bytes 3605000 | tf_op jit(solution)/shard_map/ekb,ebc->ekc/dot_general | solution.py:138
  64.5 1.4 %collective-permute-done.2 = f32[32,64]{1,0:T(8,128)S(1)} collective-permute-done((f32[32,64]{1,0:T(8,128)S(1)}, f32[32,64]{1,0:T(8,128)S(1)}, u32[]{:S(2)}, u32[]{:S(2)}) %collective-permute-start.2) | collective-permute-done | bytes 8224 | tf_op jit(solution)/shard_map/ppermute | solution.py:46
  65.9 0.0 copy-done.6
  65.9 0.1 fusion.29
  66.1 1.1 %fusion.22 = f32[8,32,625]{2,1,0:T(8,128)} fusion(bf16[32,64,1]{1,0,2:T(8,128)(2,1)S(1)} %fusion.29, bf16[8,625,64]{1,2,0:T(8,128)(2,1)S(1)} %copy-done, f32[4,32,625]{2,1,0:T(8,128)S(1)} %fusion.6, f32[4,32,625]{2,1,0:T(8,128)S(1)} %fusion.8), kind=kOutput, calls=%fused_computation.20 | convolution fusion | flops 20800000 | bytes 1924096 | tf_op jit(solution)/shard_map/km,ebm->ekb/dot_general | solution.py:153
  (8 shorter events, 0.0 us)
Async XLA Ops:
  0.0 39.3 %copy-start = (bf16[8,625,64]{1,2,0:T(8,128)(2,1)S(1)}, bf16[8,625,64]{1,2,0:T(8,128)(2,1)}, u32[]{:S(2)}) copy-start(bf16[8,625,64]{1,2,0:T(8,128)(2,1)} %param.14) | copy-start | bytes 1920004
  1.3 10.2 %copy-start.4 = (bf16[8,625,625]{2,0,1:T(8,128)(2,1)S(1)}, bf16[8,625,625]{2,0,1:T(8,128)(2,1)}, u32[]{:S(2)}) copy-start(bf16[8,625,625]{2,0,1:T(8,128)(2,1)} %param.9) | copy-start | bytes 18750004
  1.4 10.2 %copy-start.5 = (bf16[8,32,625]{2,1,0:T(8,128)(2,1)S(1)}, bf16[8,32,625]{2,1,0:T(8,128)(2,1)}, u32[]{:S(2)}) copy-start(bf16[8,32,625]{2,1,0:T(8,128)(2,1)} %param.8) | copy-start | bytes 960004
  25.6 29.1 %all-to-all-start = ((bf16[16,2,32,640]{3,2,1,0:T(8,128)(2,1)}), bf16[16,2,32,640]{3,2,1,0:T(8,128)(2,1)S(1)}, u32[]{:S(2)}, u32[]{:S(2)}) async-start(bf16[16,2,32,640]{3,2,1,0:T(8,128)(2,1)} %bitcast.5), calls=%async_computation | async-start | bytes 2621440 | tf_op jit(solution)/shard_map/all_to_all | solution.py:102
  39.3 5.2 %copy-start.1 = (bf16[625,8,625]{2,1,0:T(8,128)(2,1)S(1)}, bf16[625,8,625]{2,1,0:T(8,128)(2,1)}, u32[]{:S(2)}) copy-start(bf16[625,8,625]{2,1,0:T(8,128)(2,1)} %shard_map.83) | copy-start | bytes 18750004
  54.7 3.8 %copy-start.3 = (bf16[4,625,625]{2,0,1:T(4,128)(2,1)S(1)}, bf16[4,625,625]{2,0,1:T(4,128)(2,1)}, u32[]{:S(2)}) copy-start(bf16[4,625,625]{2,0,1:T(4,128)(2,1)} %get-tuple-element.5) | copy-start | bytes 9375004
  55.7 8.0 %copy-start.2 = (bf16[4,625,625]{2,0,1:T(4,128)(2,1)S(1)}, bf16[4,625,625]{2,0,1:T(4,128)(2,1)}, u32[]{:S(2)}) copy-start(bf16[4,625,625]{2,0,1:T(4,128)(2,1)} %get-tuple-element.6) | copy-start | bytes 9375004
  55.7 1.2 %collective-permute-start = (f32[32,64]{1,0:T(8,128)S(1)}, f32[32,64]{1,0:T(8,128)S(1)}, u32[]{:S(2)}, u32[]{:S(2)}) collective-permute-start(f32[32,64]{1,0:T(8,128)S(1)} %convolution_bitcast_fusion.1), channel_id=1, source_target_pairs={{0,1},{1,0},{2,3},{3,2},{4,5},{5,4},{6,7},{7,6},{8,9},{9,8},{10,11... | collective-permute-start | bytes 24584 | tf_op jit(solution)/shard_map/ppermute | solution.py:46
  56.9 3.7 %collective-permute-start.1 = (f32[32,64]{1,0:T(8,128)S(1)}, f32[32,64]{1,0:T(8,128)S(1)}, u32[]{:S(2)}, u32[]{:S(2)}) collective-permute-start(f32[32,64]{1,0:T(8,128)S(1)} %add.37), channel_id=1, source_target_pairs={{0,2},{1,3},{2,0},{3,1},{4,6},{5,7},{6,4},{7,5},{8,10},{9,11},{10,... | collective-permute-start | bytes 24584 | tf_op jit(solution)/shard_map/ppermute | solution.py:46
  59.2 6.7 %copy-start.6 = (f32[1,64,64]{2,1,0:T(8,128)S(1)}, f32[1,64,64]{2,1,0:T(8,128)}, u32[]{:S(2)}) copy-start(f32[1,64,64]{2,1,0:T(8,128)} %param.15) | copy-start | bytes 49156
  60.7 5.2 %collective-permute-start.2 = (f32[32,64]{1,0:T(8,128)S(1)}, f32[32,64]{1,0:T(8,128)S(1)}, u32[]{:S(2)}, u32[]{:S(2)}) collective-permute-start(f32[32,64]{1,0:T(8,128)S(1)} %add.38), channel_id=1, source_target_pairs={{0,4},{1,5},{2,6},{3,7},{4,0},{5,1},{6,2},{7,3},{8,12},{9,13},{10,... | collective-permute-start | bytes 24584 | tf_op jit(solution)/shard_map/ppermute | solution.py:46

commit v12 on v10

--- a/solution.py
+++ b/solution.py
@@ -29,6 +29,16 @@
     size = lax.axis_size(axis)
     if size & (size - 1):
         return lax.psum(value, axis)
+    if size == 8:
+        ring = size // 2
+        value = value + lax.ppermute(value, axis, [(i, i ^ 1) for i in range(size)])
+        left = lax.ppermute(value, axis, [(i, (i + 2) % size) for i in range(size)])
+        right = lax.ppermute(value, axis, [(i, (i - 2) % size) for i in range(size)])
+        far = lax.ppermute(right, axis, [(i, (i - 2) % size) for i in range(size)])
+        stacked = jnp.stack([value, right, far, left])
+        place = lax.axis_index(axis) // 2
+        parts = [stacked[(k - place) % ring] for k in range(ring)]
+        return (parts[0] + parts[1]) + (parts[2] + parts[3])
     bit = 1
     while bit < size:
         pairs = [(i, i ^ bit) for i in range(size)]

time: 60.2 us -> 61.4 us (1.020); the launches traced: 60 us -> 60.2 us
  waiting for transfers between devices: 10 us -> 2.26 us
  local copies, waits for them, and re-layouts: 6.79 us -> 13 us
  starting transfers between devices: 12.8 us -> 14.6 us
    slice x1, local copies, waits for them, and re-layouts: 4.07 us -> 10.2 us  [shards(): late_inverse[:half]]
    all_to_all x1, waiting for transfers between devices: 6.1 us -> 0.01 us  [shards(): lax.all_to_all(product_buffer.reshape(regions, CAP, vectors, padded), 'do...]
    ppermute x3 -> x4, starting transfers between devices: 4.59 us -> 6.4 us  [the longest x1 3.51 us: group_sum(): far = lax.ppermute(right, axis, [(i, (i - 2) % size) for i in range(size)])]
    ppermute x3 -> x4, waiting for transfers between devices: 3.93 us -> 2.26 us  [the longest x1 1.05 us: group_sum(): value = value + lax.ppermute(value, axis, [(i, i ^ 1) for i in range(size)])]
  transfers between devices with their start and end apart: 4 -> 5, of which waited for: 4 -> 4; matrix products, arithmetic and copies ran while one was open for 18% -> 28% of each run, Pallas kernels for 9% -> 9%
where the time goes in v12:
time: 61.4 us; the launch traced here: 60.2 us
  matrix products  22.9 us (37%)
  starting transfers between devices  14.6 us (24%)
  local copies, waits for them, and re-layouts  13 us (21%)
  Pallas kernels  5.57 us (9%)
  waiting for transfers between devices  2.26 us (4%)
  other arithmetic  1.71 us (3%)
    slice x1, local copies, waits for them, and re-layouts, shards(): late_inverse[:half]  10.2 us
    dot_general x1, matrix products, shards(): jnp.einsum('tkb,tbc->tkc', sources, coupling, preferred_element_type=jnp....  9.07 us
    all_to_all x1, starting transfers between devices, shards(): lax.all_to_all(product_buffer.reshape(regions, CAP, vectors, padded), 'do...  8.17 us
    pallas_call x1, Pallas kernels, resident(): pl.pallas_call(kernel, in_specs=[pl.BlockSpec(memory_space=pl.ANY)], out_...  5.57 us
    dot_general x1, matrix products, shards(): jnp.einsum('ekb,ebc->ekc', residual_in, block_inverse, preferred_element_...  5.17 us
    dot_general x1, matrix products, shards(): jnp.einsum('ebc,ecm->ebm', late_inverse, interface_basis, preferred_eleme...  5.04 us
    ppermute x1, starting transfers between devices, group_sum(): far = lax.ppermute(right, axis, [(i, (i - 2) % size) for i in range(size)])  3.51 us
    ppermute x1, starting transfers between devices, group_sum(): lax.ppermute(value, axis, [(i, (i - 2) % size) for i in range(size)])  2.75 us
  transfers between devices with their start and end apart: 5, of which 4 were waited for; matrix products, arithmetic and copies ran while one was open for 28% of the time, Pallas kernels for 9%

profile of v12, /device:TPU:0, one launch (start us, length us, event | category | flops | bytes accessed | tf_op | source)
XLA Modules:
  0.0 60.2 jit_solution(15407992362064565757)
XLA Ops:
  0.0 0.0 copy-start
  0.0 0.8 %pad_add_fusion = s32[48]{0:T(128)S(1)} fusion(s32[16]{0:T(128)} %param.13, s32[16]{0:T(128)} %param.12, s32[16]{0:T(128)} %bitcast.48), kind=kLoop, calls=%fused_computation.57 | loop fusion | flops 96 | bytes 384 | tf_op jit(solution)/shard_map/concatenate | solution.py:71
  0.8 0.2 convert_reduce_fusion.1
  1.0 0.1 multiply_add_fusion
  1.1 0.1 fusion.43
  1.2 0.1 select_reduce_fusion
  1.3 0.1 slice.29
  1.4 5.2 %fusion.26 = bf16[8,32,625]{2,1,0:T(8,128)(2,1)S(1)} fusion(bf16[8,32,625]{2,1,0:T(8,128)(2,1)} %param.8, bf16[8,625,625]{2,0,1:T(8,128)(2,1)} %param.9), kind=kOutput, calls=%fused_computation.22 | convolution fusion | flops 200160000 | bytes 6890000 | tf_op jit(solution)/shard_map/ekb,ebc->ekc/dot_general | solution.py:67
  6.6 0.7 %gather_fusion = bf16[16,32,625]{2,1,0:T(8,128)(2,1)S(1)} fusion(bf16[8,32,625]{2,1,0:T(8,128)(2,1)S(1)} %fusion.26, s32[1024]{0:T(1024)S(1)} %pad_clamp_fusion.1), kind=kCustom, calls=%fused_computation | custom fusion | bytes 1280064 | tf_op jit(solution)/shard_map/gather | solution.py:85
  7.2 9.1 %fusion.11 = bf16[16,32,625]{2,1,0:T(8,128)(2,1)S(1)} fusion(bf16[16,32,625]{2,1,0:T(8,128)(2,1)S(1)} %gather_fusion, bf16[16,625,625]{2,0,1:T(8,128)(2,1)} %param.10), kind=kOutput, calls=%fused_computation.14 | convolution fusion | flops 400320000 | bytes 13780000 | tf_op jit(solution)/shard_map/tkb,tbc->tkc/dot_general | solution.py:86
  16.3 0.1 pad_maximum_fusion.1
  16.4 0.1 and_select_fusion
  16.5 0.1 fusion.30
  16.6 1.8 %gather_fusion.1 = bf16[32,32,640]{2,1,0:T(8,128)(2,1)} fusion(bf16[17,32,640]{2,1,0:T(8,128)(2,1)S(1)} %fusion.30, s32[1024]{0:T(1024)S(1)} %pad_clamp_fusion), kind=kCustom, calls=%fused_computation.1 | custom fusion | bytes 2621568 | tf_op jit(solution)/shard_map/gather | solution.py:97
  18.4 8.2 %all-to-all-start = ((bf16[16,2,32,640]{3,2,1,0:T(8,128)(2,1)}), bf16[16,2,32,640]{3,2,1,0:T(8,128)(2,1)S(1)}, u32[]{:S(2)}, u32[]{:S(2)}) async-start(bf16[16,2,32,640]{3,2,1,0:T(8,128)(2,1)} %bitcast.3), calls=%async_computation | async-start | bytes 2621440 | tf_op jit(solution)/shard_map/all_to_all | solution.py:98
  26.6 5.6 %shard_map.82 = bf16[625,8,625]{2,1,0:T(8,128)(2,1)} custom-call(bf16[625,8,625]{2,1,0:T(8,128)(2,1)} %bitcast.40), custom_call_target="tpu_custom_call" | custom-call | tf_op jit(solution)/shard_map/pallas_call | solution.py:18
  32.2 0.0 copy-done
  32.2 5.0 %fusion.14 = bf16[8,625,64]{1,2,0:T(8,128)(2,1)S(1)} fusion(bf16[8,625,64]{1,2,0:T(8,128)(2,1)S(1)} %copy-done, bf16[8,625,625]{2,0,1:T(8,128)(2,1)} %bitcast.38), kind=kOutput, calls=%fused_computation.15 | convolution fusion | flops 400320000 | bytes 7530000 | tf_op jit(solution)/shard_map/ebc,ecm->ebm/dot_general | solution.py:115
  37.3 0.0 copy-start.3
  37.3 10.2 %fusion.50 = (bf16[4,625,625]{2,0,1:T(4,128)(2,1)}, bf16[4,625,625]{2,0,1:T(4,128)(2,1)}) fusion(bf16[8,625,625]{2,0,1:T(8,128)(2,1)} %bitcast.39), kind=kLoop, calls=%fused_computation.62 | loop fusion | bytes 12500000 | tf_op jit(solution)/shard_map/slice | solution.py:131
  47.5 0.0 all-to-all-done
  47.5 0.0 copy-start.2
  47.6 0.1 slice.41
  47.6 0.1 convert_reduce_fusion
  47.8 0.0 copy-done.3
  47.8 0.5 fusion.23
  48.3 0.3 convolution_bitcast_fusion.1
  48.6 0.0 copy-start.1
  48.6 0.1 collective-permute-start
  48.6 0.1 fusion.51
  48.8 1.1 %collective-permute-done = f32[32,64]{1,0:T(8,128)S(1)} collective-permute-done((f32[32,64]{1,0:T(8,128)S(1)}, f32[32,64]{1,0:T(8,128)S(1)}, u32[]{:S(2)}, u32[]{:S(2)}) %collective-permute-start) | collective-permute-done | bytes 8224 | tf_op jit(solution)/shard_map/ppermute | solution.py:34
  49.8 2.8 %collective-permute-start.1 = (f32[32,64]{1,0:T(8,128)S(1)}, f32[32,64]{1,0:T(8,128)S(1)}, u32[]{:S(2)}, u32[]{:S(2)}) collective-permute-start(f32[32,64]{1,0:T(8,128)S(1)} %add.71), channel_id=1, source_target_pairs={{0,6},{1,7},{2,0},{3,1},{4,2},{5,3},{6,4},{7,5},{8,14},{9,15},{10,... | collective-permute-start | bytes 24584 | tf_op jit(solution)/shard_map/ppermute | solution.py:36
  52.6 0.0 copy-done.2
  52.6 0.8 %fusion.6 = f32[4,32,625]{2,1,0:T(8,128)S(1)} fusion(bf16[4,625,625]{2,0,1:T(4,128)(2,1)S(1)} %copy-done.2, bf16[4,32,625]{2,0,1:T(4,128)(2,1)S(1)} %get-tuple-element.8), kind=kOutput, calls=%fused_computation.8 | convolution fusion | flops 100000000 | bytes 3605000 | tf_op jit(solution)/shard_map/ekb,ebc->ekc/dot_general | solution.py:134
  53.4 0.0 copy-start.4
  53.4 0.1 collective-permute-start.3
  53.4 0.6 collective-permute-done.1
  54.0 3.5 %collective-permute-start.2 = (f32[32,64]{1,0:T(8,128)S(1)}, f32[32,64]{1,0:T(8,128)S(1)}, u32[]{:S(2)}, u32[]{:S(2)}) collective-permute-start(f32[32,64]{1,0:T(8,128)S(1)} %collective-permute-done.1), channel_id=1, source_target_pairs={{0,6},{1,7},{2,0},{3,1},{4,2},{5,3},{6,4},{7,5},{8,14},{9,15},{10,... | collective-permute-start | bytes 24584 | tf_op jit(solution)/shard_map/ppermute | solution.py:37
  57.5 0.0 copy-done.1
  57.5 0.8 %fusion.8 = f32[4,32,625]{2,1,0:T(8,128)S(1)} fusion(bf16[4,625,625]{2,0,1:T(4,128)(2,1)S(1)} %copy-done.1, bf16[4,32,625]{2,0,1:T(4,128)(2,1)S(1)} %get-tuple-element.7), kind=kOutput, calls=%fused_computation.10 | convolution fusion | flops 100000000 | bytes 3605000 | tf_op jit(solution)/shard_map/ekb,ebc->ekc/dot_general | solution.py:128
  58.3 0.1 collective-permute-done.3
  58.4 0.6 collective-permute-done.2
  59.0 0.0 copy-done.4
  59.0 0.2 fusion.29
  59.1 1.1 %fusion.22 = f32[8,32,625]{2,1,0:T(8,128)} fusion(bf16[32,64,1]{1,0,2:T(8,128)(2,1)S(1)} %fusion.29, bf16[8,625,64]{1,2,0:T(8,128)(2,1)S(1)} %copy-done, f32[4,32,625]{2,1,0:T(8,128)S(1)} %fusion.6, f32[4,32,625]{2,1,0:T(8,128)S(1)} %fusion.8), kind=kOutput, calls=%fused_computation.20 | convolution fusion | flops 20800000 | bytes 1924096 | tf_op jit(solution)/shard_map/km,ebm->ekb/dot_general | solution.py:149
  (8 shorter events, 0.0 us)
Async XLA Ops:
  0.0 32.2 %copy-start = (bf16[8,625,64]{1,2,0:T(8,128)(2,1)S(1)}, bf16[8,625,64]{1,2,0:T(8,128)(2,1)}, u32[]{:S(2)}) copy-start(bf16[8,625,64]{1,2,0:T(8,128)(2,1)} %param.14) | copy-start | bytes 1920004
  18.4 29.2 %all-to-all-start = ((bf16[16,2,32,640]{3,2,1,0:T(8,128)(2,1)}), bf16[16,2,32,640]{3,2,1,0:T(8,128)(2,1)S(1)}, u32[]{:S(2)}, u32[]{:S(2)}) async-start(bf16[16,2,32,640]{3,2,1,0:T(8,128)(2,1)} %bitcast.3), calls=%async_computation | async-start | bytes 2621440 | tf_op jit(solution)/shard_map/all_to_all | solution.py:98
  37.3 10.5 %copy-start.3 = (bf16[8,32,625]{2,1,0:T(8,128)(2,1)S(1)}, bf16[8,32,625]{2,1,0:T(8,128)(2,1)}, u32[]{:S(2)}) copy-start(bf16[8,32,625]{2,1,0:T(8,128)(2,1)} %param.8) | copy-start | bytes 960004
  47.5 5.0 %copy-start.2 = (bf16[4,625,625]{2,0,1:T(4,128)(2,1)S(1)}, bf16[4,625,625]{2,0,1:T(4,128)(2,1)}, u32[]{:S(2)}) copy-start(bf16[4,625,625]{2,0,1:T(4,128)(2,1)} %get-tuple-element.6) | copy-start | bytes 9375004
  48.6 9.0 %copy-start.1 = (bf16[4,625,625]{2,0,1:T(4,128)(2,1)S(1)}, bf16[4,625,625]{2,0,1:T(4,128)(2,1)}, u32[]{:S(2)}) copy-start(bf16[4,625,625]{2,0,1:T(4,128)(2,1)} %get-tuple-element.5) | copy-start | bytes 9375004
  48.6 1.2 %collective-permute-start = (f32[32,64]{1,0:T(8,128)S(1)}, f32[32,64]{1,0:T(8,128)S(1)}, u32[]{:S(2)}, u32[]{:S(2)}) collective-permute-start(f32[32,64]{1,0:T(8,128)S(1)} %convolution_bitcast_fusion.1), channel_id=1, source_target_pairs={{0,1},{1,0},{2,3},{3,2},{4,5},{5,4},{6,7},{7,6},{8,9},{9,8},{10,11... | collective-permute-start | bytes 24584 | tf_op jit(solution)/shard_map/ppermute | solution.py:34
  49.8 4.2 %collective-permute-start.1 = (f32[32,64]{1,0:T(8,128)S(1)}, f32[32,64]{1,0:T(8,128)S(1)}, u32[]{:S(2)}, u32[]{:S(2)}) collective-permute-start(f32[32,64]{1,0:T(8,128)S(1)} %add.71), channel_id=1, source_target_pairs={{0,6},{1,7},{2,0},{3,1},{4,2},{5,3},{6,4},{7,5},{8,14},{9,15},{10,... | collective-permute-start | bytes 24584 | tf_op jit(solution)/shard_map/ppermute | solution.py:36
  53.4 5.6 %copy-start.4 = (f32[1,64,64]{2,1,0:T(8,128)S(1)}, f32[1,64,64]{2,1,0:T(8,128)}, u32[]{:S(2)}) copy-start(f32[1,64,64]{2,1,0:T(8,128)} %param.15) | copy-start | bytes 49156
  53.4 5.0 %collective-permute-start.3 = (f32[32,64]{1,0:T(8,128)S(1)}, f32[32,64]{1,0:T(8,128)S(1)}, u32[]{:S(2)}, u32[]{:S(2)}) collective-permute-start(f32[32,64]{1,0:T(8,128)S(1)} %add.71), channel_id=1, source_target_pairs={{0,2},{1,3},{2,4},{3,5},{4,6},{5,7},{6,0},{7,1},{8,10},{9,11},{10,... | collective-permute-start | bytes 24584 | tf_op jit(solution)/shard_map/ppermute | solution.py:35
  54.0 4.9 %collective-permute-start.2 = (f32[32,64]{1,0:T(8,128)S(1)}, f32[32,64]{1,0:T(8,128)S(1)}, u32[]{:S(2)}, u32[]{:S(2)}) collective-permute-start(f32[32,64]{1,0:T(8,128)S(1)} %collective-permute-done.1), channel_id=1, source_target_pairs={{0,6},{1,7},{2,0},{3,1},{4,2},{5,3},{6,4},{7,5},{8,14},{9,15},{10,... | collective-permute-start | bytes 24584 | tf_op jit(solution)/shard_map/ppermute | solution.py:37

commit v13 on v10

--- a/solution.py
+++ b/solution.py
@@ -72,7 +72,12 @@
     slot_tile = jnp.where(
         jnp.any(hit, axis=1), jnp.sum(jnp.where(hit, order[None, :], 0), axis=1), tiles
     ).astype(jnp.int32)
-    sources = initial[tile_source]
+    picks = (tile_source[:, None] == jnp.arange(elements, dtype=jnp.int32)[None, :]).astype(
+        jnp.bfloat16
+    )
+    sources = jnp.einsum(
+        "te,ekb->tkb", picks, initial, preferred_element_type=jnp.float32
+    ).astype(jnp.bfloat16)
     local_products = jnp.einsum(
         "tkb,tbc->tkc", sources, coupling, preferred_element_type=jnp.float32
     ).astype(jnp.bfloat16)

time: 60.2 us -> 60.1 us (level)
  local copies, waits for them, and re-layouts: 6.79 us -> 6.12 us
    gather x1 -> x0, local copies, waits for them, and re-layouts: 0.67 us -> none  [shards(): sources = initial[tile_source]]
where the time goes in v13:
time: 60.1 us; the launch traced here: 59.8 us
  matrix products  23.6 us (39%)
  starting transfers between devices  12.7 us (21%)
  waiting for transfers between devices  10 us (17%)
  local copies, waits for them, and re-layouts  6.12 us (10%)
  Pallas kernels  5.48 us (9%)
  other arithmetic  1.69 us (3%)
    dot_general x1, matrix products, shards(): jnp.einsum('tkb,tbc->tkc', sources, coupling, preferred_element_type=jnp....  9.23 us
    all_to_all x1, starting transfers between devices, shards(): lax.all_to_all(product_buffer.reshape(regions, CAP, vectors, padded), 'do...  8.17 us
    all_to_all x1, waiting for transfers between devices, shards(): lax.all_to_all(product_buffer.reshape(regions, CAP, vectors, padded), 'do...  6.1 us
    pallas_call x1, Pallas kernels, resident(): pl.pallas_call(kernel, in_specs=[pl.BlockSpec(memory_space=pl.ANY)], out_...  5.48 us
    dot_general x1, matrix products, shards(): jnp.einsum('ebc,ecm->ebm', late_inverse, interface_basis, preferred_eleme...  5.22 us
    dot_general x1, matrix products, shards(): jnp.einsum('ekb,ebc->ekc', residual_in, block_inverse, preferred_element_...  5.17 us
    ppermute x3, starting transfers between devices, group_sum(): value = value + lax.ppermute(value, axis, pairs)  4.58 us
    slice x1, local copies, waits for them, and re-layouts, shards(): late_inverse[:half]  4.07 us
  transfers between devices with their start and end apart: 4, of which 4 were waited for; matrix products, arithmetic and copies ran while one was open for 18% of the time, Pallas kernels for 9%

profile of v13, /device:TPU:0, one launch (start us, length us, event | category | flops | bytes accessed | tf_op | source)
XLA Modules:
  0.0 59.8 jit_solution(6042491499415109846)
XLA Ops:
  0.0 0.0 copy-start
  0.0 0.8 %pad_add_fusion = s32[48]{0:T(128)S(1)} fusion(s32[16]{0:T(128)} %param.13, s32[16]{0:T(128)} %param.12, s32[16]{0:T(128)} %bitcast.39), kind=kLoop, calls=%fused_computation.51 | loop fusion | flops 96 | bytes 384 | tf_op jit(solution)/shard_map/concatenate | solution.py:61
  0.8 0.2 convert_reduce_fusion.1
  1.0 0.1 multiply_add_fusion
  1.1 0.1 fusion.38
  1.2 0.1 select_reduce_fusion
  1.3 0.1 slice.29
  1.4 5.2 %fusion.26 = bf16[8,32,625]{2,1,0:T(8,128)(2,1)S(1)} fusion(bf16[8,32,625]{2,1,0:T(8,128)(2,1)} %param.8, bf16[8,625,625]{2,0,1:T(8,128)(2,1)} %param.9), kind=kOutput, calls=%fused_computation.22 | convolution fusion | flops 200160000 | bytes 6890000 | tf_op jit(solution)/shard_map/ekb,ebc->ekc/dot_general | solution.py:57
  6.5 0.4 convolution_convert_fusion
  6.9 9.2 %fusion.11 = bf16[16,32,625]{2,1,0:T(8,128)(2,1)S(1)} fusion(bf16[16,625,625]{2,0,1:T(8,128)(2,1)} %param.10, bf16[16,32,625]{2,0,1:T(8,128)(2,1)S(1)} %convolution_convert_fusion), kind=kOutput, calls=%fused_computation.13 | convolution fusion | flops 400320000 | bytes 13780000 | tf_op jit(solution)/shard_map/tkb,tbc->tkc/dot_general | solution.py:81
  16.2 0.1 pad_maximum_fusion
  16.3 0.1 and_select_fusion
  16.4 0.1 fusion.30
  16.5 1.8 %gather_fusion = bf16[32,32,640]{2,1,0:T(8,128)(2,1)} fusion(bf16[17,32,640]{2,1,0:T(8,128)(2,1)S(1)} %fusion.30, s32[1024]{0:T(1024)S(1)} %pad_clamp_fusion), kind=kCustom, calls=%fused_computation | custom fusion | bytes 2621568 | tf_op jit(solution)/shard_map/gather | solution.py:92
  18.2 8.2 %all-to-all-start = ((bf16[16,2,32,640]{3,2,1,0:T(8,128)(2,1)}), bf16[16,2,32,640]{3,2,1,0:T(8,128)(2,1)S(1)}, u32[]{:S(2)}, u32[]{:S(2)}) async-start(bf16[16,2,32,640]{3,2,1,0:T(8,128)(2,1)} %bitcast.4), calls=%async_computation | async-start | bytes 2621440 | tf_op jit(solution)/shard_map/all_to_all | solution.py:93
  26.4 5.5 %shard_map.82 = bf16[625,8,625]{2,1,0:T(8,128)(2,1)} custom-call(bf16[625,8,625]{2,1,0:T(8,128)(2,1)} %bitcast.35), custom_call_target="tpu_custom_call" | custom-call | tf_op jit(solution)/shard_map/pallas_call | solution.py:18
  31.9 0.0 copy-done
  31.9 0.0 copy-start.1
  31.9 5.2 %fusion.14 = bf16[8,625,64]{1,2,0:T(8,128)(2,1)S(1)} fusion(bf16[8,625,64]{1,2,0:T(8,128)(2,1)S(1)} %copy-done, bf16[8,625,625]{2,0,1:T(8,128)(2,1)} %bitcast.33), kind=kOutput, calls=%fused_computation.15 | convolution fusion | flops 400320000 | bytes 7530000 | tf_op jit(solution)/shard_map/ebc,ecm->ebm/dot_general | solution.py:110
  37.2 0.0 copy-done.1
  37.2 0.0 copy-start.4
  37.2 4.1 %fusion.47 = (bf16[4,625,625]{2,0,1:T(4,128)(2,1)}, bf16[4,625,625]{2,0,1:T(4,128)(2,1)}) fusion(bf16[8,625,625]{2,0,1:T(8,128)(2,1)S(1)} %bitcast.34), kind=kLoop, calls=%fused_computation.56 | loop fusion | bytes 12500000 | tf_op jit(solution)/shard_map/slice | solution.py:126
  41.2 6.1 %all-to-all-done = bf16[16,2,32,640]{3,2,1,0:T(8,128)(2,1)S(1)} async-done(((bf16[16,2,32,640]{3,2,1,0:T(8,128)(2,1)}), bf16[16,2,32,640]{3,2,1,0:T(8,128)(2,1)S(1)}, u32[]{:S(2)}, u32[]{:S(2)}) %all-to-all-start) | async-done | bytes 1310752 | tf_op jit(solution)/shard_map/all_to_all | solution.py:93
  47.4 0.0 copy-start.3
  47.4 0.1 slice.39
  47.4 0.1 convert_reduce_fusion
  47.6 0.0 copy-done.4
  47.6 0.5 fusion.23
  48.1 0.3 convolution_bitcast_fusion.1
  48.4 0.0 copy-start.2
  48.4 0.1 collective-permute-start
  48.4 0.1 fusion.48
  48.6 1.1 %collective-permute-done = f32[32,64]{1,0:T(8,128)S(1)} collective-permute-done((f32[32,64]{1,0:T(8,128)S(1)}, f32[32,64]{1,0:T(8,128)S(1)}, u32[]{:S(2)}, u32[]{:S(2)}) %collective-permute-start) | collective-permute-done | bytes 8224 | tf_op jit(solution)/shard_map/ppermute | solution.py:35
  49.6 1.5 %collective-permute-start.1 = (f32[32,64]{1,0:T(8,128)S(1)}, f32[32,64]{1,0:T(8,128)S(1)}, u32[]{:S(2)}, u32[]{:S(2)}) collective-permute-start(f32[32,64]{1,0:T(8,128)S(1)} %add.33), channel_id=1, source_target_pairs={{0,2},{1,3},{2,0},{3,1},{4,6},{5,7},{6,4},{7,5},{8,10},{9,11},{10,... | collective-permute-start | bytes 24584 | tf_op jit(solution)/shard_map/ppermute | solution.py:35
  51.1 0.0 copy-done.3
  51.1 0.8 %fusion.6 = f32[4,32,625]{2,1,0:T(8,128)S(1)} fusion(bf16[4,625,625]{2,0,1:T(4,128)(2,1)S(1)} %copy-done.3, bf16[4,32,625]{2,0,1:T(4,128)(2,1)S(1)} %get-tuple-element.8), kind=kOutput, calls=%fused_computation.7 | convolution fusion | flops 100000000 | bytes 3605000 | tf_op jit(solution)/shard_map/ekb,ebc->ekc/dot_general | solution.py:129
  51.9 0.0 copy-start.5
  51.9 1.4 %collective-permute-done.1 = f32[32,64]{1,0:T(8,128)S(1)} collective-permute-done((f32[32,64]{1,0:T(8,128)S(1)}, f32[32,64]{1,0:T(8,128)S(1)}, u32[]{:S(2)}, u32[]{:S(2)}) %collective-permute-start.1) | collective-permute-done | bytes 8224 | tf_op jit(solution)/shard_map/ppermute | solution.py:35
  53.4 3.0 %collective-permute-start.2 = (f32[32,64]{1,0:T(8,128)S(1)}, f32[32,64]{1,0:T(8,128)S(1)}, u32[]{:S(2)}, u32[]{:S(2)}) collective-permute-start(f32[32,64]{1,0:T(8,128)S(1)} %add.34), channel_id=1, source_target_pairs={{0,4},{1,5},{2,6},{3,7},{4,0},{5,1},{6,2},{7,3},{8,12},{9,13},{10,... | collective-permute-start | bytes 24584 | tf_op jit(solution)/shard_map/ppermute | solution.py:35
  56.4 0.0 copy-done.2
  56.4 0.8 %fusion.8 = f32[4,32,625]{2,1,0:T(8,128)S(1)} fusion(bf16[4,625,625]{2,0,1:T(4,128)(2,1)S(1)} %copy-done.2, bf16[4,32,625]{2,0,1:T(4,128)(2,1)S(1)} %get-tuple-element.7), kind=kOutput, calls=%fused_computation.9 | convolution fusion | flops 100000000 | bytes 3605000 | tf_op jit(solution)/shard_map/ekb,ebc->ekc/dot_general | solution.py:123
  57.2 1.4 %collective-permute-done.2 = f32[32,64]{1,0:T(8,128)S(1)} collective-permute-done((f32[32,64]{1,0:T(8,128)S(1)}, f32[32,64]{1,0:T(8,128)S(1)}, u32[]{:S(2)}, u32[]{:S(2)}) %collective-permute-start.2) | collective-permute-done | bytes 8224 | tf_op jit(solution)/shard_map/ppermute | solution.py:35
  58.6 0.0 copy-done.5
  58.6 0.1 fusion.29
  58.8 1.1 %fusion.22 = f32[8,32,625]{2,1,0:T(8,128)} fusion(bf16[32,64,1]{1,0,2:T(8,128)(2,1)S(1)} %fusion.29, bf16[8,625,64]{1,2,0:T(8,128)(2,1)S(1)} %copy-done, f32[4,32,625]{2,1,0:T(8,128)S(1)} %fusion.6, f32[4,32,625]{2,1,0:T(8,128)S(1)} %fusion.8), kind=kOutput, calls=%fused_computation.20 | convolution fusion | flops 20800000 | bytes 1924096 | tf_op jit(solution)/shard_map/km,ebm->ekb/dot_general | solution.py:144
  (7 shorter events, 0.0 us)
Async XLA Ops:
  0.0 31.9 %copy-start = (bf16[8,625,64]{1,2,0:T(8,128)(2,1)S(1)}, bf16[8,625,64]{1,2,0:T(8,128)(2,1)}, u32[]{:S(2)}) copy-start(bf16[8,625,64]{1,2,0:T(8,128)(2,1)} %param.14) | copy-start | bytes 1920004
  18.2 29.1 %all-to-all-start = ((bf16[16,2,32,640]{3,2,1,0:T(8,128)(2,1)}), bf16[16,2,32,640]{3,2,1,0:T(8,128)(2,1)S(1)}, u32[]{:S(2)}, u32[]{:S(2)}) async-start(bf16[16,2,32,640]{3,2,1,0:T(8,128)(2,1)} %bitcast.4), calls=%async_computation | async-start | bytes 2621440 | tf_op jit(solution)/shard_map/all_to_all | solution.py:93
  31.9 5.2 %copy-start.1 = (bf16[625,8,625]{2,1,0:T(8,128)(2,1)S(1)}, bf16[625,8,625]{2,1,0:T(8,128)(2,1)}, u32[]{:S(2)}) copy-start(bf16[625,8,625]{2,1,0:T(8,128)(2,1)} %shard_map.82) | copy-start | bytes 18750004
  37.2 10.4 %copy-start.4 = (bf16[8,32,625]{2,1,0:T(8,128)(2,1)S(1)}, bf16[8,32,625]{2,1,0:T(8,128)(2,1)}, u32[]{:S(2)}) copy-start(bf16[8,32,625]{2,1,0:T(8,128)(2,1)} %param.8) | copy-start | bytes 960004
  47.4 3.8 %copy-start.3 = (bf16[4,625,625]{2,0,1:T(4,128)(2,1)S(1)}, bf16[4,625,625]{2,0,1:T(4,128)(2,1)}, u32[]{:S(2)}) copy-start(bf16[4,625,625]{2,0,1:T(4,128)(2,1)} %get-tuple-element.6) | copy-start | bytes 9375004
  48.4 8.0 %copy-start.2 = (bf16[4,625,625]{2,0,1:T(4,128)(2,1)S(1)}, bf16[4,625,625]{2,0,1:T(4,128)(2,1)}, u32[]{:S(2)}) copy-start(bf16[4,625,625]{2,0,1:T(4,128)(2,1)} %get-tuple-element.5) | copy-start | bytes 9375004
  48.4 1.2 %collective-permute-start = (f32[32,64]{1,0:T(8,128)S(1)}, f32[32,64]{1,0:T(8,128)S(1)}, u32[]{:S(2)}, u32[]{:S(2)}) collective-permute-start(f32[32,64]{1,0:T(8,128)S(1)} %convolution_bitcast_fusion.1), channel_id=1, source_target_pairs={{0,1},{1,0},{2,3},{3,2},{4,5},{5,4},{6,7},{7,6},{8,9},{9,8},{10,11... | collective-permute-start | bytes 24584 | tf_op jit(solution)/shard_map/ppermute | solution.py:35
  49.6 3.7 %collective-permute-start.1 = (f32[32,64]{1,0:T(8,128)S(1)}, f32[32,64]{1,0:T(8,128)S(1)}, u32[]{:S(2)}, u32[]{:S(2)}) collective-permute-start(f32[32,64]{1,0:T(8,128)S(1)} %add.33), channel_id=1, source_target_pairs={{0,2},{1,3},{2,0},{3,1},{4,6},{5,7},{6,4},{7,5},{8,10},{9,11},{10,... | collective-permute-start | bytes 24584 | tf_op jit(solution)/shard_map/ppermute | solution.py:35
  51.9 6.7 %copy-start.5 = (f32[1,64,64]{2,1,0:T(8,128)S(1)}, f32[1,64,64]{2,1,0:T(8,128)}, u32[]{:S(2)}) copy-start(f32[1,64,64]{2,1,0:T(8,128)} %param.15) | copy-start | bytes 49156
  53.4 5.2 %collective-permute-start.2 = (f32[32,64]{1,0:T(8,128)S(1)}, f32[32,64]{1,0:T(8,128)S(1)}, u32[]{:S(2)}, u32[]{:S(2)}) collective-permute-start(f32[32,64]{1,0:T(8,128)S(1)} %add.34), channel_id=1, source_target_pairs={{0,4},{1,5},{2,6},{3,7},{4,0},{5,1},{6,2},{7,3},{8,12},{9,13},{10,... | collective-permute-start | bytes 24584 | tf_op jit(solution)/shard_map/ppermute | solution.py:35

commit v14 on v13

--- a/solution.py
+++ b/solution.py
@@ -89,7 +89,12 @@
         [local_products, jnp.zeros((1, vectors, width), jnp.bfloat16)], axis=0
     )
     extended = jnp.concatenate([body, tail], axis=2)
-    product_buffer = extended[slot_tile]
+    slot_picks = (
+        slot_tile[:, None] == jnp.arange(tiles + 1, dtype=jnp.int32)[None, :]
+    ).astype(jnp.bfloat16)
+    product_buffer = jnp.einsum(
+        "st,tkc->skc", slot_picks, extended, preferred_element_type=jnp.float32
+    ).astype(jnp.bfloat16)
     received = lax.all_to_all(
         product_buffer.reshape(regions, CAP, vectors, padded),
         "dom",

time: 60.1 us -> 65.3 us (1.087)
  matrix products: 23.6 us -> 27 us
  local copies, waits for them, and re-layouts: 6.12 us -> 8.56 us
  waiting for transfers between devices: 10 us -> 9.23 us
    reshape x0 -> x3, local copies, waits for them, and re-layouts: none -> 3.41 us  [the longest x2 2.87 us: shards(): product_buffer.reshape(regions, CAP, vectors, padded)]
    gather x1 -> x0, local copies, waits for them, and re-layouts: 1.76 us -> none  [shards(): product_buffer = extended[slot_tile]]
    dot_general x1, matrix products: 0.29 us -> 1.37 us  [shards(): jnp.einsum('ekb,ebm->km', corrected_in, lax.optimization_barrier(projecte...]
    dot_general x1, matrix products: 0.5 us -> 1.42 us  [shards(): jnp.einsum('es,skc->ekc', selector, products, preferred_element_type=jnp....]
    all_to_all x0 -> x1, local copies, waits for them, and re-layouts: none -> 0.9 us  [shards(): lax.all_to_all(product_buffer.reshape(regions, CAP, vectors, padded), 'do...]
    dot_general x1, matrix products: 5.22 us -> 6.05 us  [shards(): jnp.einsum('ebc,ecm->ebm', late_inverse, interface_basis, preferred_eleme...]
    all_to_all x1, waiting for transfers between devices: 6.1 us -> 5.3 us  [shards(): lax.all_to_all(product_buffer.reshape(regions, CAP, vectors, padded), 'do...]
  transfers between devices with their start and end apart: 4 -> 4, of which waited for: 4 -> 4; matrix products, arithmetic and copies ran while one was open for 18% -> 18% of each run, Pallas kernels for 9% -> 8%
where the time goes in v14:
time: 65.3 us; the launch traced here: 65 us
  matrix products  27 us (41%)
  starting transfers between devices  12.8 us (20%)
  waiting for transfers between devices  9.23 us (14%)
  local copies, waits for them, and re-layouts  8.56 us (13%)
  Pallas kernels  5.48 us (8%)
  other arithmetic  1.75 us (3%)
    dot_general x1, matrix products, shards(): jnp.einsum('tkb,tbc->tkc', sources, coupling, preferred_element_type=jnp....  9.23 us
    all_to_all x1, starting transfers between devices, shards(): lax.all_to_all(product_buffer.reshape(regions, CAP, vectors, padded), 'do...  8.17 us
    dot_general x1, matrix products, shards(): jnp.einsum('ebc,ecm->ebm', late_inverse, interface_basis, preferred_eleme...  6.05 us
    pallas_call x1, Pallas kernels, resident(): pl.pallas_call(kernel, in_specs=[pl.BlockSpec(memory_space=pl.ANY)], out_...  5.48 us
    all_to_all x1, waiting for transfers between devices, shards(): lax.all_to_all(product_buffer.reshape(regions, CAP, vectors, padded), 'do...  5.3 us
    dot_general x1, matrix products, shards(): jnp.einsum('ekb,ebc->ekc', residual_in, block_inverse, preferred_element_...  5.17 us
    ppermute x3, starting transfers between devices, group_sum(): value = value + lax.ppermute(value, axis, pairs)  4.6 us
    slice x1, local copies, waits for them, and re-layouts, shards(): late_inverse[:half]  4.05 us
  transfers between devices with their start and end apart: 4, of which 4 were waited for; matrix products, arithmetic and copies ran while one was open for 18% of the time, Pallas kernels for 8%

profile of v14, /device:TPU:0, one launch (start us, length us, event | category | flops | bytes accessed | tf_op | source)
XLA Modules:
  0.0 65.0 jit_solution(3017423487175390351)
XLA Ops:
  0.0 0.0 copy-start
  0.0 0.8 %pad_add_fusion = s32[48]{0:T(128)S(1)} fusion(s32[16]{0:T(128)} %param.13, s32[16]{0:T(128)} %param.12, s32[16]{0:T(128)} %bitcast.37), kind=kLoop, calls=%fused_computation.52 | loop fusion | flops 96 | bytes 384 | tf_op jit(solution)/shard_map/concatenate | solution.py:61
  0.8 0.2 convert_reduce_fusion.1
  1.0 0.1 multiply_add_fusion
  1.1 0.1 fusion.41
  1.2 0.1 select_reduce_fusion
  1.3 0.1 slice.30
  1.4 5.2 %fusion.26 = bf16[8,32,625]{2,1,0:T(8,128)(2,1)S(1)} fusion(bf16[8,32,625]{2,1,0:T(8,128)(2,1)} %param.8, bf16[8,625,625]{2,0,1:T(8,128)(2,1)} %param.9), kind=kOutput, calls=%fused_computation.22 | convolution fusion | flops 200160000 | bytes 6890000 | tf_op jit(solution)/shard_map/ekb,ebc->ekc/dot_general | solution.py:57
  6.5 0.4 convolution_convert_fusion.1
  6.9 9.2 %fusion.11 = bf16[16,32,625]{2,1,0:T(8,128)(2,1)S(1)} fusion(bf16[16,625,625]{2,0,1:T(8,128)(2,1)} %param.10, bf16[16,32,625]{2,0,1:T(8,128)(2,1)S(1)} %convolution_convert_fusion.1), kind=kOutput, calls=%fused_computation.13 | convolution fusion | flops 400320000 | bytes 13780000 | tf_op jit(solution)/shard_map/tkb,tbc->tkc/dot_general | solution.py:81
  16.2 0.1 pad_maximum_fusion
  16.3 0.1 and_select_fusion
  16.4 0.1 fusion.31
  16.5 0.6 convolution_convert_fusion
  17.1 0.5 reshape.36
  17.6 2.3 %copy.41 = bf16[16,2,32,640]{3,1,2,0:T(2,128)(2,1)} copy(bf16[16,2,32,640]{3,1,0,2:T(2,128)(2,1)S(1)} %reshape.36) | data formatting | bytes 2621440 | tf_op jit(solution)/shard_map/reshape | solution.py:99
  19.9 8.2 %all-to-all-start = ((bf16[16,2,32,640]{3,1,2,0:T(2,128)(2,1)}), bf16[16,2,32,640]{3,1,2,0:T(2,128)(2,1)S(1)}, u32[]{:S(2)}, u32[]{:S(2)}) async-start(bf16[16,2,32,640]{3,1,2,0:T(2,128)(2,1)} %copy.41), calls=%async_computation | async-start | bytes 2621440 | tf_op jit(solution)/shard_map/all_to_all | solution.py:98
  28.1 5.5 %shard_map.82 = bf16[625,8,625]{2,1,0:T(8,128)(2,1)} custom-call(bf16[625,8,625]{2,1,0:T(8,128)(2,1)} %bitcast.35), custom_call_target="tpu_custom_call" | custom-call | tf_op jit(solution)/shard_map/pallas_call | solution.py:18
  33.6 0.0 copy-done
  33.6 0.0 copy-start.1
  33.6 6.1 %fusion.14 = bf16[8,625,64]{1,2,0:T(8,128)(2,1)} fusion(bf16[8,625,64]{1,2,0:T(8,128)(2,1)S(1)} %copy-done, bf16[8,625,625]{2,0,1:T(8,128)(2,1)} %bitcast.33), kind=kOutput, calls=%fused_computation.15 | convolution fusion | flops 400320000 | bytes 7530000 | tf_op jit(solution)/shard_map/ebc,ecm->ebm/dot_general | solution.py:115
  39.7 0.0 copy-done.1
  39.7 4.0 %fusion.50 = (bf16[4,625,625]{2,0,1:T(4,128)(2,1)}, bf16[4,625,625]{2,0,1:T(4,128)(2,1)}) fusion(bf16[8,625,625]{2,0,1:T(8,128)(2,1)S(1)} %bitcast.34), kind=kLoop, calls=%fused_computation.58 | loop fusion | bytes 12500000 | tf_op jit(solution)/shard_map/slice | solution.py:131
  43.7 5.3 %all-to-all-done = bf16[16,2,32,640]{3,1,2,0:T(2,128)(2,1)S(1)} async-done(((bf16[16,2,32,640]{3,1,2,0:T(2,128)(2,1)}), bf16[16,2,32,640]{3,1,2,0:T(2,128)(2,1)S(1)}, u32[]{:S(2)}, u32[]{:S(2)}) %all-to-all-start) | async-done | bytes 1310752 | tf_op jit(solution)/shard_map/all_to_all | solution.py:98
  49.0 0.9 %copy.42 = bf16[16,2,32,640]{3,1,0,2:T(2,128)(2,1)S(1)} copy(bf16[16,2,32,640]{3,1,2,0:T(2,128)(2,1)S(1)} %all-to-all-done) | data formatting | bytes 2621440 | tf_op jit(solution)/shard_map/all_to_all | solution.py:98
  49.9 0.5 reshape.37
  50.5 0.0 copy-start.3
  50.5 0.2 convert_reduce_fusion
  50.7 1.4 %fusion.23 = bf16[8,32,625]{2,0,1:T(8,128)(2,1)S(1)} fusion(bf16[32,32,640]{2,0,1:T(8,128)(2,1)S(1)} %reshape.37, bf16[8,32,625]{2,1,0:T(8,128)(2,1)} %param.8, s32[32]{0:T(128)S(1)} %convert_reduce_fusion), kind=kOutput, calls=%fused_computation.21 | convolution fusion | flops 10720256 | bytes 1950848 | tf_op jit(solution)/shard_map/es,skc->ekc/dot_general | solution.py:110
  52.1 1.4 %convolution_bitcast_fusion.1 = f32[32,64]{1,0:T(8,128)S(1)} fusion(bf16[8,625,64]{1,2,0:T(8,128)(2,1)} %fusion.14, bf16[8,32,625]{2,0,1:T(8,128)(2,1)S(1)} %fusion.23), kind=kOutput, calls=%fused_computation.23 | convolution fusion | flops 20480000 | bytes 968192 | tf_op jit(solution)/shard_map/ekb,ebm->km/dot_general | solution.py:118
  53.5 0.0 copy-start.2
  53.5 0.1 collective-permute-start
  53.6 0.1 fusion.51
  53.7 1.1 %collective-permute-done = f32[32,64]{1,0:T(8,128)S(1)} collective-permute-done((f32[32,64]{1,0:T(8,128)S(1)}, f32[32,64]{1,0:T(8,128)S(1)}, u32[]{:S(2)}, u32[]{:S(2)}) %collective-permute-start) | collective-permute-done | bytes 8224 | tf_op jit(solution)/shard_map/ppermute | solution.py:35
  54.8 1.5 %collective-permute-start.1 = (f32[32,64]{1,0:T(8,128)S(1)}, f32[32,64]{1,0:T(8,128)S(1)}, u32[]{:S(2)}, u32[]{:S(2)}) collective-permute-start(f32[32,64]{1,0:T(8,128)S(1)} %add.18), channel_id=1, source_target_pairs={{0,2},{1,3},{2,0},{3,1},{4,6},{5,7},{6,4},{7,5},{8,10},{9,11},{10,... | collective-permute-start | bytes 24584 | tf_op jit(solution)/shard_map/ppermute | solution.py:35
  56.3 0.0 copy-done.3
  56.3 0.8 %fusion.6 = f32[4,32,625]{2,1,0:T(8,128)S(1)} fusion(bf16[4,625,625]{2,0,1:T(4,128)(2,1)S(1)} %copy-done.3, bf16[4,32,625]{2,0,1:T(4,128)(2,1)S(1)} %get-tuple-element.8), kind=kOutput, calls=%fused_computation.6 | convolution fusion | flops 100000000 | bytes 3605000 | tf_op jit(solution)/shard_map/ekb,ebc->ekc/dot_general | solution.py:134
  57.0 0.0 copy-start.4
  57.1 1.4 %collective-permute-done.1 = f32[32,64]{1,0:T(8,128)S(1)} collective-permute-done((f32[32,64]{1,0:T(8,128)S(1)}, f32[32,64]{1,0:T(8,128)S(1)}, u32[]{:S(2)}, u32[]{:S(2)}) %collective-permute-start.1) | collective-permute-done | bytes 8224 | tf_op jit(solution)/shard_map/ppermute | solution.py:35
  58.5 3.0 %collective-permute-start.2 = (f32[32,64]{1,0:T(8,128)S(1)}, f32[32,64]{1,0:T(8,128)S(1)}, u32[]{:S(2)}, u32[]{:S(2)}) collective-permute-start(f32[32,64]{1,0:T(8,128)S(1)} %add.19), channel_id=1, source_target_pairs={{0,4},{1,5},{2,6},{3,7},{4,0},{5,1},{6,2},{7,3},{8,12},{9,13},{10,... | collective-permute-start | bytes 24584 | tf_op jit(solution)/shard_map/ppermute | solution.py:35
  61.5 0.0 copy-done.2
  61.5 0.8 %fusion.8 = f32[4,32,625]{2,1,0:T(8,128)S(1)} fusion(bf16[4,625,625]{2,0,1:T(4,128)(2,1)S(1)} %copy-done.2, bf16[4,32,625]{2,0,1:T(4,128)(2,1)S(1)} %get-tuple-element.7), kind=kOutput, calls=%fused_computation.8 | convolution fusion | flops 100000000 | bytes 3605000 | tf_op jit(solution)/shard_map/ekb,ebc->ekc/dot_general | solution.py:128
  62.3 1.4 %collective-permute-done.2 = f32[32,64]{1,0:T(8,128)S(1)} collective-permute-done((f32[32,64]{1,0:T(8,128)S(1)}, f32[32,64]{1,0:T(8,128)S(1)}, u32[]{:S(2)}, u32[]{:S(2)}) %collective-permute-start.2) | collective-permute-done | bytes 8224 | tf_op jit(solution)/shard_map/ppermute | solution.py:35
  63.7 0.0 copy-done.4
  63.8 0.1 fusion.29
  63.9 1.1 %fusion.22 = f32[8,32,625]{2,1,0:T(8,128)} fusion(bf16[32,64,1]{1,0,2:T(8,128)(2,1)S(1)} %fusion.29, bf16[8,625,64]{1,2,0:T(8,128)(2,1)S(1)} %copy-done, f32[4,32,625]{2,1,0:T(8,128)S(1)} %fusion.6, f32[4,32,625]{2,1,0:T(8,128)S(1)} %fusion.8), kind=kOutput, calls=%fused_computation.20 | convolution fusion | flops 20800000 | bytes 1924096 | tf_op jit(solution)/shard_map/km,ebm->ekb/dot_general | solution.py:149
  (6 shorter events, 0.0 us)
Async XLA Ops:
  0.0 33.6 %copy-start = (bf16[8,625,64]{1,2,0:T(8,128)(2,1)S(1)}, bf16[8,625,64]{1,2,0:T(8,128)(2,1)}, u32[]{:S(2)}) copy-start(bf16[8,625,64]{1,2,0:T(8,128)(2,1)} %param.14) | copy-start | bytes 1920004
  19.9 29.1 %all-to-all-start = ((bf16[16,2,32,640]{3,1,2,0:T(2,128)(2,1)}), bf16[16,2,32,640]{3,1,2,0:T(2,128)(2,1)S(1)}, u32[]{:S(2)}, u32[]{:S(2)}) async-start(bf16[16,2,32,640]{3,1,2,0:T(2,128)(2,1)} %copy.41), calls=%async_computation | async-start | bytes 2621440 | tf_op jit(solution)/shard_map/all_to_all | solution.py:98
  33.6 6.1 %copy-start.1 = (bf16[625,8,625]{2,1,0:T(8,128)(2,1)S(1)}, bf16[625,8,625]{2,1,0:T(8,128)(2,1)}, u32[]{:S(2)}) copy-start(bf16[625,8,625]{2,1,0:T(8,128)(2,1)} %shard_map.82) | copy-start | bytes 18750004
  50.5 5.8 %copy-start.3 = (bf16[4,625,625]{2,0,1:T(4,128)(2,1)S(1)}, bf16[4,625,625]{2,0,1:T(4,128)(2,1)}, u32[]{:S(2)}) copy-start(bf16[4,625,625]{2,0,1:T(4,128)(2,1)} %get-tuple-element.6) | copy-start | bytes 9375004
  53.5 8.1 %copy-start.2 = (bf16[4,625,625]{2,0,1:T(4,128)(2,1)S(1)}, bf16[4,625,625]{2,0,1:T(4,128)(2,1)}, u32[]{:S(2)}) copy-start(bf16[4,625,625]{2,0,1:T(4,128)(2,1)} %get-tuple-element.5) | copy-start | bytes 9375004
  53.5 1.3 %collective-permute-start = (f32[32,64]{1,0:T(8,128)S(1)}, f32[32,64]{1,0:T(8,128)S(1)}, u32[]{:S(2)}, u32[]{:S(2)}) collective-permute-start(f32[32,64]{1,0:T(8,128)S(1)} %convolution_bitcast_fusion.1), channel_id=1, source_target_pairs={{0,1},{1,0},{2,3},{3,2},{4,5},{5,4},{6,7},{7,6},{8,9},{9,8},{10,11... | collective-permute-start | bytes 24584 | tf_op jit(solution)/shard_map/ppermute | solution.py:35
  54.8 3.7 %collective-permute-start.1 = (f32[32,64]{1,0:T(8,128)S(1)}, f32[32,64]{1,0:T(8,128)S(1)}, u32[]{:S(2)}, u32[]{:S(2)}) collective-permute-start(f32[32,64]{1,0:T(8,128)S(1)} %add.18), channel_id=1, source_target_pairs={{0,2},{1,3},{2,0},{3,1},{4,6},{5,7},{6,4},{7,5},{8,10},{9,11},{10,... | collective-permute-start | bytes 24584 | tf_op jit(solution)/shard_map/ppermute | solution.py:35
  57.0 6.7 %copy-start.4 = (f32[1,64,64]{2,1,0:T(8,128)S(1)}, f32[1,64,64]{2,1,0:T(8,128)}, u32[]{:S(2)}) copy-start(f32[1,64,64]{2,1,0:T(8,128)} %param.15) | copy-start | bytes 49156
  58.5 5.2 %collective-permute-start.2 = (f32[32,64]{1,0:T(8,128)S(1)}, f32[32,64]{1,0:T(8,128)S(1)}, u32[]{:S(2)}, u32[]{:S(2)}) collective-permute-start(f32[32,64]{1,0:T(8,128)S(1)} %add.19), channel_id=1, source_target_pairs={{0,4},{1,5},{2,6},{3,7},{4,0},{5,1},{6,2},{7,3},{8,12},{9,13},{10,... | collective-permute-start | bytes 24584 | tf_op jit(solution)/shard_map/ppermute | solution.py:35
